TPU v7x, 32 devices: a whole 2x2x4 slice. The times are simulated.
32 devices in a mesh: beam: 16 (over z, y, core), seg: 2 (over x).
Axes of the slice: x: 2, y: 2, z: 4, core: 2. Of those that a mesh axis runs over, the one named last changes fastest.
Arguments:
- surveillance: bfloat16 [16, 2, 4, 4096], P('beam', None, None, 'seg'), may hold values from -6 to 6
- reference_blocks: bfloat16 [16, 2, 4, 4096], P('beam', None, None, 'seg'), may hold values from -6 to 6
- owner_index: int32 [4], replicated, may hold values from 0 to 15
- doppler_start: int32 [16], P('beam'), may hold values from -256 to 0
- lag_blocks: int32 [16, 6], P('beam'), may hold values from -1 to 7, as said below
- block_count: int32 [16], P('beam'), may hold values from 1 to 6, as said below
Outputs:
- caf: float32 [16, 6, 2, 128, 256], P('beam', None, None, None, 'seg')
Inputs may be any that keep to these rules, and one draw needn't show every extreme that they name: `block_count`: every beam lists from 1 to 6 lag blocks; some beam lists 6 and some beam lists 1. `lag_blocks`: the first block_count[b] entries of row b are distinct lag blocks; the other entries are -1.
All inputs are finite; a program needn't handle non-finite values.
Results may differ from a plain program's by a relative error of at most 0.0029.
Values may be sent and summed in bfloat16 or wider, within the bound.
No kernel may reach another device: no remote copies, remote signals or barrier semaphores. Data moves between devices by JAX's collectives and lax.ppermute only.
A program may use at most 128 MiB of HBM per device.

v0:
```python
import math

import jax
import jax.numpy as jnp
from jax import lax
from jax.sharding import PartitionSpec as P

LB = 128
NLB = 8
DOP = 256


def spread(shard, axis, root):
    mine = lax.axis_index(axis) == root
    return lax.psum(jnp.where(mine, shard, jnp.zeros_like(shard)), axis)


def passed_along(value, axis, steps):
    count = lax.axis_size(axis)
    leading, last = (max(0, -steps), min(count, count - steps))
    return lax.ppermute(value, axis, [(source, source + steps) for source in range(leading, last)])


def modulate(samples, sample_times, freqs, window_len):
    phase_turns = jnp.mod(sample_times[:, None] * freqs[None, :], window_len)
    phase_angle = phase_turns.astype(jnp.float32) * (2.0 * math.pi / window_len)
    cos_part = jnp.cos(phase_angle)
    sine_part = jnp.sin(phase_angle)
    real_part = samples[0].astype(jnp.float32)[:, None]
    imag_part = samples[1].astype(jnp.float32)[:, None]
    c_real = (real_part * cos_part - imag_part * sine_part).astype(jnp.bfloat16)
    c_imag = (0.0 - (real_part * sine_part + imag_part * cos_part)).astype(jnp.bfloat16)
    return jnp.concatenate([c_real, c_imag], axis=1)


def hankel_rows(window, length):
    span = window.shape[1]
    lagcount = span - length
    repeated = jnp.tile(window, (1, lagcount + 1))[:, : lagcount * (span + 1)]
    shaped = repeated.reshape(2, lagcount, span + 1)[:, :, :length]
    return shaped.reshape(2 * lagcount, length)


def add_items(totals, extended, coefficients, blocks, first, last):
    length = coefficients.shape[0]
    bin_count = coefficients.shape[1] // 2

    def one_item(slot, running):
        offset = jnp.maximum(blocks[slot], 0) * LB
        window = lax.dynamic_slice_in_dim(extended, offset, length + LB, axis=1)
        hankel = hankel_rows(window, length)
        product = jnp.dot(hankel, coefficients, preferred_element_type=jnp.float32)
        real_sum = product[:LB, :bin_count] - product[LB:, bin_count:]
        imag_sum = product[:LB, bin_count:] + product[LB:, :bin_count]
        item_term = jnp.stack([real_sum, imag_sum])[None]
        current = lax.dynamic_slice_in_dim(running, slot, 1, axis=0)
        return lax.dynamic_update_slice_in_dim(running, current + item_term, slot, axis=0)

    return lax.fori_loop(first, last, one_item, totals)


def shards(surveillance, reference_blocks, owner_index, doppler_start, lag_blocks, block_count):
    segments = lax.axis_size("seg")
    seg_place = lax.axis_index("seg")
    seg_len = surveillance.shape[3]
    step_count = surveillance.shape[2]
    step_len = seg_len * segments
    window_len = step_count * step_len
    slot_count = lag_blocks.shape[1]
    rim_len = NLB * LB
    own_count = block_count[0]
    own_start = doppler_start[0]
    own_blocks = lag_blocks[0]
    window_bins = jnp.arange(DOP, dtype=jnp.int32)
    own_sums = jnp.zeros((slot_count, 2, LB, DOP), jnp.float32)
    for step_index in range(step_count):
        samples = surveillance[0, :, step_index, :]
        sample_times = (
            step_index * step_len + seg_place * seg_len + jnp.arange(seg_len, dtype=jnp.int32)
        )
        cleaned = spread(reference_blocks[0, :, step_index, :], "beam", owner_index[step_index])
        coefficients = modulate(cleaned, sample_times, own_start + window_bins, window_len)
        edge_rows = passed_along(samples[:, :rim_len], "seg", -1)
        extended = jnp.concatenate([samples, edge_rows], axis=1)
        own_sums = add_items(own_sums, extended, coefficients, own_blocks, 0, own_count)
    normalizer = 1.0 / math.sqrt(window_len)
    result = lax.psum_scatter(own_sums, "seg", scatter_dimension=3, tiled=True) * normalizer
    return result[None]


def solution(mesh):
    placed = (
        P("beam", None, None, "seg"),
        P("beam", None, None, "seg"),
        P(),
        P("beam"),
        P("beam", None),
        P("beam"),
    )
    return jax.shard_map(
        shards,
        mesh=mesh,
        in_specs=placed,
        out_specs=P("beam", None, None, None, "seg"),
        check_vma=False,
    )
```

profile of v0, /device:TPU:0, one launch (start us, length us, event | category | flops | bytes accessed | tf_op | source)
XLA Modules:
  0.0 440.8 jit_solution(3616809494672321963)
XLA Ops:
  18.7 63.0 %all-reduce = (bf16[2,2048]{1,0:T(2,128)(2,1)S(1)}, bf16[2,2048]{1,0:T(2,128)(2,1)S(1)}, bf16[2,2048]{1,0:T(2,128)(2,1)S(1)}, bf16[2,2048]{1,0:T(2,128)(2,1)S(1)}) all-reduce(bf16[2,2048]{1,0:T(2,128)(2,1)S(1)} %get-tuple-element.238, bf16[2,2048]{1,0:T(2,128)(2,1)S(1)} %get-tuple-element.237, ...), channel_id=1, replica_groups=mesh['beam'=16,'seg'=2] {'beam'}, use_global_device_ids=true, to_apply=%region_0.1 | all-reduce | flops 16384 | bytes 65536 | tf_op jit(solution)/shard_map/psum | solution.py:15
  81.8 35.8 %subtract_convert_fusion.1 = (bf16[2048,256]{1,0:T(8,128)(2,1)S(1)}, bf16[2048,256]{1,0:T(8,128)(2,1)S(1)}, bf16[2048,256]{1,0:T(8,128)(2,1)S(1)}, bf16[2048,256...) fusion(f32[2048]{0:T(1024)S(1)} %bitcast.193, ...), kind=kLoop, calls=%fused_computation.73 | loop fusion | flops 48234496 | bytes 8487936 | tf_op jit(solution)/shard_map/convert_element_type | solution.py:31
  125.0 59.4 %while.40 = (s32[]{:T(128)}, f32[6,2,128,256]{3,2,1,0:T(8,128)}, s32[]{:T(128)}, s32[6]{0:T(128)S(1)}, bf16[2,3072]{1,0:T(2,128)(2,1)S(1)}, /*index=5*/bf16[2048...) while((s32[]{:T(128)}, f32[6,2,128,256]{3,2,1,0:T(8,128)}, ...), condition=%wide.region_2.3_spmd, body=%wide.region_1.2_spmd.sunk | while | flops 537067520 | bytes 25811208 | solution.py:59
  129.0 1.9 reshape.168
  130.9 2.0 reshape.169
  140.7 1.9 reshape.168
  142.6 2.0 reshape.169
  152.4 1.9 reshape.168
  154.3 2.0 reshape.169
  164.1 1.9 reshape.168
  166.0 2.0 reshape.169
  175.8 1.9 reshape.168
  177.7 2.0 reshape.169
  184.4 58.7 %while.41 = (s32[]{:T(128)}, f32[6,2,128,256]{3,2,1,0:T(8,128)}, s32[]{:T(128)}, s32[6]{0:T(128)S(1)}, bf16[2,3072]{1,0:T(2,128)(2,1)S(1)}, /*index=5*/bf16[2048...) while((s32[]{:T(128)}, f32[6,2,128,256]{3,2,1,0:T(8,128)}, ...), condition=%wide.region_5.6_spmd, body=%wide.region_4.5_spmd.sunk | while | flops 537067520 | bytes 25811208 | solution.py:59
  188.1 1.9 reshape.170
  190.0 2.0 reshape.171
  199.7 1.9 reshape.170
  201.6 2.0 reshape.171
  211.4 1.9 reshape.170
  213.3 2.0 reshape.171
  223.0 1.9 reshape.170
  224.9 2.0 reshape.171
  234.6 1.9 reshape.170
  236.5 2.0 reshape.171
  243.2 59.5 %while.42 = (s32[]{:T(128)}, f32[6,2,128,256]{3,2,1,0:T(8,128)}, s32[]{:T(128)}, s32[6]{0:T(128)S(1)}, bf16[2,3072]{1,0:T(2,128)(2,1)S(1)}, /*index=5*/bf16[2048...) while((s32[]{:T(128)}, f32[6,2,128,256]{3,2,1,0:T(8,128)}, ...), condition=%wide.region_8.9_spmd, body=%wide.region_7.8_spmd.sunk | while | flops 537067520 | bytes 25811208 | solution.py:59
  247.2 1.9 reshape.172
  249.1 2.0 reshape.173
  259.0 1.9 reshape.172
  260.9 2.0 reshape.173
  270.7 1.9 reshape.172
  272.6 2.0 reshape.173
  282.4 1.9 reshape.172
  284.3 2.0 reshape.173
  294.2 1.9 reshape.172
  296.1 2.0 reshape.173
  302.8 59.0 %while.43 = (s32[]{:T(128)}, f32[6,2,128,256]{3,2,1,0:T(8,128)}, s32[]{:T(128)}, s32[6]{0:T(128)S(1)}, bf16[2,3072]{1,0:T(2,128)(2,1)S(1)}, /*index=5*/bf16[2048...) while((s32[]{:T(128)}, f32[6,2,128,256]{3,2,1,0:T(8,128)}, ...), condition=%wide.region_11.12_spmd, body=%wide.region_10.11_spmd.sunk | while | flops 537067520 | bytes 25811208 | solution.py:59
  306.5 1.9 reshape.174
  308.4 2.0 reshape.175
  318.2 1.9 reshape.174
  320.1 2.0 reshape.175
  329.9 1.9 reshape.174
  331.8 2.0 reshape.175
  341.6 1.9 reshape.174
  343.5 2.0 reshape.175
  353.2 1.9 reshape.174
  355.1 2.0 reshape.175
  361.9 70.0 %reduce-scatter.2.cloned.1.call-done = f32[6,2,128,128]{3,2,1,0:T(8,128)} async-done(((f32[6,2,128,256]{3,2,1,0:T(8,128)}), f32[6,2,128,128]{3,2,1,0:T(8,128)}) %reduce-scatter.2.cloned.1.call-update) | async-done | bytes 786448 | tf_op jit(solution)/shard_map/reduce_scatter | solution.py:87
  431.9 2.1 multiply_bitcast_fusion
  (261 shorter events, 145.1 us)
Async XLA Ops:
  6.5 425.3 %reduce-scatter.2.cloned.1.call-start = ((), (), s32[]{:S(2)}) async-start(), calls=%async_computation.1 | async-start | bytes 2359296 | tf_op jit(solution)/shard_map/reduce_scatter | solution.py:87
  7.5 116.1 %collective-permute-start = (bf16[2,1024]{1,0:T(2,128)(2,1)S(1)}, bf16[2,1024]{1,0:T(2,128)(2,1)S(1)}, u32[]{:S(2)}, u32[]{:S(2)}) collective-permute-start(bf16[2,1024]{1,0:T(2,128)(2,1)S(1)} %slice.192), channel_id=1, source_target_pairs={{1,0},{3,2},{5,4},{7,6},{9,8},{11,10},{13,12},{15,14},{17,16},{19,... | collective-permute-start | bytes 12296 | tf_op jit(solution)/shard_map/ppermute | solution.py:21
  8.9 175.5 %collective-permute-start.1 = (bf16[2,1024]{1,0:T(2,128)(2,1)S(1)}, bf16[2,1024]{1,0:T(2,128)(2,1)S(1)}, u32[]{:S(2)}, u32[]{:S(2)}) collective-permute-start(bf16[2,1024]{1,0:T(2,128)(2,1)S(1)} %slice.195), channel_id=1, source_target_pairs={{1,0},{3,2},{5,4},{7,6},{9,8},{11,10},{13,12},{15,14},{17,16},{19,... | collective-permute-start | bytes 12296 | tf_op jit(solution)/shard_map/ppermute | solution.py:21
  10.2 233.0 %collective-permute-start.2 = (bf16[2,1024]{1,0:T(2,128)(2,1)S(1)}, bf16[2,1024]{1,0:T(2,128)(2,1)S(1)}, u32[]{:S(2)}, u32[]{:S(2)}) collective-permute-start(bf16[2,1024]{1,0:T(2,128)(2,1)S(1)} %slice.198), channel_id=1, source_target_pairs={{1,0},{3,2},{5,4},{7,6},{9,8},{11,10},{13,12},{15,14},{17,16},{19,... | collective-permute-start | bytes 12296 | tf_op jit(solution)/shard_map/ppermute | solution.py:21
  11.5 291.2 %collective-permute-start.3 = (bf16[2,1024]{1,0:T(2,128)(2,1)S(1)}, bf16[2,1024]{1,0:T(2,128)(2,1)S(1)}, u32[]{:S(2)}, u32[]{:S(2)}) collective-permute-start(bf16[2,1024]{1,0:T(2,128)(2,1)S(1)} %slice.201), channel_id=1, source_target_pairs={{1,0},{3,2},{5,4},{7,6},{9,8},{11,10},{13,12},{15,14},{17,16},{19,... | collective-permute-start | bytes 12296 | tf_op jit(solution)/shard_map/ppermute | solution.py:21
  122.1 2.9 copy-start.4
  132.9 1.6 copy-start.3
  144.6 1.6 copy-start.3
  156.3 1.6 copy-start.3
  168.0 1.6 copy-start.3
  179.7 1.6 copy-start.3
  192.0 1.6 copy-start.2
  203.6 1.6 copy-start.2
  215.3 1.6 copy-start.2
  226.9 1.6 copy-start.2
  238.5 1.6 copy-start.2
  251.1 1.6 copy-start.1
  262.9 1.6 copy-start.1
  274.6 1.6 copy-start.1
  286.3 1.6 copy-start.1
  298.1 1.6 copy-start.1
  310.4 1.6 copy-start
  322.1 1.6 copy-start
  333.8 1.6 copy-start
  345.5 1.6 copy-start
  357.1 1.6 copy-start
Sparse Core Ops, SparseCore 0:
  362.0 69.8 reduce-scatter.1
where the time goes:
time: 444 us; the launch traced here: 441 us
  local copies, waits for them, and re-layouts  162 us (36%)
  other arithmetic  79.8 us (18%)
  waiting for transfers between devices  70.1 us (16%)
  blocking collectives  63 us (14%)
  loops' own time  30.2 us (7%)
  between operations  17 us (4%)
  matrix products  13.9 us (3%)
  starting transfers between devices  5.17 us (1%)
    while x100, local copies, waits for them, and re-layouts  86.1 us
    reduce_scatter x1, waiting for transfers between devices, shards(): lax.psum_scatter(own_sums, 'seg', scatter_dimension=3, tiled=True)  70 us
    psum x1, blocking collectives, spread(): return lax.psum(jnp.where(mine, shard, jnp.zeros_like(shard)), axis)  63 us
    reshape x20, local copies, waits for them, and re-layouts, hankel_rows(): shaped = repeated.reshape(2, lagcount, span + 1)[:, :, :length]  39.8 us
    convert_element_type x1, other arithmetic, modulate(): c_real = (real_part * cos_part - imag_part * sine_part).astype(jnp.bfloat16)  35.8 us
    dynamic_update_slice x20, other arithmetic, one_item(): lax.dynamic_update_slice_in_dim(running, current + item_term, slot, axis=0)  34 us
    another operation x4, loops' own time, add_items(): return lax.fori_loop(first, last, one_item, totals)  30.2 us
    slice x20, local copies, waits for them, and re-layouts, hankel_rows(): repeated = jnp.tile(window, (1, lagcount + 1))[:, :lagcount * (span + 1)]  16.7 us
  transfers between devices with their start and end apart: 5, of which 1 were waited for; matrix products, arithmetic and copies ran while one was open for 41% of the time, Pallas kernels for 0%

commit v1 on v0

v1 whole, which is shorter than its diff:
```python
import functools
import math

import jax
import jax.numpy as jnp
from jax import lax
from jax.experimental import pallas as pl
from jax.experimental.pallas import tpu as pltpu
from jax.sharding import PartitionSpec as P

LB = 128
NLB = 8
DOP = 256
CHUNK = 512


def phase_table(freqs, times, window_len):
    turns = jnp.mod(times[:, None] * freqs[None, :], window_len)
    angle = turns.astype(jnp.float32) * (2.0 * math.pi / window_len)
    return jnp.cos(angle), jnp.sin(angle)


def caf_kernel(blocks_ref, count_ref, wpad_ref, ref_ref, ac_ref, as_ref, bc_ref, bs_ref,
               out_ref, shifted, acc, *, chunks, slots, span, norm):
    k = pl.program_id(0)
    lanes = CHUNK + LB

    @pl.when(k == 0)
    def _():
        acc[...] = jnp.zeros_like(acc)

    for comp in range(2):
        def build(i, carry):
            v0 = pl.multiple_of(i * CHUNK, CHUNK)
            win = wpad_ref[k, comp:comp + 1, pl.ds(v0, lanes)]
            tile = jnp.broadcast_to(win, (LB, lanes))
            rolled = pltpu.roll(tile, lanes - LB + 1, 1, stride=1, stride_axis=0)
            shifted[comp * LB:(comp + 1) * LB, pl.ds(v0, CHUNK)] = rolled[:, :CHUNK].astype(jnp.bfloat16)
            return carry
        lax.fori_loop(0, span // CHUNK, build, 0)

    offsets = [jnp.maximum(blocks_ref[q], 0) * LB for q in range(slots)]

    def chunk(c, carry):
        g = k * chunks + c
        rr = ref_ref[g]
        r_re = rr[0:1, :]
        r_im = rr[1:2, :]
        a_c = jnp.broadcast_to(ac_ref[g], (LB, CHUNK))
        a_s = jnp.broadcast_to(as_ref[g], (LB, CHUNK))
        b_c = bc_ref[...]
        b_s = bs_ref[...]
        cos_part = a_c * b_c - a_s * b_s
        sine_part = a_s * b_c + a_c * b_s
        c_re = (r_re * cos_part - r_im * sine_part).astype(jnp.bfloat16)
        c_im = (0.0 - (r_re * sine_part + r_im * cos_part)).astype(jnp.bfloat16)
        coef = jnp.concatenate([c_re, c_im], axis=0)
        base = c * CHUNK
        for q in range(slots):
            off = pl.multiple_of(offsets[q] + base, LB)
            hank = shifted[:, pl.ds(off, CHUNK)]
            acc[q] += lax.dot_general(hank, coef, (((1,), (1,)), ((), ())),
                                      preferred_element_type=jnp.float32)
        return carry

    lax.fori_loop(0, chunks, chunk, 0)

    @pl.when(k == pl.num_programs(0) - 1)
    def _():
        count = count_ref[0]
        for q in range(slots):
            part = acc[q]
            re = part[:LB, :LB] - part[LB:, LB:]
            im = part[:LB, LB:] + part[LB:, :LB]
            keep = q < count
            out_ref[q, 0] = jnp.where(keep, re * norm, 0.0)
            out_ref[q, 1] = jnp.where(keep, im * norm, 0.0)


def shards(surveillance, reference_blocks, owner_index, doppler_start, lag_blocks, block_count):
    segments = lax.axis_size("seg")
    seg_place = lax.axis_index("seg")
    beam_place = lax.axis_index("beam")
    seg_len = surveillance.shape[3]
    step_count = surveillance.shape[2]
    step_len = seg_len * segments
    window_len = step_count * step_len
    slot_count = lag_blocks.shape[1]
    rim_len = NLB * LB
    bins = DOP // segments
    chunks = step_len // CHUNK

    mine = (owner_index == beam_place)[None, :, None]
    cleaned = lax.psum(jnp.where(mine, reference_blocks[0], jnp.zeros_like(reference_blocks[0])), "beam")
    both = jnp.stack([surveillance[0], cleaned])
    both = lax.all_gather(both, "seg", axis=3, tiled=True)
    samples = both[0]
    refs = both[1]

    span = step_len + rim_len
    wpad = jnp.transpose(samples, (1, 0, 2)).astype(jnp.float32)
    wpad = jnp.pad(wpad, ((0, 0), (0, 0), (0, span + LB - step_len)))
    refrows = jnp.transpose(refs.reshape(2, step_count * chunks, CHUNK), (1, 0, 2))
    refrows = refrows.astype(jnp.float32)

    freqs = doppler_start[0] + seg_place * bins + jnp.arange(bins, dtype=jnp.int32)
    a_c, a_s = phase_table(freqs, jnp.arange(step_count * chunks, dtype=jnp.int32) * CHUNK, window_len)
    b_c, b_s = phase_table(freqs, jnp.arange(CHUNK, dtype=jnp.int32), window_len)
    a_c = a_c[:, :, None]
    a_s = a_s[:, :, None]
    b_c = b_c.T
    b_s = b_s.T

    kernel = functools.partial(caf_kernel, chunks=chunks, slots=slot_count, span=span,
                               norm=1.0 / math.sqrt(window_len))
    full = lambda shape: pl.BlockSpec(shape, lambda k, *_: (0,) * len(shape))
    out = pl.pallas_call(
        kernel,
        out_shape=jax.ShapeDtypeStruct((slot_count, 2, LB, bins), jnp.float32),
        grid_spec=pltpu.PrefetchScalarGridSpec(
            num_scalar_prefetch=2,
            grid=(step_count,),
            in_specs=[full(wpad.shape), full(refrows.shape), full(a_c.shape), full(a_s.shape),
                      full(b_c.shape), full(b_s.shape)],
            out_specs=full((slot_count, 2, LB, bins)),
            scratch_shapes=[pltpu.VMEM((2 * LB, span), jnp.bfloat16),
                            pltpu.VMEM((slot_count, 2 * LB, 2 * bins), jnp.float32)],
        ),
        compiler_params=pltpu.CompilerParams(dimension_semantics=("arbitrary",)),
    )(lag_blocks[0], block_count, wpad, refrows, a_c, a_s, b_c, b_s)
    return jnp.flip(out, axis=2)[None]


def solution(mesh):
    placed = (
        P("beam", None, None, "seg"),
        P("beam", None, None, "seg"),
        P(),
        P("beam"),
        P("beam", None),
        P("beam"),
    )
    return jax.shard_map(
        shards,
        mesh=mesh,
        in_specs=placed,
        out_specs=P("beam", None, None, None, "seg"),
        check_vma=False,
    )
```

time: 444 us -> 130 us (0.29)
  local copies, waits for them, and re-layouts: 162 us -> 8.33 us
  waiting for transfers between devices: 70.1 us -> 0 us
  other arithmetic: 79.8 us -> 13.3 us
  Pallas kernels: 0 us -> 37.8 us
  loops' own time: 30.2 us -> 0 us
  between operations: 17 us -> 1.34 us
  matrix products: 13.9 us -> 0 us
  starting transfers between devices: 5.17 us -> 0 us
  blocking collectives: 63 us -> 67.9 us
    while x100 -> x0, local copies, waits for them, and re-layouts: 86.1 us -> none
    reduce_scatter x1 -> x0, waiting for transfers between devices: 70 us -> none  [shards(): lax.psum_scatter(own_sums, 'seg', scatter_dimension=3, tiled=True)]
    reshape x20 -> x0, local copies, waits for them, and re-layouts: 39.8 us -> none  [hankel_rows(): shaped = repeated.reshape(2, lagcount, span + 1)[:, :, :length]]
    pallas_call x0 -> x1, Pallas kernels: none -> 37.8 us  [shards(): pl.pallas_call(kernel, out_shape=jax.ShapeDtypeStruct((slot_count, 2, LB,...]
    convert_element_type x5 -> x2, other arithmetic: 35.9 us -> 0.78 us  [the longest x1 0.7 us: shards(): refrows = refrows.astype(jnp.float32)]
    dynamic_update_slice x20 -> x0, other arithmetic: 34 us -> none  [one_item(): lax.dynamic_update_slice_in_dim(running, current + item_term, slot, axis=0)]
    another operation x4 -> x0, loops' own time: 30.2 us -> none  [add_items(): return lax.fori_loop(first, last, one_item, totals)]
    slice x46 -> x1, local copies, waits for them, and re-layouts: 21.5 us -> 0.09 us  [shards(): refs = both[1]]
  transfers between devices with their start and end apart: 5 -> 0, of which waited for: 1 -> 0; matrix products, arithmetic and copies ran while one was open for 41% -> 0% of each run, Pallas kernels for 0% -> 0%
where the time goes in v1:
time: 130 us; the launch traced here: 129 us
  blocking collectives  67.9 us (52%)
  Pallas kernels  37.8 us (29%)
  other arithmetic  13.3 us (10%)
  local copies, waits for them, and re-layouts  8.33 us (6%)
  between operations  1.34 us (1%)
    psum x1, blocking collectives, shards(): lax.psum(jnp.where(mine, reference_blocks[0], jnp.zeros_like(reference_bl...  63 us
    pallas_call x1, Pallas kernels, shards(): pl.pallas_call(kernel, out_shape=jax.ShapeDtypeStruct((slot_count, 2, LB,...  37.8 us
    sin x2, other arithmetic, phase_table(): return (jnp.cos(angle), jnp.sin(angle))  10.2 us
    rev x1, local copies, waits for them, and re-layouts, shards(): return jnp.flip(out, axis=2)[None]  6.8 us
    all_gather x1, blocking collectives, shards(): both = lax.all_gather(both, 'seg', axis=3, tiled=True)  4.94 us

profile of v1, /device:TPU:0, one launch (start us, length us, event | category | flops | bytes accessed | tf_op | source)
XLA Modules:
  0.0 128.7 jit_solution(17148626039988854619)
XLA Ops:
  1.3 0.7 broadcast_compare_fusion
  2.0 0.1 fusion.9
  2.1 0.9 fusion.8
  2.9 63.0 %psum.7 = bf16[1,2,4,2048]{3,1,2,0:T(2,128)(2,1)S(1)} all-reduce(bf16[1,2,4,2048]{3,1,2,0:T(2,128)(2,1)S(1)} %fusion.8), channel_id=1, replica_groups=mesh['beam'=16,'seg'=2] {'beam'}, use_global_device_ids=true, to_apply=%region_0.1 | all-reduce | flops 16384 | bytes 65536 | tf_op jit(solution)/shard_map/psum | solution.py:94
  65.9 0.8 copy.10
  66.7 0.1 pad_maximum_fusion
  66.8 4.9 %all_gather.3 = bf16[2,2,4,4096]{3,1,2,0:T(2,128)(2,1)S(1)} all-gather(bf16[2,2,4,2048]{3,1,2,0:T(2,128)(2,1)S(1)} %pad_maximum_fusion), channel_id=1, replica_groups=mesh['beam'=16,'seg'=2] {'seg'}, dimensions={3}, use_global_device_ids=true | all-gather | bytes 196608 | tf_op jit(solution)/shard_map/all_gather | solution.py:96
  71.7 0.1 fusion.11
  71.8 0.7 convert_bitcast_fusion.ref_ref
  72.5 0.7 pad_convert_fusion.wpad_ref
  73.3 1.9 %fusion.6 = (f32[128,512]{1,0:T(8,128)}, f32[128,512]{1,0:T(8,128)}) fusion(s32[128]{0:T(128)S(1)} %iota_add_fusion), kind=kLoop, calls=%fused_computation.12 | loop fusion | flops 917504 | bytes 524800 | tf_op jit(solution)/shard_map/sin | solution.py:20
  75.2 0.6 copy.11
  75.8 8.3 %multiply_sine_fusion = (f32[32,128,1]{2,1,0:T(8,128)}, f32[32,128,1]{2,1,0:T(8,128)}) fusion(f32[32,128,1]{2,1,0:T(8,128)S(1)} %copy.11), kind=kLoop, calls=%fused_computation | loop fusion | flops 4096 | bytes 49152 | tf_op jit(solution)/shard_map/sin | solution.py:20
  84.1 37.8 %shard_map.64 = f32[6,2,128,128]{3,2,1,0:T(8,128)} custom-call(s32[6]{0:T(128)} %bitcast.19, s32[1]{0:T(128)S(6)} %copy.16.count_ref, f32[4,2,5248]{2,1,0:T(2,128)} %pad_convert_fusion.wpad_ref, f32[32,2,512]{2,1,0:T(2,128)} %convert_bitcast_fusion.ref_ref, f32[32,128,1]{2,1,0:T(8,128)} %get-tuple-element.6.ac_ref, f32[32,128,1]{2,1,0:T(8,128)} %get-tuple-element.5.as_ref, ...), custom_call_target="tpu_custom_call" | custom-call | tf_op jit(solution)/shard_map/pallas_call | solution.py:117
  121.9 6.8 %rev.4 = f32[6,2,128,128]{3,2,1,0:T(8,128)} reverse(f32[6,2,128,128]{3,2,1,0:T(8,128)} %shard_map.64), dimensions={2} | reverse | bytes 1572864 | tf_op jit(solution)/shard_map/jit(_flip)/rev | solution.py:131
  (2 shorter events, 0.0 us)

commit v2 on v1

--- a/solution.py
+++ b/solution.py
@@ -21,7 +21,7 @@
 
 
 def caf_kernel(blocks_ref, count_ref, wpad_ref, ref_ref, ac_ref, as_ref, bc_ref, bs_ref,
-               out_ref, shifted, acc, *, chunks, slots, span, norm):
+               out_ref, shifted, acc, *, chunks, slots, span, far, norm):
     k = pl.program_id(0)
     lanes = CHUNK + LB
 
@@ -55,9 +55,9 @@
         c_re = (r_re * cos_part - r_im * sine_part).astype(jnp.bfloat16)
         c_im = (0.0 - (r_re * sine_part + r_im * cos_part)).astype(jnp.bfloat16)
         coef = jnp.concatenate([c_re, c_im], axis=0)
-        base = c * CHUNK
+        base = far - c * CHUNK
         for q in range(slots):
-            off = pl.multiple_of(offsets[q] + base, LB)
+            off = pl.multiple_of(base - offsets[q], LB)
             hank = shifted[:, pl.ds(off, CHUNK)]
             acc[q] += lax.dot_general(hank, coef, (((1,), (1,)), ((), ())),
                                       preferred_element_type=jnp.float32)
@@ -77,6 +77,27 @@
             out_ref[q, 1] = jnp.where(keep, im * norm, 0.0)
 
 
+def butterfly_sum(value, axis):
+    count = lax.axis_size(axis)
+    if count & (count - 1):
+        return lax.psum(value, axis)
+    bit = 1
+    while bit < count:
+        value = value + lax.ppermute(value, axis, [(i, i ^ bit) for i in range(count)])
+        bit *= 2
+    return value
+
+
+def seg_join(half, axis):
+    count = lax.axis_size(axis)
+    parts = lax.all_gather(half, axis, axis=half.ndim - 1, tiled=True) if count != 2 else None
+    if parts is not None:
+        return parts
+    other = lax.ppermute(half, axis, [(0, 1), (1, 0)])
+    first = lax.axis_index(axis) == 0
+    return jnp.where(first, jnp.concatenate([half, other], -1), jnp.concatenate([other, half], -1))
+
+
 def shards(surveillance, reference_blocks, owner_index, doppler_start, lag_blocks, block_count):
     segments = lax.axis_size("seg")
     seg_place = lax.axis_index("seg")
@@ -90,28 +111,32 @@
     bins = DOP // segments
     chunks = step_len // CHUNK
 
+    samples = seg_join(surveillance[0], "seg")
     mine = (owner_index == beam_place)[None, :, None]
-    cleaned = lax.psum(jnp.where(mine, reference_blocks[0], jnp.zeros_like(reference_blocks[0])), "beam")
-    both = jnp.stack([surveillance[0], cleaned])
-    both = lax.all_gather(both, "seg", axis=3, tiled=True)
-    samples = both[0]
-    refs = both[1]
+    cleaned = butterfly_sum(jnp.where(mine, reference_blocks[0], jnp.zeros_like(reference_blocks[0])), "beam")
+    refs = seg_join(cleaned, "seg")
 
     span = step_len + rim_len
-    wpad = jnp.transpose(samples, (1, 0, 2)).astype(jnp.float32)
-    wpad = jnp.pad(wpad, ((0, 0), (0, 0), (0, span + LB - step_len)))
-    refrows = jnp.transpose(refs.reshape(2, step_count * chunks, CHUNK), (1, 0, 2))
+    far = rim_len - LB + step_len - CHUNK
+    lead = far + CHUNK + LB - 2 - (step_len - 1)
+    wpad = jnp.flip(jnp.transpose(samples, (1, 0, 2)), axis=2).astype(jnp.float32)
+    wpad = jnp.pad(wpad, ((0, 0), (0, 0), (lead, span + LB - step_len - lead)))
+    refrows = jnp.flip(jnp.transpose(refs.reshape(2, step_count * chunks, CHUNK), (1, 0, 2)), axis=2)
     refrows = refrows.astype(jnp.float32)
 
     freqs = doppler_start[0] + seg_place * bins + jnp.arange(bins, dtype=jnp.int32)
     a_c, a_s = phase_table(freqs, jnp.arange(step_count * chunks, dtype=jnp.int32) * CHUNK, window_len)
-    b_c, b_s = phase_table(freqs, jnp.arange(CHUNK, dtype=jnp.int32), window_len)
+    fine = 64
+    h_c, h_s = phase_table(freqs, jnp.arange(CHUNK // fine, dtype=jnp.int32) * fine, window_len)
+    l_c, l_s = phase_table(freqs, jnp.arange(fine, dtype=jnp.int32), window_len)
+    b_c = (h_c[:, None] * l_c[None] - h_s[:, None] * l_s[None]).reshape(CHUNK, bins)
+    b_s = (h_s[:, None] * l_c[None] + h_c[:, None] * l_s[None]).reshape(CHUNK, bins)
     a_c = a_c[:, :, None]
     a_s = a_s[:, :, None]
-    b_c = b_c.T
-    b_s = b_s.T
+    b_c = jnp.flip(b_c, axis=0).T
+    b_s = jnp.flip(b_s, axis=0).T
 
-    kernel = functools.partial(caf_kernel, chunks=chunks, slots=slot_count, span=span,
+    kernel = functools.partial(caf_kernel, chunks=chunks, slots=slot_count, span=span, far=far,
                                norm=1.0 / math.sqrt(window_len))
     full = lambda shape: pl.BlockSpec(shape, lambda k, *_: (0,) * len(shape))
     out = pl.pallas_call(
@@ -128,7 +153,7 @@
         ),
         compiler_params=pltpu.CompilerParams(dimension_semantics=("arbitrary",)),
     )(lag_blocks[0], block_count, wpad, refrows, a_c, a_s, b_c, b_s)
-    return jnp.flip(out, axis=2)[None]
+    return out[None]
 
 
 def solution(mesh):

time: 130 us -> 76.6 us (0.59)
  blocking collectives: 67.9 us -> 0 us
  starting transfers between devices: 0 us -> 9.24 us
  waiting for transfers between devices: 0 us -> 6.7 us
    psum x1 -> x0, blocking collectives: 63 us -> none  [shards(): lax.psum(jnp.where(mine, reference_blocks[0], jnp.zeros_like(reference_bl...]
    ppermute x0 -> x6, starting transfers between devices: none -> 9.24 us  [the longest x4 6.4 us: butterfly_sum(): lax.ppermute(value, axis, [(i, i ^ bit) for i in range(count)])]
    ppermute x0 -> x6, waiting for transfers between devices: none -> 6.7 us  [the longest x4 6.69 us: butterfly_sum(): lax.ppermute(value, axis, [(i, i ^ bit) for i in range(count)])]
    all_gather x1 -> x0, blocking collectives: 4.94 us -> none  [shards(): both = lax.all_gather(both, 'seg', axis=3, tiled=True)]
    sin x2 -> x1, other arithmetic: 10.2 us -> 8.25 us  [phase_table(): return (jnp.cos(angle), jnp.sin(angle))]
    rev x1 -> x4, local copies, waits for them, and re-layouts: 6.8 us -> 6.81 us  [the longest x1 2.97 us: shards(): jnp.flip(jnp.transpose(samples, (1, 0, 2)), axis=2).astype(jnp.float32)]
  transfers between devices with their start and end apart: 0 -> 6, of which waited for: 0 -> 3; matrix products, arithmetic and copies ran while one was open for 0% -> 18% of each run, Pallas kernels for 0% -> 0%
where the time goes in v2:
time: 76.6 us; the launch traced here: 76.4 us
  Pallas kernels  38.4 us (50%)
  other arithmetic  12.1 us (16%)
  starting transfers between devices  9.24 us (12%)
  local copies, waits for them, and re-layouts  8.5 us (11%)
  waiting for transfers between devices  6.7 us (9%)
  between operations  1.41 us (2%)
    pallas_call x1, Pallas kernels, shards(): pl.pallas_call(kernel, out_shape=jax.ShapeDtypeStruct((slot_count, 2, LB,...  38.4 us
    sin x1, other arithmetic, phase_table(): return (jnp.cos(angle), jnp.sin(angle))  8.25 us
    ppermute x4, waiting for transfers between devices, butterfly_sum(): lax.ppermute(value, axis, [(i, i ^ bit) for i in range(count)])  6.69 us
    ppermute x4, starting transfers between devices, butterfly_sum(): lax.ppermute(value, axis, [(i, i ^ bit) for i in range(count)])  6.4 us
    rev x1, local copies, waits for them, and re-layouts, shards(): jnp.flip(jnp.transpose(samples, (1, 0, 2)), axis=2).astype(jnp.float32)  2.97 us
    ppermute x2, starting transfers between devices, seg_join(): other = lax.ppermute(half, axis, [(0, 1), (1, 0)])  2.84 us
    rev x1, local copies, waits for them, and re-layouts, shards(): b_s = jnp.flip(b_s, axis=0).T  1.61 us
    rev x1, local copies, waits for them, and re-layouts, shards(): b_c = jnp.flip(b_c, axis=0).T  1.59 us
  transfers between devices with their start and end apart: 6, of which 3 were waited for; matrix products, arithmetic and copies ran while one was open for 18% of the time, Pallas kernels for 0%

profile of v2, /device:TPU:0, one launch (start us, length us, event | category | flops | bytes accessed | tf_op | source)
XLA Modules:
  0.0 76.4 jit_solution(8595901114195277558)
XLA Ops:
  0.0 0.7 broadcast_compare_fusion
  0.7 0.9 %broadcast_select_fusion.2 = bf16[2,4,2048]{2,0,1:T(2,128)(2,1)S(1)} fusion(pred[4]{0:T(512)(128)(4,1)S(1)} %broadcast_compare_fusion, bf16[1,2,4,2048]{3,2,1,0:T(4,128)(2,1)} %param.7), kind=kLoop, calls=%fused_computation.8 | loop fusion | flops 16384 | bytes 65540 | tf_op jit(solution)/shard_map/jit(_where)/select_n | solution.py:116
  1.5 0.5 collective-permute-start.1
  2.0 0.8 %copy.22 = bf16[1,2,4,2048]{3,1,2,0:T(2,128)(2,1)S(1)} copy(bf16[1,2,4,2048]{3,2,1,0:T(4,128)(2,1)} %param.6) | data formatting | bytes 65536 | tf_op args[0]
  2.8 2.6 %collective-permute-start = (bf16[2,4,2048]{2,0,1:T(2,128)(2,1)S(1)}, bf16[2,4,2048]{2,0,1:T(2,128)(2,1)S(1)}, u32[]{:S(2)}, u32[]{:S(2)}) collective-permute-start(bf16[2,4,2048]{2,0,1:T(2,128)(2,1)S(1)} %bitcast.25), channel_id=1, source_target_pairs={{0,1},{1,0},{2,3},{3,2},{4,5},{5,4},{6,7},{7,6},{8,9},{9,8},{10,11... | collective-permute-start | bytes 98312 | tf_op jit(solution)/shard_map/ppermute | solution.py:96
  6.1 0.1 fusion.7
  6.2 0.6 copy.15
  6.8 0.0 copy-start
  6.8 8.2 %multiply_sine_fusion = (f32[32,128,1]{2,1,0:T(8,128)}, f32[32,128,1]{2,1,0:T(8,128)}) fusion(f32[32,128,1]{2,1,0:T(8,128)S(1)} %copy.15), kind=kLoop, calls=%fused_computation | loop fusion | flops 4096 | bytes 49152 | tf_op jit(solution)/shard_map/sin | solution.py:20
  15.1 0.0 collective-permute-done.1
  15.1 0.0 copy-done
  15.1 0.1 fusion.16
  15.2 1.6 %collective-permute-start.2 = (bf16[2,4,2048]{2,0,1:T(2,128)(2,1)S(1)}, bf16[2,4,2048]{2,0,1:T(2,128)(2,1)S(1)}, u32[]{:S(2)}, u32[]{:S(2)}) collective-permute-start(bf16[2,4,2048]{2,0,1:T(2,128)(2,1)S(1)} %fusion.16), channel_id=1, source_target_pairs={{0,4},{2,6},{4,0},{6,2},{8,12},{10,14},{12,8},{14,10},{16,20},{18,... | collective-permute-start | bytes 98312 | tf_op jit(solution)/shard_map/ppermute | solution.py:86
  16.8 0.1 fusion.10
  16.9 2.2 %collective-permute-done.2 = bf16[2,4,2048]{2,0,1:T(2,128)(2,1)S(1)} collective-permute-done((bf16[2,4,2048]{2,0,1:T(2,128)(2,1)S(1)}, bf16[2,4,2048]{2,0,1:T(2,128)(2,1)S(1)}, u32[]{:S(2)}, u32[]{:S(2)}) %collective-permute-start.2) | collective-permute-done | bytes 32800 | tf_op jit(solution)/shard_map/ppermute | solution.py:86
  19.2 1.6 %collective-permute-start.3 = (bf16[2,4,2048]{2,0,1:T(2,128)(2,1)S(1)}, bf16[2,4,2048]{2,0,1:T(2,128)(2,1)S(1)}, u32[]{:S(2)}, u32[]{:S(2)}) collective-permute-start(bf16[2,4,2048]{2,0,1:T(2,128)(2,1)S(1)} %add.78), channel_id=1, source_target_pairs={{0,8},{2,10},{4,12},{6,14},{8,0},{10,2},{12,4},{14,6},{16,24},{18,... | collective-permute-start | bytes 98312 | tf_op jit(solution)/shard_map/ppermute | solution.py:86
  20.8 2.3 %collective-permute-done.3 = bf16[2,4,2048]{2,0,1:T(2,128)(2,1)S(1)} collective-permute-done((bf16[2,4,2048]{2,0,1:T(2,128)(2,1)S(1)}, bf16[2,4,2048]{2,0,1:T(2,128)(2,1)S(1)}, u32[]{:S(2)}, u32[]{:S(2)}) %collective-permute-start.3) | collective-permute-done | bytes 32800 | tf_op jit(solution)/shard_map/ppermute | solution.py:86
  23.2 2.7 %collective-permute-start.4 = (bf16[2,4,2048]{2,0,1:T(2,128)(2,1)S(1)}, bf16[2,4,2048]{2,0,1:T(2,128)(2,1)S(1)}, u32[]{:S(2)}, u32[]{:S(2)}) collective-permute-start(bf16[2,4,2048]{2,0,1:T(2,128)(2,1)S(1)} %add.79), channel_id=1, source_target_pairs={{0,16},{2,18},{4,20},{6,22},{8,24},{10,26},{12,28},{14,30},{16,0},... | collective-permute-start | bytes 98312 | tf_op jit(solution)/shard_map/ppermute | solution.py:86
  25.9 0.1 fusion.15
  26.0 2.1 %collective-permute-done.4 = bf16[2,4,2048]{2,0,1:T(2,128)(2,1)S(1)} collective-permute-done((bf16[2,4,2048]{2,0,1:T(2,128)(2,1)S(1)}, bf16[2,4,2048]{2,0,1:T(2,128)(2,1)S(1)}, u32[]{:S(2)}, u32[]{:S(2)}) %collective-permute-start.4) | collective-permute-done | bytes 32800 | tf_op jit(solution)/shard_map/ppermute | solution.py:86
  28.1 0.3 collective-permute-start.5
  28.4 0.1 multiply_add_fusion
  29.1 0.1 copy.17
  29.3 1.6 %rev.18 = f32[512,128]{0,1:T(8,128)} reverse(f32[512,128]{0,1:T(8,128)S(1)} %copy.17), dimensions={0} | reverse | bytes 524288 | tf_op jit(solution)/shard_map/jit(_flip)/rev | solution.py:137
  30.9 0.1 copy.16
  31.0 1.6 %rev.17 = f32[512,128]{0,1:T(8,128)} reverse(f32[512,128]{0,1:T(8,128)S(1)} %copy.16), dimensions={0} | reverse | bytes 524288 | tf_op jit(solution)/shard_map/jit(_flip)/rev | solution.py:136
  32.6 0.0 collective-permute-done
  32.6 0.0 collective-permute-done.5
  32.6 0.2 broadcast_select_fusion
  32.8 0.6 rev.16
  33.5 0.7 convert_element_type.40.ref_ref
  34.2 3.0 %rev.15 = bf16[4,2,4096]{2,1,0:T(2,128)(2,1)S(1)} reverse(bf16[4,2,4096]{2,1,0:T(2,128)(2,1)S(1)} %get-tuple-element.14), dimensions={2} | reverse | bytes 131072 | tf_op jit(solution)/shard_map/jit(_flip)/rev | solution.py:122
  37.1 0.8 %pad_convert_fusion.wpad_ref = f32[4,2,5248]{2,1,0:T(2,128)} fusion(bf16[4,2,4096]{2,1,0:T(2,128)(2,1)S(1)} %rev.15), kind=kLoop, calls=%fused_computation.6 | loop fusion | flops 41984 | bytes 233472 | tf_op jit(solution)/shard_map/jit(_pad)/pad | solution.py:123
  38.0 38.4 %shard_map.64 = f32[6,2,128,128]{3,2,1,0:T(8,128)} custom-call(s32[6]{0:T(128)} %bitcast.27, s32[1]{0:T(128)S(6)} %copy.24.count_ref, f32[4,2,5248]{2,1,0:T(2,128)} %pad_convert_fusion.wpad_ref, f32[32,2,512]{2,1,0:T(2,128)} %convert_element_type.40.ref_ref, f32[32,128,1]{2,1,0:T(8,128)} %get-tuple-element.6.ac_ref, f32[32,128,1]{2,1,0:T(8,128)} %get-tuple-element.5.as_ref, ...), custom_call_target="tpu_custom_call" | custom-call | tf_op jit(solution)/shard_map/pallas_call | solution.py:142
  (6 shorter events, 0.1 us)
Async XLA Ops:
  1.5 13.5 %collective-permute-start.1 = (bf16[2,4,2048]{2,0,1:T(2,128)(2,1)S(1)}, bf16[2,4,2048]{2,0,1:T(2,128)(2,1)S(1)}, u32[]{:S(2)}, u32[]{:S(2)}) collective-permute-start(bf16[2,4,2048]{2,0,1:T(2,128)(2,1)S(1)} %broadcast_select_fusion.2), channel_id=1, source_target_pairs={{0,2},{2,0},{4,6},{6,4},{8,10},{10,8},{12,14},{14,12},{16,18},{18,... | collective-permute-start | bytes 98312 | tf_op jit(solution)/shard_map/ppermute | solution.py:86
  2.8 29.8 %collective-permute-start = (bf16[2,4,2048]{2,0,1:T(2,128)(2,1)S(1)}, bf16[2,4,2048]{2,0,1:T(2,128)(2,1)S(1)}, u32[]{:S(2)}, u32[]{:S(2)}) collective-permute-start(bf16[2,4,2048]{2,0,1:T(2,128)(2,1)S(1)} %bitcast.25), channel_id=1, source_target_pairs={{0,1},{1,0},{2,3},{3,2},{4,5},{5,4},{6,7},{7,6},{8,9},{9,8},{10,11... | collective-permute-start | bytes 98312 | tf_op jit(solution)/shard_map/ppermute | solution.py:96
  6.8 8.3 %copy-start = (bf16[1,2,4,2048]{3,2,1,0:T(4,128)(2,1)S(1)}, bf16[1,2,4,2048]{3,2,1,0:T(4,128)(2,1)}, u32[]{:S(2)}) copy-start(bf16[1,2,4,2048]{3,2,1,0:T(4,128)(2,1)} %param.7) | copy-start | bytes 98308
  15.2 4.0 %collective-permute-start.2 = (bf16[2,4,2048]{2,0,1:T(2,128)(2,1)S(1)}, bf16[2,4,2048]{2,0,1:T(2,128)(2,1)S(1)}, u32[]{:S(2)}, u32[]{:S(2)}) collective-permute-start(bf16[2,4,2048]{2,0,1:T(2,128)(2,1)S(1)} %fusion.16), channel_id=1, source_target_pairs={{0,4},{2,6},{4,0},{6,2},{8,12},{10,14},{12,8},{14,10},{16,20},{18,... | collective-permute-start | bytes 98312 | tf_op jit(solution)/shard_map/ppermute | solution.py:86
  19.2 4.0 %collective-permute-start.3 = (bf16[2,4,2048]{2,0,1:T(2,128)(2,1)S(1)}, bf16[2,4,2048]{2,0,1:T(2,128)(2,1)S(1)}, u32[]{:S(2)}, u32[]{:S(2)}) collective-permute-start(bf16[2,4,2048]{2,0,1:T(2,128)(2,1)S(1)} %add.78), channel_id=1, source_target_pairs={{0,8},{2,10},{4,12},{6,14},{8,0},{10,2},{12,4},{14,6},{16,24},{18,... | collective-permute-start | bytes 98312 | tf_op jit(solution)/shard_map/ppermute | solution.py:86
  23.2 4.9 %collective-permute-start.4 = (bf16[2,4,2048]{2,0,1:T(2,128)(2,1)S(1)}, bf16[2,4,2048]{2,0,1:T(2,128)(2,1)S(1)}, u32[]{:S(2)}, u32[]{:S(2)}) collective-permute-start(bf16[2,4,2048]{2,0,1:T(2,128)(2,1)S(1)} %add.79), channel_id=1, source_target_pairs={{0,16},{2,18},{4,20},{6,22},{8,24},{10,26},{12,28},{14,30},{16,0},... | collective-permute-start | bytes 98312 | tf_op jit(solution)/shard_map/ppermute | solution.py:86
  28.1 4.5 %collective-permute-start.5 = (bf16[2,4,2048]{2,0,1:T(2,128)(2,1)S(1)}, bf16[2,4,2048]{2,0,1:T(2,128)(2,1)S(1)}, u32[]{:S(2)}, u32[]{:S(2)}) collective-permute-start(bf16[2,4,2048]{2,0,1:T(2,128)(2,1)S(1)} %add.80), channel_id=1, source_target_pairs={{0,1},{1,0},{2,3},{3,2},{4,5},{5,4},{6,7},{7,6},{8,9},{9,8},{10,11... | collective-permute-start | bytes 98312 | tf_op jit(solution)/shard_map/ppermute | solution.py:96

commit v3 on v1

--- a/solution.py
+++ b/solution.py
@@ -18,6 +18,19 @@
     turns = jnp.mod(times[:, None] * freqs[None, :], window_len)
     angle = turns.astype(jnp.float32) * (2.0 * math.pi / window_len)
     return jnp.cos(angle), jnp.sin(angle)
+
+
+def reverse_rows(x):
+    n = x.shape[0]
+    rows = lax.broadcasted_iota(jnp.int32, (n, n), 0)
+    cols = lax.broadcasted_iota(jnp.int32, (n, n), 1)
+    flip = jnp.where(rows + cols == n - 1, 1.0, 0.0).astype(jnp.bfloat16)
+    high = x.astype(jnp.bfloat16)
+    rest = x - high.astype(jnp.float32)
+    mid = rest.astype(jnp.bfloat16)
+    low = (rest - mid.astype(jnp.float32)).astype(jnp.bfloat16)
+    turn = lambda piece: jnp.dot(flip, piece, preferred_element_type=jnp.float32)
+    return (turn(high) + turn(mid)) + turn(low)
 
 
 def caf_kernel(blocks_ref, count_ref, wpad_ref, ref_ref, ac_ref, as_ref, bc_ref, bs_ref,
@@ -73,8 +86,32 @@
             re = part[:LB, :LB] - part[LB:, LB:]
             im = part[:LB, LB:] + part[LB:, :LB]
             keep = q < count
-            out_ref[q, 0] = jnp.where(keep, re * norm, 0.0)
-            out_ref[q, 1] = jnp.where(keep, im * norm, 0.0)
+            out_ref[q, 0] = jnp.where(keep, reverse_rows(re) * norm, 0.0)
+            out_ref[q, 1] = jnp.where(keep, reverse_rows(im) * norm, 0.0)
+
+
+def butterfly_sum(value, axes):
+    count = lax.axis_size(axes)
+    if count & (count - 1):
+        return lax.psum(value, axes)
+    stride = 1
+    while stride < count:
+        radix = 4 if stride * 4 <= count else 2
+        parts = [lax.ppermute(value, axes, [(i, i ^ (m * stride)) for i in range(count)]) for m in range(1, radix)]
+        for part in parts:
+            value = value + part
+        stride *= radix
+    return value
+
+
+def seg_join(half, axis):
+    count = lax.axis_size(axis)
+    parts = lax.all_gather(half, axis, axis=half.ndim - 1, tiled=True) if count != 2 else None
+    if parts is not None:
+        return parts
+    other = lax.ppermute(half, axis, [(0, 1), (1, 0)])
+    first = lax.axis_index(axis) == 0
+    return jnp.where(first, jnp.concatenate([half, other], -1), jnp.concatenate([other, half], -1))
 
 
 def shards(surveillance, reference_blocks, owner_index, doppler_start, lag_blocks, block_count):
@@ -90,26 +127,32 @@
     bins = DOP // segments
     chunks = step_len // CHUNK
 
+    samples = seg_join(surveillance[0], "seg")
     mine = (owner_index == beam_place)[None, :, None]
-    cleaned = lax.psum(jnp.where(mine, reference_blocks[0], jnp.zeros_like(reference_blocks[0])), "beam")
-    both = jnp.stack([surveillance[0], cleaned])
-    both = lax.all_gather(both, "seg", axis=3, tiled=True)
-    samples = both[0]
-    refs = both[1]
+    local = jnp.where(mine, reference_blocks[0], jnp.zeros_like(reference_blocks[0]))
+    if segments == 2:
+        first = seg_place == 0
+        zero = jnp.zeros_like(local)
+        placed = jnp.where(first, jnp.concatenate([local, zero], -1), jnp.concatenate([zero, local], -1))
+        refs = butterfly_sum(placed, ("beam", "seg"))
+    else:
+        refs = seg_join(butterfly_sum(local, "beam"), "seg")
 
     span = step_len + rim_len
     wpad = jnp.transpose(samples, (1, 0, 2)).astype(jnp.float32)
     wpad = jnp.pad(wpad, ((0, 0), (0, 0), (0, span + LB - step_len)))
-    refrows = jnp.transpose(refs.reshape(2, step_count * chunks, CHUNK), (1, 0, 2))
-    refrows = refrows.astype(jnp.float32)
+    refrows = jnp.transpose(refs.reshape(2, step_count * chunks, CHUNK), (1, 0, 2)).astype(jnp.float32)
 
     freqs = doppler_start[0] + seg_place * bins + jnp.arange(bins, dtype=jnp.int32)
+    fine = 64
     a_c, a_s = phase_table(freqs, jnp.arange(step_count * chunks, dtype=jnp.int32) * CHUNK, window_len)
-    b_c, b_s = phase_table(freqs, jnp.arange(CHUNK, dtype=jnp.int32), window_len)
+    h_c, h_s = phase_table(freqs, jnp.arange(CHUNK // fine, dtype=jnp.int32) * fine, window_len)
+    l_c, l_s = phase_table(freqs, jnp.arange(fine, dtype=jnp.int32), window_len)
+    a_c, a_s, h_c, h_s, l_c, l_s = lax.optimization_barrier((a_c, a_s, h_c, h_s, l_c, l_s))
+    b_c = (h_c[:, None] * l_c[None] - h_s[:, None] * l_s[None]).reshape(CHUNK, bins).T
+    b_s = (h_s[:, None] * l_c[None] + h_c[:, None] * l_s[None]).reshape(CHUNK, bins).T
     a_c = a_c[:, :, None]
     a_s = a_s[:, :, None]
-    b_c = b_c.T
-    b_s = b_s.T
 
     kernel = functools.partial(caf_kernel, chunks=chunks, slots=slot_count, span=span,
                                norm=1.0 / math.sqrt(window_len))
@@ -128,7 +171,7 @@
         ),
         compiler_params=pltpu.CompilerParams(dimension_semantics=("arbitrary",)),
     )(lag_blocks[0], block_count, wpad, refrows, a_c, a_s, b_c, b_s)
-    return jnp.flip(out, axis=2)[None]
+    return out[None]
 
 
 def solution(mesh):

time: 130 us -> 66.9 us (0.51)
  blocking collectives: 67.9 us -> 0 us
  starting transfers between devices: 0 us -> 11.4 us
  other arithmetic: 13.3 us -> 3.87 us
  waiting for transfers between devices: 0 us -> 5.5 us
  local copies, waits for them, and re-layouts: 8.33 us -> 6.42 us
    psum x1 -> x0, blocking collectives: 63 us -> none  [shards(): lax.psum(jnp.where(mine, reference_blocks[0], jnp.zeros_like(reference_bl...]
    ppermute x0 -> x8, starting transfers between devices: none -> 11.4 us  [the longest x7 9.38 us: butterfly_sum(): lax.ppermute(value, axes, [(i, i ^ m * stride) for i in range(count)])]
    sin x2 -> x3, other arithmetic: 10.2 us -> 0.42 us  [phase_table(): return (jnp.cos(angle), jnp.sin(angle))]
    rev x1 -> x0, local copies, waits for them, and re-layouts: 6.8 us -> none  [shards(): return jnp.flip(out, axis=2)[None]]
    ppermute x0 -> x8, waiting for transfers between devices: none -> 5.5 us  [the longest x7 5.49 us: butterfly_sum(): lax.ppermute(value, axes, [(i, i ^ m * stride) for i in range(count)])]
    all_gather x1 -> x0, blocking collectives: 4.94 us -> none  [shards(): both = lax.all_gather(both, 'seg', axis=3, tiled=True)]
    broadcast_in_dim x0 -> x2, local copies, waits for them, and re-layouts: none -> 3.95 us  [the longest x1 1.98 us: shards(): a_c = a_c[:, :, None]]
  transfers between devices with their start and end apart: 0 -> 8, of which waited for: 0 -> 4; matrix products, arithmetic and copies ran while one was open for 0% -> 12% of each run, Pallas kernels for 0% -> 0%
where the time goes in v3:
time: 66.9 us; the launch traced here: 66.7 us
  Pallas kernels  38.1 us (57%)
  starting transfers between devices  11.4 us (17%)
  local copies, waits for them, and re-layouts  6.42 us (10%)
  waiting for transfers between devices  5.5 us (8%)
  other arithmetic  3.87 us (6%)
  between operations  1.38 us (2%)
    pallas_call x1, Pallas kernels, shards(): pl.pallas_call(kernel, out_shape=jax.ShapeDtypeStruct((slot_count, 2, LB,...  38.1 us
    ppermute x7, starting transfers between devices, butterfly_sum(): lax.ppermute(value, axes, [(i, i ^ m * stride) for i in range(count)])  9.38 us
    ppermute x7, waiting for transfers between devices, butterfly_sum(): lax.ppermute(value, axes, [(i, i ^ m * stride) for i in range(count)])  5.49 us
    ppermute x1, starting transfers between devices, seg_join(): other = lax.ppermute(half, axis, [(0, 1), (1, 0)])  2.05 us
    broadcast_in_dim x1, local copies, waits for them, and re-layouts, shards(): a_c = a_c[:, :, None]  1.98 us
    broadcast_in_dim x1, local copies, waits for them, and re-layouts, shards(): a_s = a_s[:, :, None]  1.97 us
  transfers between devices with their start and end apart: 8, of which 4 were waited for; matrix products, arithmetic and copies ran while one was open for 12% of the time, Pallas kernels for 0%

profile of v3, /device:TPU:0, one launch (start us, length us, event | category | flops | bytes accessed | tf_op | source)
XLA Modules:
  0.0 66.7 jit_solution(5781350687026614378)
XLA Ops:
  0.0 0.7 broadcast_compare_fusion
  0.7 0.9 %broadcast_select_fusion.2 = bf16[2,4,2048]{2,0,1:T(2,128)(2,1)S(1)} fusion(pred[4]{0:T(512)(128)(4,1)S(1)} %broadcast_compare_fusion, bf16[1,2,4,2048]{3,2,1,0:T(4,128)(2,1)} %param.7), kind=kLoop, calls=%fused_computation.9 | loop fusion | flops 16384 | bytes 65540 | tf_op jit(solution)/shard_map/jit(_where)/select_n | solution.py:132
  1.5 0.1 broadcast_select_fusion
  1.6 0.5 collective-permute-start.2
  2.1 2.6 %collective-permute-start.3 = (bf16[2,4,4096]{2,0,1:T(2,128)(2,1)S(1)}, bf16[2,4,4096]{2,0,1:T(2,128)(2,1)S(1)}, u32[]{:S(2)}, u32[]{:S(2)}) collective-permute-start(bf16[2,4,4096]{2,0,1:T(2,128)(2,1)S(1)} %broadcast_select_fusion), channel_id=1, source_target_pairs={{0,3},{1,2},{2,1},{3,0},{4,7},{5,6},{6,5},{7,4},{8,11},{9,10},{10,... | collective-permute-start | bytes 196616 | tf_op jit(solution)/shard_map/ppermute | solution.py:100
  4.7 0.0 collective-permute-start.1
  4.8 0.8 %copy.23 = bf16[1,2,4,2048]{3,1,2,0:T(2,128)(2,1)S(1)} copy(bf16[1,2,4,2048]{3,2,1,0:T(4,128)(2,1)} %param.6) | data formatting | bytes 65536 | tf_op args[0]
  5.6 2.0 %collective-permute-start = (bf16[2,4,2048]{2,0,1:T(2,128)(2,1)S(1)}, bf16[2,4,2048]{2,0,1:T(2,128)(2,1)S(1)}, u32[]{:S(2)}, u32[]{:S(2)}) collective-permute-start(bf16[2,4,2048]{2,0,1:T(2,128)(2,1)S(1)} %bitcast.34), channel_id=1, source_target_pairs={{0,1},{1,0},{2,3},{3,2},{4,5},{5,4},{6,7},{7,6},{8,9},{9,8},{10,11... | collective-permute-start | bytes 98312 | tf_op jit(solution)/shard_map/ppermute | solution.py:112
  8.3 0.1 fusion.10
  8.4 0.1 fusion.17
  8.5 0.2 fusion.12
  8.7 0.1 multiply_add_fusion
  9.4 0.8 %copy.18 = f32[512,128]{0,1:T(8,128)} copy(f32[512,128]{1,0:T(8,128)S(1)} %bitcast.29) | data formatting | bytes 524288 | tf_op jit(solution)/shard_map/add | solution.py:153
  10.3 0.8 %copy.17 = f32[512,128]{0,1:T(8,128)} copy(f32[512,128]{1,0:T(8,128)S(1)} %bitcast.28) | data formatting | bytes 524288 | tf_op jit(solution)/shard_map/sub | solution.py:152
  11.1 2.0 %copy.20.as_ref = f32[32,128,1]{2,1,0:T(8,128)} copy(f32[32,128,1]{1,0,2:T(8,128)S(1)} %bitcast.37) | data formatting | bytes 32768 | tf_op jit(solution)/shard_map/broadcast_in_dim | solution.py:155
  13.1 2.0 %copy.19.ac_ref = f32[32,128,1]{2,1,0:T(8,128)} copy(f32[32,128,1]{1,0,2:T(8,128)S(1)} %bitcast.36) | data formatting | bytes 32768 | tf_op jit(solution)/shard_map/broadcast_in_dim | solution.py:154
  15.1 0.0 collective-permute-done.2
  15.1 0.0 collective-permute-done.3
  15.1 0.0 collective-permute-done.1
  15.1 0.2 add_add_fusion.1
  15.3 2.6 %collective-permute-start.6 = (bf16[2,4,4096]{2,0,1:T(2,128)(2,1)S(1)}, bf16[2,4,4096]{2,0,1:T(2,128)(2,1)S(1)}, u32[]{:S(2)}, u32[]{:S(2)}) collective-permute-start(bf16[2,4,4096]{2,0,1:T(2,128)(2,1)S(1)} %add_add_fusion.1), channel_id=1, source_target_pairs={{0,12},{1,13},{2,14},{3,15},{4,8},{5,9},{6,10},{7,11},{8,4},{9,5},... | collective-permute-start | bytes 196616 | tf_op jit(solution)/shard_map/ppermute | solution.py:100
  17.9 0.4 collective-permute-start.5
  18.3 0.5 collective-permute-start.4
  18.8 0.0 collective-permute-done
  18.8 0.1 fusion
  18.9 2.2 %collective-permute-done.6 = bf16[2,4,4096]{2,0,1:T(2,128)(2,1)S(1)} collective-permute-done((bf16[2,4,4096]{2,0,1:T(2,128)(2,1)S(1)}, bf16[2,4,4096]{2,0,1:T(2,128)(2,1)S(1)}, u32[]{:S(2)}, u32[]{:S(2)}) %collective-permute-start.6) | collective-permute-done | bytes 65568 | tf_op jit(solution)/shard_map/ppermute | solution.py:100
  21.1 1.0 %collective-permute-done.5 = bf16[2,4,4096]{2,0,1:T(2,128)(2,1)S(1)} collective-permute-done((bf16[2,4,4096]{2,0,1:T(2,128)(2,1)S(1)}, bf16[2,4,4096]{2,0,1:T(2,128)(2,1)S(1)}, u32[]{:S(2)}, u32[]{:S(2)}) %collective-permute-start.5) | collective-permute-done | bytes 65568 | tf_op jit(solution)/shard_map/ppermute | solution.py:100
  22.1 0.4 collective-permute-done.4
  22.6 2.7 %collective-permute-start.7 = (bf16[2,4,4096]{2,0,1:T(2,128)(2,1)S(1)}, bf16[2,4,4096]{2,0,1:T(2,128)(2,1)S(1)}, u32[]{:S(2)}, u32[]{:S(2)}) collective-permute-start(bf16[2,4,4096]{2,0,1:T(2,128)(2,1)S(1)} %bitcast.30), channel_id=1, source_target_pairs={{0,16},{1,17},{2,18},{3,19},{4,20},{5,21},{6,22},{7,23},{8,24},{9,... | collective-permute-start | bytes 196616 | tf_op jit(solution)/shard_map/ppermute | solution.py:100
  25.2 0.7 %pad_convert_fusion.wpad_ref = f32[4,2,5248]{2,1,0:T(2,128)} fusion(bf16[4,2,4096]{2,1,0:T(2,128)(2,1)S(1)} %fusion), kind=kLoop, calls=%fused_computation.5 | loop fusion | flops 41984 | bytes 233472 | tf_op jit(solution)/shard_map/jit(_pad)/pad | solution.py:143
  26.0 1.8 %collective-permute-done.7 = bf16[2,4,4096]{2,0,1:T(2,128)(2,1)S(1)} collective-permute-done((bf16[2,4,4096]{2,0,1:T(2,128)(2,1)S(1)}, bf16[2,4,4096]{2,0,1:T(2,128)(2,1)S(1)}, u32[]{:S(2)}, u32[]{:S(2)}) %collective-permute-start.7) | collective-permute-done | bytes 65568 | tf_op jit(solution)/shard_map/ppermute | solution.py:100
  27.8 0.1 add.71
  27.9 0.7 %convert_bitcast_fusion.ref_ref = f32[32,2,512]{2,1,0:T(2,128)} fusion(bf16[2,32,512]{2,0,1:T(2,128)(2,1)S(1)} %bitcast.32), kind=kLoop, calls=%fused_computation.2 | loop fusion | flops 32768 | bytes 196608 | tf_op jit(solution)/shard_map/convert_element_type | solution.py:144
  28.6 38.1 %shard_map.64 = f32[6,2,128,128]{3,2,1,0:T(8,128)} custom-call(s32[6]{0:T(128)} %bitcast.41, s32[1]{0:T(128)S(6)} %copy.25.count_ref, f32[4,2,5248]{2,1,0:T(2,128)} %pad_convert_fusion.wpad_ref, f32[32,2,512]{2,1,0:T(2,128)} %convert_bitcast_fusion.ref_ref, f32[32,128,1]{2,1,0:T(8,128)} %copy.19.ac_ref, f32[32,128,1]{2,1,0:T(8,128)} %copy.20.as_ref, ...), custom_call_target="tpu_custom_call" | custom-call | tf_op jit(solution)/shard_map/pallas_call | solution.py:160
  (4 shorter events, 0.0 us)
Async XLA Ops:
  1.6 13.5 %collective-permute-start.2 = (bf16[2,4,4096]{2,0,1:T(2,128)(2,1)S(1)}, bf16[2,4,4096]{2,0,1:T(2,128)(2,1)S(1)}, u32[]{:S(2)}, u32[]{:S(2)}) collective-permute-start(bf16[2,4,4096]{2,0,1:T(2,128)(2,1)S(1)} %broadcast_select_fusion), channel_id=1, source_target_pairs={{0,2},{1,3},{2,0},{3,1},{4,6},{5,7},{6,4},{7,5},{8,10},{9,11},{10,... | collective-permute-start | bytes 196616 | tf_op jit(solution)/shard_map/ppermute | solution.py:100
  2.1 13.0 %collective-permute-start.3 = (bf16[2,4,4096]{2,0,1:T(2,128)(2,1)S(1)}, bf16[2,4,4096]{2,0,1:T(2,128)(2,1)S(1)}, u32[]{:S(2)}, u32[]{:S(2)}) collective-permute-start(bf16[2,4,4096]{2,0,1:T(2,128)(2,1)S(1)} %broadcast_select_fusion), channel_id=1, source_target_pairs={{0,3},{1,2},{2,1},{3,0},{4,7},{5,6},{6,5},{7,4},{8,11},{9,10},{10,... | collective-permute-start | bytes 196616 | tf_op jit(solution)/shard_map/ppermute | solution.py:100
  4.7 10.4 %collective-permute-start.1 = (bf16[2,4,4096]{2,0,1:T(2,128)(2,1)S(1)}, bf16[2,4,4096]{2,0,1:T(2,128)(2,1)S(1)}, u32[]{:S(2)}, u32[]{:S(2)}) collective-permute-start(bf16[2,4,4096]{2,0,1:T(2,128)(2,1)S(1)} %broadcast_select_fusion), channel_id=1, source_target_pairs={{0,1},{1,0},{2,3},{3,2},{4,5},{5,4},{6,7},{7,6},{8,9},{9,8},{10,11... | collective-permute-start | bytes 196616 | tf_op jit(solution)/shard_map/ppermute | solution.py:100
  5.6 13.3 %collective-permute-start = (bf16[2,4,2048]{2,0,1:T(2,128)(2,1)S(1)}, bf16[2,4,2048]{2,0,1:T(2,128)(2,1)S(1)}, u32[]{:S(2)}, u32[]{:S(2)}) collective-permute-start(bf16[2,4,2048]{2,0,1:T(2,128)(2,1)S(1)} %bitcast.34), channel_id=1, source_target_pairs={{0,1},{1,0},{2,3},{3,2},{4,5},{5,4},{6,7},{7,6},{8,9},{9,8},{10,11... | collective-permute-start | bytes 98312 | tf_op jit(solution)/shard_map/ppermute | solution.py:112
  15.3 5.9 %collective-permute-start.6 = (bf16[2,4,4096]{2,0,1:T(2,128)(2,1)S(1)}, bf16[2,4,4096]{2,0,1:T(2,128)(2,1)S(1)}, u32[]{:S(2)}, u32[]{:S(2)}) collective-permute-start(bf16[2,4,4096]{2,0,1:T(2,128)(2,1)S(1)} %add_add_fusion.1), channel_id=1, source_target_pairs={{0,12},{1,13},{2,14},{3,15},{4,8},{5,9},{6,10},{7,11},{8,4},{9,5},... | collective-permute-start | bytes 196616 | tf_op jit(solution)/shard_map/ppermute | solution.py:100
  17.9 4.3 %collective-permute-start.5 = (bf16[2,4,4096]{2,0,1:T(2,128)(2,1)S(1)}, bf16[2,4,4096]{2,0,1:T(2,128)(2,1)S(1)}, u32[]{:S(2)}, u32[]{:S(2)}) collective-permute-start(bf16[2,4,4096]{2,0,1:T(2,128)(2,1)S(1)} %add_add_fusion.1), channel_id=1, source_target_pairs={{0,8},{1,9},{2,10},{3,11},{4,12},{5,13},{6,14},{7,15},{8,0},{9,1},... | collective-permute-start | bytes 196616 | tf_op jit(solution)/shard_map/ppermute | solution.py:100
  18.3 4.3 %collective-permute-start.4 = (bf16[2,4,4096]{2,0,1:T(2,128)(2,1)S(1)}, bf16[2,4,4096]{2,0,1:T(2,128)(2,1)S(1)}, u32[]{:S(2)}, u32[]{:S(2)}) collective-permute-start(bf16[2,4,4096]{2,0,1:T(2,128)(2,1)S(1)} %add_add_fusion.1), channel_id=1, source_target_pairs={{0,4},{1,5},{2,6},{3,7},{4,0},{5,1},{6,2},{7,3},{8,12},{9,13},{10,... | collective-permute-start | bytes 196616 | tf_op jit(solution)/shard_map/ppermute | solution.py:100
  22.6 5.2 %collective-permute-start.7 = (bf16[2,4,4096]{2,0,1:T(2,128)(2,1)S(1)}, bf16[2,4,4096]{2,0,1:T(2,128)(2,1)S(1)}, u32[]{:S(2)}, u32[]{:S(2)}) collective-permute-start(bf16[2,4,4096]{2,0,1:T(2,128)(2,1)S(1)} %bitcast.30), channel_id=1, source_target_pairs={{0,16},{1,17},{2,18},{3,19},{4,20},{5,21},{6,22},{7,23},{8,24},{9,... | collective-permute-start | bytes 196616 | tf_op jit(solution)/shard_map/ppermute | solution.py:100

commit v4 on v3

--- a/solution.py
+++ b/solution.py
@@ -11,7 +11,8 @@
 LB = 128
 NLB = 8
 DOP = 256
-CHUNK = 512
+CHUNK = 2048
+PIECE = 1024
 
 
 def phase_table(freqs, times, window_len):
@@ -36,7 +37,7 @@
 def caf_kernel(blocks_ref, count_ref, wpad_ref, ref_ref, ac_ref, as_ref, bc_ref, bs_ref,
                out_ref, shifted, acc, *, chunks, slots, span, norm):
     k = pl.program_id(0)
-    lanes = CHUNK + LB
+    lanes = PIECE + LB
 
     @pl.when(k == 0)
     def _():
@@ -44,13 +45,13 @@
 
     for comp in range(2):
         def build(i, carry):
-            v0 = pl.multiple_of(i * CHUNK, CHUNK)
+            v0 = pl.multiple_of(i * PIECE, PIECE)
             win = wpad_ref[k, comp:comp + 1, pl.ds(v0, lanes)]
             tile = jnp.broadcast_to(win, (LB, lanes))
             rolled = pltpu.roll(tile, lanes - LB + 1, 1, stride=1, stride_axis=0)
-            shifted[comp * LB:(comp + 1) * LB, pl.ds(v0, CHUNK)] = rolled[:, :CHUNK].astype(jnp.bfloat16)
+            shifted[comp * LB:(comp + 1) * LB, pl.ds(v0, PIECE)] = rolled[:, :PIECE].astype(jnp.bfloat16)
             return carry
-        lax.fori_loop(0, span // CHUNK, build, 0)
+        lax.fori_loop(0, span // PIECE, build, 0)
 
     offsets = [jnp.maximum(blocks_ref[q], 0) * LB for q in range(slots)]
 

time: 66.9 us -> 54.2 us (0.81)
  Pallas kernels: 38.1 us -> 26.8 us
  local copies, waits for them, and re-layouts: 6.42 us -> 5.41 us
    pallas_call x1, Pallas kernels: 38.1 us -> 26.8 us  [shards(): pl.pallas_call(kernel, out_shape=jax.ShapeDtypeStruct((slot_count, 2, LB,...]
    broadcast_in_dim x1, local copies, waits for them, and re-layouts: 1.98 us -> 1.03 us  [shards(): a_c = a_c[:, :, None]]
    broadcast_in_dim x1, local copies, waits for them, and re-layouts: 1.97 us -> 1.04 us  [shards(): a_s = a_s[:, :, None]]
where the time goes in v4:
time: 54.2 us; the launch traced here: 53.9 us
  Pallas kernels  26.8 us (49%)
  starting transfers between devices  11.4 us (21%)
  waiting for transfers between devices  5.48 us (10%)
  local copies, waits for them, and re-layouts  5.41 us (10%)
  other arithmetic  3.47 us (6%)
  between operations  1.41 us (3%)
    pallas_call x1, Pallas kernels, shards(): pl.pallas_call(kernel, out_shape=jax.ShapeDtypeStruct((slot_count, 2, LB,...  26.8 us
    ppermute x7, starting transfers between devices, butterfly_sum(): lax.ppermute(value, axes, [(i, i ^ m * stride) for i in range(count)])  9.42 us
    ppermute x7, waiting for transfers between devices, butterfly_sum(): lax.ppermute(value, axes, [(i, i ^ m * stride) for i in range(count)])  5.48 us
    ppermute x1, starting transfers between devices, seg_join(): other = lax.ppermute(half, axis, [(0, 1), (1, 0)])  2 us
    add x1, local copies, waits for them, and re-layouts, shards(): h_s[:, None] * l_c[None] + h_c[:, None] * l_s[None]  1.34 us
    sub x1, local copies, waits for them, and re-layouts, shards(): h_c[:, None] * l_c[None] - h_s[:, None] * l_s[None]  1.31 us
  transfers between devices with their start and end apart: 8, of which 4 were waited for; matrix products, arithmetic and copies ran while one was open for 12% of the time, Pallas kernels for 0%

profile of v4, /device:TPU:0, one launch (start us, length us, event | category | flops | bytes accessed | tf_op | source)
XLA Modules:
  0.0 53.9 jit_solution(36950529823283308)
XLA Ops:
  0.0 0.0 copy-start.1
  0.0 0.7 %copy-done.1 = s32[4]{0:T(128)S(1)} copy-done((s32[4]{0:T(128)S(1)}, s32[4]{0:T(128)}, u32[]{:S(2)}) %copy-start.1) | copy-done | bytes 40
  0.7 0.9 %broadcast_select_fusion.2 = bf16[2,4,2048]{2,0,1:T(2,128)(2,1)S(1)} fusion(pred[4]{0:T(512)(128)(4,1)S(1)} %broadcast_compare_fusion, bf16[1,2,4,2048]{3,2,1,0:T(4,128)(2,1)} %param.7), kind=kLoop, calls=%fused_computation.9 | loop fusion | flops 16384 | bytes 65540 | tf_op jit(solution)/shard_map/jit(_where)/select_n | solution.py:133
  1.5 0.0 copy-start
  1.5 0.1 broadcast_select_fusion
  1.6 3.0 %collective-permute-start.1 = (bf16[2,4,4096]{2,0,1:T(2,128)(2,1)S(1)}, bf16[2,4,4096]{2,0,1:T(2,128)(2,1)S(1)}, u32[]{:S(2)}, u32[]{:S(2)}) collective-permute-start(bf16[2,4,4096]{2,0,1:T(2,128)(2,1)S(1)} %broadcast_select_fusion), channel_id=1, source_target_pairs={{0,1},{1,0},{2,3},{3,2},{4,5},{5,4},{6,7},{7,6},{8,9},{9,8},{10,11... | collective-permute-start | bytes 196616 | tf_op jit(solution)/shard_map/ppermute | solution.py:101
  4.6 0.0 collective-permute-start.2
  4.6 0.2 collective-permute-start.3
  4.8 0.0 copy-done
  4.8 2.0 %collective-permute-start = (bf16[2,4,2048]{2,0,1:T(2,128)(2,1)S(1)}, bf16[2,4,2048]{2,0,1:T(2,128)(2,1)S(1)}, u32[]{:S(2)}, u32[]{:S(2)}) collective-permute-start(bf16[2,4,2048]{2,0,1:T(2,128)(2,1)S(1)} %bitcast.34), channel_id=1, source_target_pairs={{0,1},{1,0},{2,3},{3,2},{4,5},{5,4},{6,7},{7,6},{8,9},{9,8},{10,11... | collective-permute-start | bytes 98312 | tf_op jit(solution)/shard_map/ppermute | solution.py:113
  7.5 0.1 fusion.10
  7.7 0.2 fusion.12
  7.8 0.1 fusion.17
  7.9 0.3 multiply_add_fusion
  8.3 1.3 %copy.17 = f32[2048,128]{0,1:T(8,128)} copy(f32[2048,128]{1,0:T(8,128)S(1)} %bitcast.27) | data formatting | bytes 2097152 | tf_op jit(solution)/shard_map/sub | solution.py:153
  9.6 1.3 %copy.18 = f32[2048,128]{0,1:T(8,128)} copy(f32[2048,128]{1,0:T(8,128)S(1)} %bitcast.26) | data formatting | bytes 2097152 | tf_op jit(solution)/shard_map/add | solution.py:154
  10.9 1.0 %copy.19.ac_ref = f32[8,128,1]{2,1,0:T(8,128)} copy(f32[8,128,1]{1,0,2:T(8,128)S(1)} %bitcast.40) | data formatting | bytes 8192 | tf_op jit(solution)/shard_map/broadcast_in_dim | solution.py:155
  11.9 1.0 %copy.20.as_ref = f32[8,128,1]{2,1,0:T(8,128)} copy(f32[8,128,1]{1,0,2:T(8,128)S(1)} %bitcast.39) | data formatting | bytes 8192 | tf_op jit(solution)/shard_map/broadcast_in_dim | solution.py:156
  13.6 0.0 collective-permute-done.1
  13.6 0.0 collective-permute-done.2
  13.6 0.0 collective-permute-done.3
  13.7 0.2 add_add_fusion.1
  13.8 2.6 %collective-permute-start.6 = (bf16[2,4,4096]{2,0,1:T(2,128)(2,1)S(1)}, bf16[2,4,4096]{2,0,1:T(2,128)(2,1)S(1)}, u32[]{:S(2)}, u32[]{:S(2)}) collective-permute-start(bf16[2,4,4096]{2,0,1:T(2,128)(2,1)S(1)} %add_add_fusion.1), channel_id=1, source_target_pairs={{0,12},{1,13},{2,14},{3,15},{4,8},{5,9},{6,10},{7,11},{8,4},{9,5},... | collective-permute-start | bytes 196616 | tf_op jit(solution)/shard_map/ppermute | solution.py:101
  16.4 0.4 collective-permute-start.5
  16.9 0.5 collective-permute-start.4
  17.4 0.0 collective-permute-done
  17.4 0.1 fusion
  17.5 2.2 %collective-permute-done.6 = bf16[2,4,4096]{2,0,1:T(2,128)(2,1)S(1)} collective-permute-done((bf16[2,4,4096]{2,0,1:T(2,128)(2,1)S(1)}, bf16[2,4,4096]{2,0,1:T(2,128)(2,1)S(1)}, u32[]{:S(2)}, u32[]{:S(2)}) %collective-permute-start.6) | collective-permute-done | bytes 65568 | tf_op jit(solution)/shard_map/ppermute | solution.py:101
  19.7 1.0 %collective-permute-done.5 = bf16[2,4,4096]{2,0,1:T(2,128)(2,1)S(1)} collective-permute-done((bf16[2,4,4096]{2,0,1:T(2,128)(2,1)S(1)}, bf16[2,4,4096]{2,0,1:T(2,128)(2,1)S(1)}, u32[]{:S(2)}, u32[]{:S(2)}) %collective-permute-start.5) | collective-permute-done | bytes 65568 | tf_op jit(solution)/shard_map/ppermute | solution.py:101
  20.7 0.4 collective-permute-done.4
  21.2 2.7 %collective-permute-start.7 = (bf16[2,4,4096]{2,0,1:T(2,128)(2,1)S(1)}, bf16[2,4,4096]{2,0,1:T(2,128)(2,1)S(1)}, u32[]{:S(2)}, u32[]{:S(2)}) collective-permute-start(bf16[2,4,4096]{2,0,1:T(2,128)(2,1)S(1)} %bitcast.30), channel_id=1, source_target_pairs={{0,16},{1,17},{2,18},{3,19},{4,20},{5,21},{6,22},{7,23},{8,24},{9,... | collective-permute-start | bytes 196616 | tf_op jit(solution)/shard_map/ppermute | solution.py:101
  23.8 0.8 %pad_convert_fusion.wpad_ref = f32[4,2,5248]{2,1,0:T(2,128)} fusion(bf16[4,2,4096]{2,1,0:T(2,128)(2,1)S(1)} %fusion), kind=kLoop, calls=%fused_computation.5 | loop fusion | flops 41984 | bytes 233472 | tf_op jit(solution)/shard_map/jit(_pad)/pad | solution.py:144
  24.6 1.8 %collective-permute-done.7 = bf16[2,4,4096]{2,0,1:T(2,128)(2,1)S(1)} collective-permute-done((bf16[2,4,4096]{2,0,1:T(2,128)(2,1)S(1)}, bf16[2,4,4096]{2,0,1:T(2,128)(2,1)S(1)}, u32[]{:S(2)}, u32[]{:S(2)}) %collective-permute-start.7) | collective-permute-done | bytes 65568 | tf_op jit(solution)/shard_map/ppermute | solution.py:101
  26.4 0.1 add.71
  26.5 0.7 %convert_bitcast_fusion.ref_ref = f32[8,2,2048]{2,1,0:T(2,128)} fusion(bf16[2,8,2048]{2,0,1:T(2,128)(2,1)S(1)} %bitcast.32), kind=kLoop, calls=%fused_computation.2 | loop fusion | flops 32768 | bytes 196608 | tf_op jit(solution)/shard_map/convert_element_type | solution.py:145
  27.2 26.8 %shard_map.64 = f32[6,2,128,128]{3,2,1,0:T(8,128)} custom-call(s32[6]{0:T(128)} %bitcast.41, s32[1]{0:T(128)S(6)} %copy.25.count_ref, f32[4,2,5248]{2,1,0:T(2,128)} %pad_convert_fusion.wpad_ref, f32[8,2,2048]{2,1,0:T(2,128)} %convert_bitcast_fusion.ref_ref, f32[8,128,1]{2,1,0:T(8,128)} %copy.19.ac_ref, f32[8,128,1]{2,1,0:T(8,128)} %copy.20.as_ref, ...), custom_call_target="tpu_custom_call" | custom-call | tf_op jit(solution)/shard_map/pallas_call | solution.py:161
  (6 shorter events, 0.1 us)
Async XLA Ops:
  0.0 0.7 %copy-start.1 = (s32[4]{0:T(128)S(1)}, s32[4]{0:T(128)}, u32[]{:S(2)}) copy-start(s32[4]{0:T(128)} %param.8) | copy-start | bytes 52
  1.5 3.3 %copy-start = (bf16[1,2,4,2048]{3,2,1,0:T(4,128)(2,1)S(1)}, bf16[1,2,4,2048]{3,2,1,0:T(4,128)(2,1)}, u32[]{:S(2)}) copy-start(bf16[1,2,4,2048]{3,2,1,0:T(4,128)(2,1)} %param.6) | copy-start | bytes 98308
  1.6 12.0 %collective-permute-start.1 = (bf16[2,4,4096]{2,0,1:T(2,128)(2,1)S(1)}, bf16[2,4,4096]{2,0,1:T(2,128)(2,1)S(1)}, u32[]{:S(2)}, u32[]{:S(2)}) collective-permute-start(bf16[2,4,4096]{2,0,1:T(2,128)(2,1)S(1)} %broadcast_select_fusion), channel_id=1, source_target_pairs={{0,1},{1,0},{2,3},{3,2},{4,5},{5,4},{6,7},{7,6},{8,9},{9,8},{10,11... | collective-permute-start | bytes 196616 | tf_op jit(solution)/shard_map/ppermute | solution.py:101
  4.6 9.0 %collective-permute-start.2 = (bf16[2,4,4096]{2,0,1:T(2,128)(2,1)S(1)}, bf16[2,4,4096]{2,0,1:T(2,128)(2,1)S(1)}, u32[]{:S(2)}, u32[]{:S(2)}) collective-permute-start(bf16[2,4,4096]{2,0,1:T(2,128)(2,1)S(1)} %broadcast_select_fusion), channel_id=1, source_target_pairs={{0,2},{1,3},{2,0},{3,1},{4,6},{5,7},{6,4},{7,5},{8,10},{9,11},{10,... | collective-permute-start | bytes 196616 | tf_op jit(solution)/shard_map/ppermute | solution.py:101
  4.6 9.0 %collective-permute-start.3 = (bf16[2,4,4096]{2,0,1:T(2,128)(2,1)S(1)}, bf16[2,4,4096]{2,0,1:T(2,128)(2,1)S(1)}, u32[]{:S(2)}, u32[]{:S(2)}) collective-permute-start(bf16[2,4,4096]{2,0,1:T(2,128)(2,1)S(1)} %broadcast_select_fusion), channel_id=1, source_target_pairs={{0,3},{1,2},{2,1},{3,0},{4,7},{5,6},{6,5},{7,4},{8,11},{9,10},{10,... | collective-permute-start | bytes 196616 | tf_op jit(solution)/shard_map/ppermute | solution.py:101
  4.8 12.6 %collective-permute-start = (bf16[2,4,2048]{2,0,1:T(2,128)(2,1)S(1)}, bf16[2,4,2048]{2,0,1:T(2,128)(2,1)S(1)}, u32[]{:S(2)}, u32[]{:S(2)}) collective-permute-start(bf16[2,4,2048]{2,0,1:T(2,128)(2,1)S(1)} %bitcast.34), channel_id=1, source_target_pairs={{0,1},{1,0},{2,3},{3,2},{4,5},{5,4},{6,7},{7,6},{8,9},{9,8},{10,11... | collective-permute-start | bytes 98312 | tf_op jit(solution)/shard_map/ppermute | solution.py:113
  13.8 5.9 %collective-permute-start.6 = (bf16[2,4,4096]{2,0,1:T(2,128)(2,1)S(1)}, bf16[2,4,4096]{2,0,1:T(2,128)(2,1)S(1)}, u32[]{:S(2)}, u32[]{:S(2)}) collective-permute-start(bf16[2,4,4096]{2,0,1:T(2,128)(2,1)S(1)} %add_add_fusion.1), channel_id=1, source_target_pairs={{0,12},{1,13},{2,14},{3,15},{4,8},{5,9},{6,10},{7,11},{8,4},{9,5},... | collective-permute-start | bytes 196616 | tf_op jit(solution)/shard_map/ppermute | solution.py:101
  16.4 4.3 %collective-permute-start.5 = (bf16[2,4,4096]{2,0,1:T(2,128)(2,1)S(1)}, bf16[2,4,4096]{2,0,1:T(2,128)(2,1)S(1)}, u32[]{:S(2)}, u32[]{:S(2)}) collective-permute-start(bf16[2,4,4096]{2,0,1:T(2,128)(2,1)S(1)} %add_add_fusion.1), channel_id=1, source_target_pairs={{0,8},{1,9},{2,10},{3,11},{4,12},{5,13},{6,14},{7,15},{8,0},{9,1},... | collective-permute-start | bytes 196616 | tf_op jit(solution)/shard_map/ppermute | solution.py:101
  16.9 4.3 %collective-permute-start.4 = (bf16[2,4,4096]{2,0,1:T(2,128)(2,1)S(1)}, bf16[2,4,4096]{2,0,1:T(2,128)(2,1)S(1)}, u32[]{:S(2)}, u32[]{:S(2)}) collective-permute-start(bf16[2,4,4096]{2,0,1:T(2,128)(2,1)S(1)} %add_add_fusion.1), channel_id=1, source_target_pairs={{0,4},{1,5},{2,6},{3,7},{4,0},{5,1},{6,2},{7,3},{8,12},{9,13},{10,... | collective-permute-start | bytes 196616 | tf_op jit(solution)/shard_map/ppermute | solution.py:101
  21.2 5.2 %collective-permute-start.7 = (bf16[2,4,4096]{2,0,1:T(2,128)(2,1)S(1)}, bf16[2,4,4096]{2,0,1:T(2,128)(2,1)S(1)}, u32[]{:S(2)}, u32[]{:S(2)}) collective-permute-start(bf16[2,4,4096]{2,0,1:T(2,128)(2,1)S(1)} %bitcast.30), channel_id=1, source_target_pairs={{0,16},{1,17},{2,18},{3,19},{4,20},{5,21},{6,22},{7,23},{8,24},{9,... | collective-permute-start | bytes 196616 | tf_op jit(solution)/shard_map/ppermute | solution.py:101

commit v5 on v4

--- a/solution.py
+++ b/solution.py
@@ -35,51 +35,55 @@
 
 
 def caf_kernel(blocks_ref, count_ref, wpad_ref, ref_ref, ac_ref, as_ref, bc_ref, bs_ref,
-               out_ref, shifted, acc, *, chunks, slots, span, norm):
-    k = pl.program_id(0)
+               out_ref, first_buf, second_buf, acc, *, chunks, slots, span, steps, norm):
+    pair = pl.program_id(0)
     lanes = PIECE + LB
+    pieces = [(comp, i) for comp in range(2) for i in range(span // PIECE)]
+    share = -(-len(pieces) // chunks)
 
-    @pl.when(k == 0)
+    def build_piece(step, comp, i, dst):
+        v0 = i * PIECE
+        win = wpad_ref[step, comp:comp + 1, v0:v0 + lanes]
+        tile = jnp.broadcast_to(win, (LB, lanes))
+        rolled = pltpu.roll(tile, lanes - LB + 1, 1, stride=1, stride_axis=0)
+        dst[comp * LB:(comp + 1) * LB, v0:v0 + PIECE] = rolled[:, :PIECE].astype(jnp.bfloat16)
+
+    @pl.when(pair == 0)
     def _():
         acc[...] = jnp.zeros_like(acc)
-
-    for comp in range(2):
-        def build(i, carry):
-            v0 = pl.multiple_of(i * PIECE, PIECE)
-            win = wpad_ref[k, comp:comp + 1, pl.ds(v0, lanes)]
-            tile = jnp.broadcast_to(win, (LB, lanes))
-            rolled = pltpu.roll(tile, lanes - LB + 1, 1, stride=1, stride_axis=0)
-            shifted[comp * LB:(comp + 1) * LB, pl.ds(v0, PIECE)] = rolled[:, :PIECE].astype(jnp.bfloat16)
-            return carry
-        lax.fori_loop(0, span // PIECE, build, 0)
+        for comp, i in pieces:
+            build_piece(0, comp, i, first_buf)
 
     offsets = [jnp.maximum(blocks_ref[q], 0) * LB for q in range(slots)]
 
-    def chunk(c, carry):
-        g = k * chunks + c
-        rr = ref_ref[g]
-        r_re = rr[0:1, :]
-        r_im = rr[1:2, :]
-        a_c = jnp.broadcast_to(ac_ref[g], (LB, CHUNK))
-        a_s = jnp.broadcast_to(as_ref[g], (LB, CHUNK))
-        b_c = bc_ref[...]
-        b_s = bs_ref[...]
-        cos_part = a_c * b_c - a_s * b_s
-        sine_part = a_s * b_c + a_c * b_s
-        c_re = (r_re * cos_part - r_im * sine_part).astype(jnp.bfloat16)
-        c_im = (0.0 - (r_re * sine_part + r_im * cos_part)).astype(jnp.bfloat16)
-        coef = jnp.concatenate([c_re, c_im], axis=0)
-        base = c * CHUNK
-        for q in range(slots):
-            off = pl.multiple_of(offsets[q] + base, LB)
-            hank = shifted[:, pl.ds(off, CHUNK)]
-            acc[q] += lax.dot_general(hank, coef, (((1,), (1,)), ((), ())),
-                                      preferred_element_type=jnp.float32)
-        return carry
+    def one_step(step, cur, nxt, next_step):
+        for c in range(chunks):
+            g = step * chunks + c
+            rr = ref_ref[g]
+            r_re = rr[0:1, :]
+            r_im = rr[1:2, :]
+            a_c = jnp.broadcast_to(ac_ref[g], (LB, CHUNK))
+            a_s = jnp.broadcast_to(as_ref[g], (LB, CHUNK))
+            b_c = bc_ref[...]
+            b_s = bs_ref[...]
+            cos_part = a_c * b_c - a_s * b_s
+            sine_part = a_s * b_c + a_c * b_s
+            c_re = (r_re * cos_part - r_im * sine_part).astype(jnp.bfloat16)
+            c_im = (0.0 - (r_re * sine_part + r_im * cos_part)).astype(jnp.bfloat16)
+            coef = jnp.concatenate([c_re, c_im], axis=0)
+            for q in range(slots):
+                off = pl.multiple_of(offsets[q] + c * CHUNK, LB)
+                hank = cur[:, pl.ds(off, CHUNK)]
+                acc[q] += lax.dot_general(hank, coef, (((1,), (1,)), ((), ())),
+                                          preferred_element_type=jnp.float32)
+            for comp, i in pieces[c * share:(c + 1) * share]:
+                build_piece(next_step, comp, i, nxt)
 
-    lax.fori_loop(0, chunks, chunk, 0)
+    step = 2 * pair
+    one_step(step, first_buf, second_buf, step + 1)
+    one_step(step + 1, second_buf, first_buf, jnp.minimum(step + 2, steps - 1))
 
-    @pl.when(k == pl.num_programs(0) - 1)
+    @pl.when(pair == pl.num_programs(0) - 1)
     def _():
         count = count_ref[0]
         for q in range(slots):
@@ -155,7 +159,8 @@
     a_c = a_c[:, :, None]
     a_s = a_s[:, :, None]
 
-    kernel = functools.partial(caf_kernel, chunks=chunks, slots=slot_count, span=span,
+    assert step_count % 2 == 0
+    kernel = functools.partial(caf_kernel, chunks=chunks, slots=slot_count, span=span, steps=step_count,
                                norm=1.0 / math.sqrt(window_len))
     full = lambda shape: pl.BlockSpec(shape, lambda k, *_: (0,) * len(shape))
     out = pl.pallas_call(
@@ -163,11 +168,11 @@
         out_shape=jax.ShapeDtypeStruct((slot_count, 2, LB, bins), jnp.float32),
         grid_spec=pltpu.PrefetchScalarGridSpec(
             num_scalar_prefetch=2,
-            grid=(step_count,),
+            grid=(step_count // 2,),
             in_specs=[full(wpad.shape), full(refrows.shape), full(a_c.shape), full(a_s.shape),
                       full(b_c.shape), full(b_s.shape)],
             out_specs=full((slot_count, 2, LB, bins)),
-            scratch_shapes=[pltpu.VMEM((2 * LB, span), jnp.bfloat16),
+            scratch_shapes=[pltpu.VMEM((2 * LB, span), jnp.bfloat16), pltpu.VMEM((2 * LB, span), jnp.bfloat16),
                             pltpu.VMEM((slot_count, 2 * LB, 2 * bins), jnp.float32)],
         ),
         compiler_params=pltpu.CompilerParams(dimension_semantics=("arbitrary",)),

time: 54.2 us -> 47.5 us (0.88)
  Pallas kernels: 26.8 us -> 19.8 us
    pallas_call x1, Pallas kernels: 26.8 us -> 19.8 us  [shards(): pl.pallas_call(kernel, out_shape=jax.ShapeDtypeStruct((slot_count, 2, LB,...]
  transfers between devices with their start and end apart: 8 -> 8, of which waited for: 4 -> 4; matrix products, arithmetic and copies ran while one was open for 12% -> 14% of each run, Pallas kernels for 0% -> 0%
where the time goes in v5:
time: 47.5 us; the launch traced here: 47 us
  Pallas kernels  19.8 us (42%)
  starting transfers between devices  11.4 us (24%)
  waiting for transfers between devices  5.48 us (12%)
  local copies, waits for them, and re-layouts  5.41 us (11%)
  other arithmetic  3.47 us (7%)
  between operations  1.41 us (3%)
    pallas_call x1, Pallas kernels, shards(): pl.pallas_call(kernel, out_shape=jax.ShapeDtypeStruct((slot_count, 2, LB,...  19.8 us
    ppermute x7, starting transfers between devices, butterfly_sum(): lax.ppermute(value, axes, [(i, i ^ m * stride) for i in range(count)])  9.42 us
    ppermute x7, waiting for transfers between devices, butterfly_sum(): lax.ppermute(value, axes, [(i, i ^ m * stride) for i in range(count)])  5.48 us
    ppermute x1, starting transfers between devices, seg_join(): other = lax.ppermute(half, axis, [(0, 1), (1, 0)])  2 us
    add x1, local copies, waits for them, and re-layouts, shards(): h_s[:, None] * l_c[None] + h_c[:, None] * l_s[None]  1.34 us
    sub x1, local copies, waits for them, and re-layouts, shards(): h_c[:, None] * l_c[None] - h_s[:, None] * l_s[None]  1.31 us
    broadcast_in_dim x1, local copies, waits for them, and re-layouts, shards(): a_s = a_s[:, :, None]  1.04 us
    broadcast_in_dim x1, local copies, waits for them, and re-layouts, shards(): a_c = a_c[:, :, None]  1.03 us
  transfers between devices with their start and end apart: 8, of which 4 were waited for; matrix products, arithmetic and copies ran while one was open for 14% of the time, Pallas kernels for 0%

profile of v5, /device:TPU:0, one launch (start us, length us, event | category | flops | bytes accessed | tf_op | source)
XLA Modules:
  0.0 47.0 jit_solution(7081090167013255324)
XLA Ops:
  0.0 0.0 copy-start.1
  0.0 0.7 %copy-done.1 = s32[4]{0:T(128)S(1)} copy-done((s32[4]{0:T(128)S(1)}, s32[4]{0:T(128)}, u32[]{:S(2)}) %copy-start.1) | copy-done | bytes 40
  0.7 0.9 %broadcast_select_fusion.2 = bf16[2,4,2048]{2,0,1:T(2,128)(2,1)S(1)} fusion(pred[4]{0:T(512)(128)(4,1)S(1)} %broadcast_compare_fusion, bf16[1,2,4,2048]{3,2,1,0:T(4,128)(2,1)} %param.7), kind=kLoop, calls=%fused_computation.9 | loop fusion | flops 16384 | bytes 65540 | tf_op jit(solution)/shard_map/jit(_where)/select_n | solution.py:137
  1.5 0.0 copy-start
  1.5 0.1 broadcast_select_fusion
  1.6 3.0 %collective-permute-start.1 = (bf16[2,4,4096]{2,0,1:T(2,128)(2,1)S(1)}, bf16[2,4,4096]{2,0,1:T(2,128)(2,1)S(1)}, u32[]{:S(2)}, u32[]{:S(2)}) collective-permute-start(bf16[2,4,4096]{2,0,1:T(2,128)(2,1)S(1)} %broadcast_select_fusion), channel_id=1, source_target_pairs={{0,1},{1,0},{2,3},{3,2},{4,5},{5,4},{6,7},{7,6},{8,9},{9,8},{10,11... | collective-permute-start | bytes 196616 | tf_op jit(solution)/shard_map/ppermute | solution.py:105
  4.6 0.0 collective-permute-start.2
  4.6 0.2 collective-permute-start.3
  4.8 0.0 copy-done
  4.8 2.0 %collective-permute-start = (bf16[2,4,2048]{2,0,1:T(2,128)(2,1)S(1)}, bf16[2,4,2048]{2,0,1:T(2,128)(2,1)S(1)}, u32[]{:S(2)}, u32[]{:S(2)}) collective-permute-start(bf16[2,4,2048]{2,0,1:T(2,128)(2,1)S(1)} %bitcast.34), channel_id=1, source_target_pairs={{0,1},{1,0},{2,3},{3,2},{4,5},{5,4},{6,7},{7,6},{8,9},{9,8},{10,11... | collective-permute-start | bytes 98312 | tf_op jit(solution)/shard_map/ppermute | solution.py:117
  7.5 0.1 fusion.10
  7.7 0.2 fusion.12
  7.8 0.1 fusion.17
  7.9 0.3 multiply_add_fusion
  8.3 1.3 %copy.17 = f32[2048,128]{0,1:T(8,128)} copy(f32[2048,128]{1,0:T(8,128)S(1)} %bitcast.27) | data formatting | bytes 2097152 | tf_op jit(solution)/shard_map/sub | solution.py:157
  9.6 1.3 %copy.18 = f32[2048,128]{0,1:T(8,128)} copy(f32[2048,128]{1,0:T(8,128)S(1)} %bitcast.26) | data formatting | bytes 2097152 | tf_op jit(solution)/shard_map/add | solution.py:158
  10.9 1.0 %copy.19.ac_ref = f32[8,128,1]{2,1,0:T(8,128)} copy(f32[8,128,1]{1,0,2:T(8,128)S(1)} %bitcast.40) | data formatting | bytes 8192 | tf_op jit(solution)/shard_map/broadcast_in_dim | solution.py:159
  11.9 1.0 %copy.20.as_ref = f32[8,128,1]{2,1,0:T(8,128)} copy(f32[8,128,1]{1,0,2:T(8,128)S(1)} %bitcast.39) | data formatting | bytes 8192 | tf_op jit(solution)/shard_map/broadcast_in_dim | solution.py:160
  13.6 0.0 collective-permute-done.1
  13.6 0.0 collective-permute-done.2
  13.6 0.0 collective-permute-done.3
  13.7 0.2 add_add_fusion.1
  13.8 2.6 %collective-permute-start.6 = (bf16[2,4,4096]{2,0,1:T(2,128)(2,1)S(1)}, bf16[2,4,4096]{2,0,1:T(2,128)(2,1)S(1)}, u32[]{:S(2)}, u32[]{:S(2)}) collective-permute-start(bf16[2,4,4096]{2,0,1:T(2,128)(2,1)S(1)} %add_add_fusion.1), channel_id=1, source_target_pairs={{0,12},{1,13},{2,14},{3,15},{4,8},{5,9},{6,10},{7,11},{8,4},{9,5},... | collective-permute-start | bytes 196616 | tf_op jit(solution)/shard_map/ppermute | solution.py:105
  16.4 0.4 collective-permute-start.5
  16.9 0.5 %collective-permute-start.4 = (bf16[2,4,4096]{2,0,1:T(2,128)(2,1)S(1)}, bf16[2,4,4096]{2,0,1:T(2,128)(2,1)S(1)}, u32[]{:S(2)}, u32[]{:S(2)}) collective-permute-start(bf16[2,4,4096]{2,0,1:T(2,128)(2,1)S(1)} %add_add_fusion.1), channel_id=1, source_target_pairs={{0,4},{1,5},{2,6},{3,7},{4,0},{5,1},{6,2},{7,3},{8,12},{9,13},{10,... | collective-permute-start | bytes 196616 | tf_op jit(solution)/shard_map/ppermute | solution.py:105
  17.4 0.0 collective-permute-done
  17.4 0.1 fusion
  17.5 2.2 %collective-permute-done.6 = bf16[2,4,4096]{2,0,1:T(2,128)(2,1)S(1)} collective-permute-done((bf16[2,4,4096]{2,0,1:T(2,128)(2,1)S(1)}, bf16[2,4,4096]{2,0,1:T(2,128)(2,1)S(1)}, u32[]{:S(2)}, u32[]{:S(2)}) %collective-permute-start.6) | collective-permute-done | bytes 65568 | tf_op jit(solution)/shard_map/ppermute | solution.py:105
  19.7 1.0 %collective-permute-done.5 = bf16[2,4,4096]{2,0,1:T(2,128)(2,1)S(1)} collective-permute-done((bf16[2,4,4096]{2,0,1:T(2,128)(2,1)S(1)}, bf16[2,4,4096]{2,0,1:T(2,128)(2,1)S(1)}, u32[]{:S(2)}, u32[]{:S(2)}) %collective-permute-start.5) | collective-permute-done | bytes 65568 | tf_op jit(solution)/shard_map/ppermute | solution.py:105
  20.7 0.4 collective-permute-done.4
  21.2 2.7 %collective-permute-start.7 = (bf16[2,4,4096]{2,0,1:T(2,128)(2,1)S(1)}, bf16[2,4,4096]{2,0,1:T(2,128)(2,1)S(1)}, u32[]{:S(2)}, u32[]{:S(2)}) collective-permute-start(bf16[2,4,4096]{2,0,1:T(2,128)(2,1)S(1)} %bitcast.30), channel_id=1, source_target_pairs={{0,16},{1,17},{2,18},{3,19},{4,20},{5,21},{6,22},{7,23},{8,24},{9,... | collective-permute-start | bytes 196616 | tf_op jit(solution)/shard_map/ppermute | solution.py:105
  23.8 0.8 %pad_convert_fusion.wpad_ref = f32[4,2,5248]{2,1,0:T(2,128)} fusion(bf16[4,2,4096]{2,1,0:T(2,128)(2,1)S(1)} %fusion), kind=kLoop, calls=%fused_computation.5 | loop fusion | flops 41984 | bytes 233472 | tf_op jit(solution)/shard_map/jit(_pad)/pad | solution.py:148
  24.6 1.8 %collective-permute-done.7 = bf16[2,4,4096]{2,0,1:T(2,128)(2,1)S(1)} collective-permute-done((bf16[2,4,4096]{2,0,1:T(2,128)(2,1)S(1)}, bf16[2,4,4096]{2,0,1:T(2,128)(2,1)S(1)}, u32[]{:S(2)}, u32[]{:S(2)}) %collective-permute-start.7) | collective-permute-done | bytes 65568 | tf_op jit(solution)/shard_map/ppermute | solution.py:105
  26.4 0.1 add.71
  26.5 0.7 %convert_bitcast_fusion.ref_ref = f32[8,2,2048]{2,1,0:T(2,128)} fusion(bf16[2,8,2048]{2,0,1:T(2,128)(2,1)S(1)} %bitcast.32), kind=kLoop, calls=%fused_computation.2 | loop fusion | flops 32768 | bytes 196608 | tf_op jit(solution)/shard_map/convert_element_type | solution.py:149
  27.2 19.8 %shard_map.64 = f32[6,2,128,128]{3,2,1,0:T(8,128)} custom-call(s32[6]{0:T(128)} %bitcast.41, s32[1]{0:T(128)S(6)} %copy.25.count_ref, f32[4,2,5248]{2,1,0:T(2,128)} %pad_convert_fusion.wpad_ref, f32[8,2,2048]{2,1,0:T(2,128)} %convert_bitcast_fusion.ref_ref, f32[8,128,1]{2,1,0:T(8,128)} %copy.19.ac_ref, f32[8,128,1]{2,1,0:T(8,128)} %copy.20.as_ref, ...), custom_call_target="tpu_custom_call" | custom-call | tf_op jit(solution)/shard_map/pallas_call | solution.py:166
  (6 shorter events, 0.1 us)
Async XLA Ops:
  0.0 0.7 %copy-start.1 = (s32[4]{0:T(128)S(1)}, s32[4]{0:T(128)}, u32[]{:S(2)}) copy-start(s32[4]{0:T(128)} %param.8) | copy-start | bytes 52
  1.5 3.3 %copy-start = (bf16[1,2,4,2048]{3,2,1,0:T(4,128)(2,1)S(1)}, bf16[1,2,4,2048]{3,2,1,0:T(4,128)(2,1)}, u32[]{:S(2)}) copy-start(bf16[1,2,4,2048]{3,2,1,0:T(4,128)(2,1)} %param.6) | copy-start | bytes 98308
  1.6 12.0 %collective-permute-start.1 = (bf16[2,4,4096]{2,0,1:T(2,128)(2,1)S(1)}, bf16[2,4,4096]{2,0,1:T(2,128)(2,1)S(1)}, u32[]{:S(2)}, u32[]{:S(2)}) collective-permute-start(bf16[2,4,4096]{2,0,1:T(2,128)(2,1)S(1)} %broadcast_select_fusion), channel_id=1, source_target_pairs={{0,1},{1,0},{2,3},{3,2},{4,5},{5,4},{6,7},{7,6},{8,9},{9,8},{10,11... | collective-permute-start | bytes 196616 | tf_op jit(solution)/shard_map/ppermute | solution.py:105
  4.6 9.0 %collective-permute-start.2 = (bf16[2,4,4096]{2,0,1:T(2,128)(2,1)S(1)}, bf16[2,4,4096]{2,0,1:T(2,128)(2,1)S(1)}, u32[]{:S(2)}, u32[]{:S(2)}) collective-permute-start(bf16[2,4,4096]{2,0,1:T(2,128)(2,1)S(1)} %broadcast_select_fusion), channel_id=1, source_target_pairs={{0,2},{1,3},{2,0},{3,1},{4,6},{5,7},{6,4},{7,5},{8,10},{9,11},{10,... | collective-permute-start | bytes 196616 | tf_op jit(solution)/shard_map/ppermute | solution.py:105
  4.6 9.0 %collective-permute-start.3 = (bf16[2,4,4096]{2,0,1:T(2,128)(2,1)S(1)}, bf16[2,4,4096]{2,0,1:T(2,128)(2,1)S(1)}, u32[]{:S(2)}, u32[]{:S(2)}) collective-permute-start(bf16[2,4,4096]{2,0,1:T(2,128)(2,1)S(1)} %broadcast_select_fusion), channel_id=1, source_target_pairs={{0,3},{1,2},{2,1},{3,0},{4,7},{5,6},{6,5},{7,4},{8,11},{9,10},{10,... | collective-permute-start | bytes 196616 | tf_op jit(solution)/shard_map/ppermute | solution.py:105
  4.8 12.6 %collective-permute-start = (bf16[2,4,2048]{2,0,1:T(2,128)(2,1)S(1)}, bf16[2,4,2048]{2,0,1:T(2,128)(2,1)S(1)}, u32[]{:S(2)}, u32[]{:S(2)}) collective-permute-start(bf16[2,4,2048]{2,0,1:T(2,128)(2,1)S(1)} %bitcast.34), channel_id=1, source_target_pairs={{0,1},{1,0},{2,3},{3,2},{4,5},{5,4},{6,7},{7,6},{8,9},{9,8},{10,11... | collective-permute-start | bytes 98312 | tf_op jit(solution)/shard_map/ppermute | solution.py:117
  13.8 5.9 %collective-permute-start.6 = (bf16[2,4,4096]{2,0,1:T(2,128)(2,1)S(1)}, bf16[2,4,4096]{2,0,1:T(2,128)(2,1)S(1)}, u32[]{:S(2)}, u32[]{:S(2)}) collective-permute-start(bf16[2,4,4096]{2,0,1:T(2,128)(2,1)S(1)} %add_add_fusion.1), channel_id=1, source_target_pairs={{0,12},{1,13},{2,14},{3,15},{4,8},{5,9},{6,10},{7,11},{8,4},{9,5},... | collective-permute-start | bytes 196616 | tf_op jit(solution)/shard_map/ppermute | solution.py:105
  16.4 4.3 %collective-permute-start.5 = (bf16[2,4,4096]{2,0,1:T(2,128)(2,1)S(1)}, bf16[2,4,4096]{2,0,1:T(2,128)(2,1)S(1)}, u32[]{:S(2)}, u32[]{:S(2)}) collective-permute-start(bf16[2,4,4096]{2,0,1:T(2,128)(2,1)S(1)} %add_add_fusion.1), channel_id=1, source_target_pairs={{0,8},{1,9},{2,10},{3,11},{4,12},{5,13},{6,14},{7,15},{8,0},{9,1},... | collective-permute-start | bytes 196616 | tf_op jit(solution)/shard_map/ppermute | solution.py:105
  16.9 4.3 %collective-permute-start.4 = (bf16[2,4,4096]{2,0,1:T(2,128)(2,1)S(1)}, bf16[2,4,4096]{2,0,1:T(2,128)(2,1)S(1)}, u32[]{:S(2)}, u32[]{:S(2)}) collective-permute-start(bf16[2,4,4096]{2,0,1:T(2,128)(2,1)S(1)} %add_add_fusion.1), channel_id=1, source_target_pairs={{0,4},{1,5},{2,6},{3,7},{4,0},{5,1},{6,2},{7,3},{8,12},{9,13},{10,... | collective-permute-start | bytes 196616 | tf_op jit(solution)/shard_map/ppermute | solution.py:105
  21.2 5.2 %collective-permute-start.7 = (bf16[2,4,4096]{2,0,1:T(2,128)(2,1)S(1)}, bf16[2,4,4096]{2,0,1:T(2,128)(2,1)S(1)}, u32[]{:S(2)}, u32[]{:S(2)}) collective-permute-start(bf16[2,4,4096]{2,0,1:T(2,128)(2,1)S(1)} %bitcast.30), channel_id=1, source_target_pairs={{0,16},{1,17},{2,18},{3,19},{4,20},{5,21},{6,22},{7,23},{8,24},{9,... | collective-permute-start | bytes 196616 | tf_op jit(solution)/shard_map/ppermute | solution.py:105

commit v6 on v5

--- a/solution.py
+++ b/solution.py
@@ -15,8 +15,8 @@
 PIECE = 1024
 
 
-def phase_table(freqs, times, window_len):
-    turns = jnp.mod(times[:, None] * freqs[None, :], window_len)
+def phase_rows(freqs, times, window_len):
+    turns = jnp.mod(freqs[:, None] * times[None, :], window_len)
     angle = turns.astype(jnp.float32) * (2.0 * math.pi / window_len)
     return jnp.cos(angle), jnp.sin(angle)
 
@@ -62,8 +62,8 @@
             rr = ref_ref[g]
             r_re = rr[0:1, :]
             r_im = rr[1:2, :]
-            a_c = jnp.broadcast_to(ac_ref[g], (LB, CHUNK))
-            a_s = jnp.broadcast_to(as_ref[g], (LB, CHUNK))
+            a_c = jnp.concatenate([ac_ref[g]] * (CHUNK // LB), axis=1)
+            a_s = jnp.concatenate([as_ref[g]] * (CHUNK // LB), axis=1)
             b_c = bc_ref[...]
             b_s = bs_ref[...]
             cos_part = a_c * b_c - a_s * b_s
@@ -149,15 +149,14 @@
     refrows = jnp.transpose(refs.reshape(2, step_count * chunks, CHUNK), (1, 0, 2)).astype(jnp.float32)
 
     freqs = doppler_start[0] + seg_place * bins + jnp.arange(bins, dtype=jnp.int32)
-    fine = 64
-    a_c, a_s = phase_table(freqs, jnp.arange(step_count * chunks, dtype=jnp.int32) * CHUNK, window_len)
-    h_c, h_s = phase_table(freqs, jnp.arange(CHUNK // fine, dtype=jnp.int32) * fine, window_len)
-    l_c, l_s = phase_table(freqs, jnp.arange(fine, dtype=jnp.int32), window_len)
+    a_c, a_s = phase_rows(freqs, jnp.arange(step_count * chunks, dtype=jnp.int32) * CHUNK, window_len)
+    h_c, h_s = phase_rows(freqs, jnp.arange(CHUNK // LB, dtype=jnp.int32) * LB, window_len)
+    l_c, l_s = phase_rows(freqs, jnp.arange(LB, dtype=jnp.int32), window_len)
     a_c, a_s, h_c, h_s, l_c, l_s = lax.optimization_barrier((a_c, a_s, h_c, h_s, l_c, l_s))
-    b_c = (h_c[:, None] * l_c[None] - h_s[:, None] * l_s[None]).reshape(CHUNK, bins).T
-    b_s = (h_s[:, None] * l_c[None] + h_c[:, None] * l_s[None]).reshape(CHUNK, bins).T
-    a_c = a_c[:, :, None]
-    a_s = a_s[:, :, None]
+    b_c = jnp.concatenate([h_c[:, i:i + 1] * l_c - h_s[:, i:i + 1] * l_s for i in range(CHUNK // LB)], axis=1)
+    b_s = jnp.concatenate([h_s[:, i:i + 1] * l_c + h_c[:, i:i + 1] * l_s for i in range(CHUNK // LB)], axis=1)
+    a_c = jnp.broadcast_to(a_c.T[:, :, None], (step_count * chunks, bins, LB))
+    a_s = jnp.broadcast_to(a_s.T[:, :, None], (step_count * chunks, bins, LB))
 
     assert step_count % 2 == 0
     kernel = functools.partial(caf_kernel, chunks=chunks, slots=slot_count, span=span, steps=step_count,

time: 47.5 us -> 46.9 us (0.987)
  local copies, waits for them, and re-layouts: 5.41 us -> 2.72 us
  other arithmetic: 3.47 us -> 4.94 us
  Pallas kernels: 19.8 us -> 20.6 us
    unnamed x0 -> x15, other arithmetic: none -> 1.52 us
    add x1 -> x0, local copies, waits for them, and re-layouts: 1.34 us -> none  [shards(): h_s[:, None] * l_c[None] + h_c[:, None] * l_s[None]]
    sub x1 -> x0, local copies, waits for them, and re-layouts: 1.31 us -> none  [shards(): h_c[:, None] * l_c[None] - h_s[:, None] * l_s[None]]
    pallas_call x1, Pallas kernels: 19.8 us -> 20.6 us  [shards(): pl.pallas_call(kernel, out_shape=jax.ShapeDtypeStruct((slot_count, 2, LB,...]
  transfers between devices with their start and end apart: 8 -> 8, of which waited for: 4 -> 4; matrix products, arithmetic and copies ran while one was open for 14% -> 7% of each run, Pallas kernels for 0% -> 0%
where the time goes in v6:
time: 46.9 us; the launch traced here: 46.7 us
  Pallas kernels  20.6 us (44%)
  starting transfers between devices  11.4 us (24%)
  waiting for transfers between devices  5.49 us (12%)
  other arithmetic  4.94 us (11%)
  local copies, waits for them, and re-layouts  2.72 us (6%)
  between operations  1.57 us (3%)
    pallas_call x1, Pallas kernels, shards(): pl.pallas_call(kernel, out_shape=jax.ShapeDtypeStruct((slot_count, 2, LB,...  20.6 us
    ppermute x7, starting transfers between devices, butterfly_sum(): lax.ppermute(value, axes, [(i, i ^ m * stride) for i in range(count)])  9.42 us
    ppermute x7, waiting for transfers between devices, butterfly_sum(): lax.ppermute(value, axes, [(i, i ^ m * stride) for i in range(count)])  5.49 us
    ppermute x1, starting transfers between devices, seg_join(): other = lax.ppermute(half, axis, [(0, 1), (1, 0)])  2 us
    unnamed x15, other arithmetic  1.52 us
    broadcast_in_dim x1, local copies, waits for them, and re-layouts, shards(): a_c = jnp.broadcast_to(a_c.T[:, :, None], (step_count * chunks, bins, LB))  1.01 us
    broadcast_in_dim x1, local copies, waits for them, and re-layouts, shards(): a_s = jnp.broadcast_to(a_s.T[:, :, None], (step_count * chunks, bins, LB))  0.99 us
  transfers between devices with their start and end apart: 8, of which 4 were waited for; matrix products, arithmetic and copies ran while one was open for 7% of the time, Pallas kernels for 0%

profile of v6, /device:TPU:0, one launch (start us, length us, event | category | flops | bytes accessed | tf_op | source)
XLA Modules:
  0.0 46.7 jit_solution(2176839229060247021)
XLA Ops:
  0.0 0.7 %copy-done.3 = s32[4]{0:T(128)S(1)} copy-done((s32[4]{0:T(128)S(1)}, s32[4]{0:T(128)}, u32[]{:S(2)}) %copy-start.3) | copy-done | bytes 40
  0.7 0.9 %broadcast_select_fusion.2 = bf16[2,4,2048]{2,0,1:T(2,128)(2,1)S(1)} fusion(pred[4]{0:T(512)(128)(4,1)S(1)} %broadcast_compare_fusion, bf16[1,2,4,2048]{3,2,1,0:T(4,128)(2,1)} %param.7), kind=kLoop, calls=%fused_computation.48 | loop fusion | flops 16384 | bytes 65540 | tf_op jit(solution)/shard_map/jit(_where)/select_n | solution.py:137
  1.5 0.0 copy-start.2
  1.5 0.1 broadcast_select_fusion
  1.6 3.0 %collective-permute-start.1 = (bf16[2,4,4096]{2,0,1:T(2,128)(2,1)S(1)}, bf16[2,4,4096]{2,0,1:T(2,128)(2,1)S(1)}, u32[]{:S(2)}, u32[]{:S(2)}) collective-permute-start(bf16[2,4,4096]{2,0,1:T(2,128)(2,1)S(1)} %broadcast_select_fusion), channel_id=1, source_target_pairs={{0,1},{1,0},{2,3},{3,2},{4,5},{5,4},{6,7},{7,6},{8,9},{9,8},{10,11... | collective-permute-start | bytes 196616 | tf_op jit(solution)/shard_map/ppermute | solution.py:105
  4.6 0.0 collective-permute-start.2
  4.6 0.2 collective-permute-start.3
  4.8 0.0 copy-done.2
  4.8 2.0 %collective-permute-start = (bf16[2,4,2048]{2,0,1:T(2,128)(2,1)S(1)}, bf16[2,4,2048]{2,0,1:T(2,128)(2,1)S(1)}, u32[]{:S(2)}, u32[]{:S(2)}) collective-permute-start(bf16[2,4,2048]{2,0,1:T(2,128)(2,1)S(1)} %bitcast.90), channel_id=1, source_target_pairs={{0,1},{1,0},{2,3},{3,2},{4,5},{5,4},{6,7},{7,6},{8,9},{9,8},{10,11... | collective-permute-start | bytes 98312 | tf_op jit(solution)/shard_map/ppermute | solution.py:117
  7.5 0.3 fusion.7
  7.9 0.1 fusion.15
  8.0 0.1 fusion.17
  8.1 0.1 constant_dynamic-update-slice_fusion.31
  8.3 0.1 constant_dynamic-update-slice_fusion.30
  8.4 0.1 constant_dynamic-update-slice_fusion.29
  8.5 0.1 constant_dynamic-update-slice_fusion.28
  8.6 0.1 constant_dynamic-update-slice_fusion.27
  8.7 0.1 constant_dynamic-update-slice_fusion.26
  8.8 0.1 constant_dynamic-update-slice_fusion.25
  8.9 0.1 constant_dynamic-update-slice_fusion.24
  9.0 0.1 constant_dynamic-update-slice_fusion.23
  9.1 0.1 constant_dynamic-update-slice_fusion.22
  9.2 0.1 constant_dynamic-update-slice_fusion.21
  9.3 0.1 constant_dynamic-update-slice_fusion.20
  9.5 0.1 constant_dynamic-update-slice_fusion.19
  9.6 0.1 constant_dynamic-update-slice_fusion.18
  9.7 0.1 constant_dynamic-update-slice_fusion.17
  9.8 0.1 constant_dynamic-update-slice_fusion.16
  10.6 0.0 collective-permute-done.1
  10.6 0.0 collective-permute-done.2
  10.6 0.0 collective-permute-done.3
  10.6 0.2 add_add_fusion.1
  10.8 2.6 %collective-permute-start.6 = (bf16[2,4,4096]{2,0,1:T(2,128)(2,1)S(1)}, bf16[2,4,4096]{2,0,1:T(2,128)(2,1)S(1)}, u32[]{:S(2)}, u32[]{:S(2)}) collective-permute-start(bf16[2,4,4096]{2,0,1:T(2,128)(2,1)S(1)} %add_add_fusion.1), channel_id=1, source_target_pairs={{0,12},{1,13},{2,14},{3,15},{4,8},{5,9},{6,10},{7,11},{8,4},{9,5},... | collective-permute-start | bytes 196616 | tf_op jit(solution)/shard_map/ppermute | solution.py:105
  13.4 0.4 collective-permute-start.5
  13.8 0.5 %collective-permute-start.4 = (bf16[2,4,4096]{2,0,1:T(2,128)(2,1)S(1)}, bf16[2,4,4096]{2,0,1:T(2,128)(2,1)S(1)}, u32[]{:S(2)}, u32[]{:S(2)}) collective-permute-start(bf16[2,4,4096]{2,0,1:T(2,128)(2,1)S(1)} %add_add_fusion.1), channel_id=1, source_target_pairs={{0,4},{1,5},{2,6},{3,7},{4,0},{5,1},{6,2},{7,3},{8,12},{9,13},{10,... | collective-permute-start | bytes 196616 | tf_op jit(solution)/shard_map/ppermute | solution.py:105
  14.4 0.0 collective-permute-done
  14.4 0.1 fusion.3
  14.5 2.2 %collective-permute-done.6 = bf16[2,4,4096]{2,0,1:T(2,128)(2,1)S(1)} collective-permute-done((bf16[2,4,4096]{2,0,1:T(2,128)(2,1)S(1)}, bf16[2,4,4096]{2,0,1:T(2,128)(2,1)S(1)}, u32[]{:S(2)}, u32[]{:S(2)}) %collective-permute-start.6) | collective-permute-done | bytes 65568 | tf_op jit(solution)/shard_map/ppermute | solution.py:105
  16.7 1.0 %collective-permute-done.5 = bf16[2,4,4096]{2,0,1:T(2,128)(2,1)S(1)} collective-permute-done((bf16[2,4,4096]{2,0,1:T(2,128)(2,1)S(1)}, bf16[2,4,4096]{2,0,1:T(2,128)(2,1)S(1)}, u32[]{:S(2)}, u32[]{:S(2)}) %collective-permute-start.5) | collective-permute-done | bytes 65568 | tf_op jit(solution)/shard_map/ppermute | solution.py:105
  17.7 0.4 collective-permute-done.4
  18.1 2.7 %collective-permute-start.7 = (bf16[2,4,4096]{2,0,1:T(2,128)(2,1)S(1)}, bf16[2,4,4096]{2,0,1:T(2,128)(2,1)S(1)}, u32[]{:S(2)}, u32[]{:S(2)}) collective-permute-start(bf16[2,4,4096]{2,0,1:T(2,128)(2,1)S(1)} %bitcast.86), channel_id=1, source_target_pairs={{0,16},{1,17},{2,18},{3,19},{4,20},{5,21},{6,22},{7,23},{8,24},{9,... | collective-permute-start | bytes 196616 | tf_op jit(solution)/shard_map/ppermute | solution.py:105
  20.8 0.7 %pad_convert_fusion.wpad_ref = f32[4,2,5248]{2,1,0:T(2,128)} fusion(bf16[4,2,4096]{2,1,0:T(2,128)(2,1)S(1)} %fusion.3), kind=kLoop, calls=%fused_computation.6 | loop fusion | flops 41984 | bytes 233472 | tf_op jit(solution)/shard_map/jit(_pad)/pad | solution.py:148
  21.5 1.8 %collective-permute-done.7 = bf16[2,4,4096]{2,0,1:T(2,128)(2,1)S(1)} collective-permute-done((bf16[2,4,4096]{2,0,1:T(2,128)(2,1)S(1)}, bf16[2,4,4096]{2,0,1:T(2,128)(2,1)S(1)}, u32[]{:S(2)}, u32[]{:S(2)}) %collective-permute-start.7) | collective-permute-done | bytes 65568 | tf_op jit(solution)/shard_map/ppermute | solution.py:105
  23.4 0.1 add.112
  23.4 0.7 %convert_bitcast_fusion.ref_ref = f32[8,2,2048]{2,1,0:T(2,128)} fusion(bf16[2,8,2048]{2,0,1:T(2,128)(2,1)S(1)} %bitcast.88), kind=kLoop, calls=%fused_computation | loop fusion | flops 32768 | bytes 196608 | tf_op jit(solution)/shard_map/convert_element_type | solution.py:149
  24.1 1.0 %broadcast_in_dim.15.ac_ref = f32[8,128,128]{2,1,0:T(8,128)} broadcast(f32[8,128]{1,0:T(8,128)S(1)} %bitcast.96), dimensions={0,1} | broadcast | bytes 528384 | tf_op jit(solution)/shard_map/broadcast_in_dim | solution.py:158
  25.1 1.0 %broadcast_in_dim.16.as_ref = f32[8,128,128]{2,1,0:T(8,128)} broadcast(f32[8,128]{1,0:T(8,128)S(1)} %bitcast.95), dimensions={0,1} | broadcast | bytes 528384 | tf_op jit(solution)/shard_map/broadcast_in_dim | solution.py:159
  26.1 20.6 %shard_map.64 = f32[6,2,128,128]{3,2,1,0:T(8,128)} custom-call(s32[6]{0:T(128)} %bitcast.97, s32[1]{0:T(128)S(6)} %copy.43.count_ref, f32[4,2,5248]{2,1,0:T(2,128)} %pad_convert_fusion.wpad_ref, f32[8,2,2048]{2,1,0:T(2,128)} %convert_bitcast_fusion.ref_ref, f32[8,128,128]{2,1,0:T(8,128)} %broadcast_in_dim.15.ac_ref, f32[8,128,128]{2,1,0:T(8,128)} %broadcast_in_dim.16.as_ref, ...), custom_call_target="tpu_custom_call" | custom-call | tf_op jit(solution)/shard_map/pallas_call | solution.py:165
  (13 shorter events, 0.1 us)
Async XLA Ops:
  0.0 0.7 %copy-start.3 = (s32[4]{0:T(128)S(1)}, s32[4]{0:T(128)}, u32[]{:S(2)}) copy-start(s32[4]{0:T(128)} %param.8) | copy-start | bytes 52
  1.5 3.3 %copy-start.2 = (bf16[1,2,4,2048]{3,2,1,0:T(4,128)(2,1)S(1)}, bf16[1,2,4,2048]{3,2,1,0:T(4,128)(2,1)}, u32[]{:S(2)}) copy-start(bf16[1,2,4,2048]{3,2,1,0:T(4,128)(2,1)} %param.6) | copy-start | bytes 98308
  1.6 9.0 %collective-permute-start.1 = (bf16[2,4,4096]{2,0,1:T(2,128)(2,1)S(1)}, bf16[2,4,4096]{2,0,1:T(2,128)(2,1)S(1)}, u32[]{:S(2)}, u32[]{:S(2)}) collective-permute-start(bf16[2,4,4096]{2,0,1:T(2,128)(2,1)S(1)} %broadcast_select_fusion), channel_id=1, source_target_pairs={{0,1},{1,0},{2,3},{3,2},{4,5},{5,4},{6,7},{7,6},{8,9},{9,8},{10,11... | collective-permute-start | bytes 196616 | tf_op jit(solution)/shard_map/ppermute | solution.py:105
  4.6 6.0 %collective-permute-start.2 = (bf16[2,4,4096]{2,0,1:T(2,128)(2,1)S(1)}, bf16[2,4,4096]{2,0,1:T(2,128)(2,1)S(1)}, u32[]{:S(2)}, u32[]{:S(2)}) collective-permute-start(bf16[2,4,4096]{2,0,1:T(2,128)(2,1)S(1)} %broadcast_select_fusion), channel_id=1, source_target_pairs={{0,2},{1,3},{2,0},{3,1},{4,6},{5,7},{6,4},{7,5},{8,10},{9,11},{10,... | collective-permute-start | bytes 196616 | tf_op jit(solution)/shard_map/ppermute | solution.py:105
  4.6 6.0 %collective-permute-start.3 = (bf16[2,4,4096]{2,0,1:T(2,128)(2,1)S(1)}, bf16[2,4,4096]{2,0,1:T(2,128)(2,1)S(1)}, u32[]{:S(2)}, u32[]{:S(2)}) collective-permute-start(bf16[2,4,4096]{2,0,1:T(2,128)(2,1)S(1)} %broadcast_select_fusion), channel_id=1, source_target_pairs={{0,3},{1,2},{2,1},{3,0},{4,7},{5,6},{6,5},{7,4},{8,11},{9,10},{10,... | collective-permute-start | bytes 196616 | tf_op jit(solution)/shard_map/ppermute | solution.py:105
  4.8 9.5 %collective-permute-start = (bf16[2,4,2048]{2,0,1:T(2,128)(2,1)S(1)}, bf16[2,4,2048]{2,0,1:T(2,128)(2,1)S(1)}, u32[]{:S(2)}, u32[]{:S(2)}) collective-permute-start(bf16[2,4,2048]{2,0,1:T(2,128)(2,1)S(1)} %bitcast.90), channel_id=1, source_target_pairs={{0,1},{1,0},{2,3},{3,2},{4,5},{5,4},{6,7},{7,6},{8,9},{9,8},{10,11... | collective-permute-start | bytes 98312 | tf_op jit(solution)/shard_map/ppermute | solution.py:117
  9.9 16.2 %copy-start = (f32[128,2048]{1,0:T(8,128)}, f32[128,2048]{1,0:T(8,128)S(1)}, u32[]{:S(2)}) copy-start(f32[128,2048]{1,0:T(8,128)S(1)} %get-tuple-element.17.bs_ref) | copy-start | bytes 3145732
  9.9 16.2 %copy-start.1 = (f32[128,2048]{1,0:T(8,128)}, f32[128,2048]{1,0:T(8,128)S(1)}, u32[]{:S(2)}) copy-start(f32[128,2048]{1,0:T(8,128)S(1)} %get-tuple-element.18.bc_ref) | copy-start | bytes 3145732
  10.8 5.9 %collective-permute-start.6 = (bf16[2,4,4096]{2,0,1:T(2,128)(2,1)S(1)}, bf16[2,4,4096]{2,0,1:T(2,128)(2,1)S(1)}, u32[]{:S(2)}, u32[]{:S(2)}) collective-permute-start(bf16[2,4,4096]{2,0,1:T(2,128)(2,1)S(1)} %add_add_fusion.1), channel_id=1, source_target_pairs={{0,12},{1,13},{2,14},{3,15},{4,8},{5,9},{6,10},{7,11},{8,4},{9,5},... | collective-permute-start | bytes 196616 | tf_op jit(solution)/shard_map/ppermute | solution.py:105
  13.4 4.3 %collective-permute-start.5 = (bf16[2,4,4096]{2,0,1:T(2,128)(2,1)S(1)}, bf16[2,4,4096]{2,0,1:T(2,128)(2,1)S(1)}, u32[]{:S(2)}, u32[]{:S(2)}) collective-permute-start(bf16[2,4,4096]{2,0,1:T(2,128)(2,1)S(1)} %add_add_fusion.1), channel_id=1, source_target_pairs={{0,8},{1,9},{2,10},{3,11},{4,12},{5,13},{6,14},{7,15},{8,0},{9,1},... | collective-permute-start | bytes 196616 | tf_op jit(solution)/shard_map/ppermute | solution.py:105
  13.8 4.3 %collective-permute-start.4 = (bf16[2,4,4096]{2,0,1:T(2,128)(2,1)S(1)}, bf16[2,4,4096]{2,0,1:T(2,128)(2,1)S(1)}, u32[]{:S(2)}, u32[]{:S(2)}) collective-permute-start(bf16[2,4,4096]{2,0,1:T(2,128)(2,1)S(1)} %add_add_fusion.1), channel_id=1, source_target_pairs={{0,4},{1,5},{2,6},{3,7},{4,0},{5,1},{6,2},{7,3},{8,12},{9,13},{10,... | collective-permute-start | bytes 196616 | tf_op jit(solution)/shard_map/ppermute | solution.py:105
  18.1 5.2 %collective-permute-start.7 = (bf16[2,4,4096]{2,0,1:T(2,128)(2,1)S(1)}, bf16[2,4,4096]{2,0,1:T(2,128)(2,1)S(1)}, u32[]{:S(2)}, u32[]{:S(2)}) collective-permute-start(bf16[2,4,4096]{2,0,1:T(2,128)(2,1)S(1)} %bitcast.86), channel_id=1, source_target_pairs={{0,16},{1,17},{2,18},{3,19},{4,20},{5,21},{6,22},{7,23},{8,24},{9,... | collective-permute-start | bytes 196616 | tf_op jit(solution)/shard_map/ppermute | solution.py:105

commit v7 on v6

--- a/solution.py
+++ b/solution.py
@@ -34,8 +34,8 @@
     return (turn(high) + turn(mid)) + turn(low)
 
 
-def caf_kernel(blocks_ref, count_ref, wpad_ref, ref_ref, ac_ref, as_ref, bc_ref, bs_ref,
-               out_ref, first_buf, second_buf, acc, *, chunks, slots, span, steps, norm):
+def caf_kernel(blocks_ref, count_ref, wpad_ref, ref_ref, ac_ref, as_ref, hc_ref, hs_ref, lc_ref, ls_ref,
+               out_ref, first_buf, second_buf, acc, bc_ref, bs_ref, *, chunks, slots, span, steps, norm):
     pair = pl.program_id(0)
     lanes = PIECE + LB
     pieces = [(comp, i) for comp in range(2) for i in range(span // PIECE)]
@@ -51,6 +51,13 @@
     @pl.when(pair == 0)
     def _():
         acc[...] = jnp.zeros_like(acc)
+        l_c = lc_ref[...]
+        l_s = ls_ref[...]
+        for i in range(CHUNK // LB):
+            h_c = jnp.broadcast_to(hc_ref[:, i:i + 1], (LB, LB))
+            h_s = jnp.broadcast_to(hs_ref[:, i:i + 1], (LB, LB))
+            bc_ref[:, i * LB:(i + 1) * LB] = h_c * l_c - h_s * l_s
+            bs_ref[:, i * LB:(i + 1) * LB] = h_s * l_c + h_c * l_s
         for comp, i in pieces:
             build_piece(0, comp, i, first_buf)
 
@@ -62,8 +69,9 @@
             rr = ref_ref[g]
             r_re = rr[0:1, :]
             r_im = rr[1:2, :]
-            a_c = jnp.concatenate([ac_ref[g]] * (CHUNK // LB), axis=1)
-            a_s = jnp.concatenate([as_ref[g]] * (CHUNK // LB), axis=1)
+            pick = lax.broadcasted_iota(jnp.int32, ac_ref.shape, 1) == g
+            a_c = jnp.broadcast_to(jnp.sum(jnp.where(pick, ac_ref[...], 0.0), axis=1, keepdims=True), (LB, CHUNK))
+            a_s = jnp.broadcast_to(jnp.sum(jnp.where(pick, as_ref[...], 0.0), axis=1, keepdims=True), (LB, CHUNK))
             b_c = bc_ref[...]
             b_s = bs_ref[...]
             cos_part = a_c * b_c - a_s * b_s
@@ -152,12 +160,8 @@
     a_c, a_s = phase_rows(freqs, jnp.arange(step_count * chunks, dtype=jnp.int32) * CHUNK, window_len)
     h_c, h_s = phase_rows(freqs, jnp.arange(CHUNK // LB, dtype=jnp.int32) * LB, window_len)
     l_c, l_s = phase_rows(freqs, jnp.arange(LB, dtype=jnp.int32), window_len)
-    a_c, a_s, h_c, h_s, l_c, l_s = lax.optimization_barrier((a_c, a_s, h_c, h_s, l_c, l_s))
-    b_c = jnp.concatenate([h_c[:, i:i + 1] * l_c - h_s[:, i:i + 1] * l_s for i in range(CHUNK // LB)], axis=1)
-    b_s = jnp.concatenate([h_s[:, i:i + 1] * l_c + h_c[:, i:i + 1] * l_s for i in range(CHUNK // LB)], axis=1)
-    a_c = jnp.broadcast_to(a_c.T[:, :, None], (step_count * chunks, bins, LB))
-    a_s = jnp.broadcast_to(a_s.T[:, :, None], (step_count * chunks, bins, LB))
-
+
+    tables = (a_c, a_s, h_c, h_s, l_c, l_s)
     assert step_count % 2 == 0
     kernel = functools.partial(caf_kernel, chunks=chunks, slots=slot_count, span=span, steps=step_count,
                                norm=1.0 / math.sqrt(window_len))
@@ -168,14 +172,14 @@
         grid_spec=pltpu.PrefetchScalarGridSpec(
             num_scalar_prefetch=2,
             grid=(step_count // 2,),
-            in_specs=[full(wpad.shape), full(refrows.shape), full(a_c.shape), full(a_s.shape),
-                      full(b_c.shape), full(b_s.shape)],
+            in_specs=[full(wpad.shape), full(refrows.shape)] + [full(t.shape) for t in tables],
             out_specs=full((slot_count, 2, LB, bins)),
             scratch_shapes=[pltpu.VMEM((2 * LB, span), jnp.bfloat16), pltpu.VMEM((2 * LB, span), jnp.bfloat16),
-                            pltpu.VMEM((slot_count, 2 * LB, 2 * bins), jnp.float32)],
+                            pltpu.VMEM((slot_count, 2 * LB, 2 * bins), jnp.float32),
+                            pltpu.VMEM((bins, CHUNK), jnp.float32), pltpu.VMEM((bins, CHUNK), jnp.float32)],
         ),
         compiler_params=pltpu.CompilerParams(dimension_semantics=("arbitrary",)),
-    )(lag_blocks[0], block_count, wpad, refrows, a_c, a_s, b_c, b_s)
+    )(lag_blocks[0], block_count, wpad, refrows, *tables)
     return out[None]
 
 

time: 46.9 us -> 45 us (0.959)
  local copies, waits for them, and re-layouts: 2.72 us -> 0.9 us
  Pallas kernels: 20.6 us -> 19.8 us
  other arithmetic: 4.94 us -> 5.67 us
    sin x3, other arithmetic: 0.58 us -> 2.77 us  [phase_rows(): return (jnp.cos(angle), jnp.sin(angle))]
    broadcast_in_dim x2 -> x0, local copies, waits for them, and re-layouts: 2 us -> none  [the longest x1 1.01 us: shards(): a_c = jnp.broadcast_to(a_c.T[:, :, None], (step_count * chunks, bins, LB))]
    unnamed x15 -> x0, other arithmetic: 1.52 us -> none
    pallas_call x1, Pallas kernels: 20.6 us -> 19.8 us  [shards(): pl.pallas_call(kernel, out_shape=jax.ShapeDtypeStruct((slot_count, 2, LB,...]
  transfers between devices with their start and end apart: 8 -> 8, of which waited for: 4 -> 4; matrix products, arithmetic and copies ran while one was open for 7% -> 9% of each run, Pallas kernels for 0% -> 0%
where the time goes in v7:
time: 45 us; the launch traced here: 44.6 us
  Pallas kernels  19.8 us (44%)
  starting transfers between devices  11.4 us (25%)
  other arithmetic  5.67 us (13%)
  waiting for transfers between devices  5.49 us (12%)
  between operations  1.39 us (3%)
  local copies, waits for them, and re-layouts  0.9 us (2%)
    pallas_call x1, Pallas kernels, shards(): pl.pallas_call(kernel, out_shape=jax.ShapeDtypeStruct((slot_count, 2, LB,...  19.8 us
    ppermute x7, starting transfers between devices, butterfly_sum(): lax.ppermute(value, axes, [(i, i ^ m * stride) for i in range(count)])  9.38 us
    ppermute x7, waiting for transfers between devices, butterfly_sum(): lax.ppermute(value, axes, [(i, i ^ m * stride) for i in range(count)])  5.48 us
    sin x3, other arithmetic, phase_rows(): return (jnp.cos(angle), jnp.sin(angle))  2.77 us
    ppermute x1, starting transfers between devices, seg_join(): other = lax.ppermute(half, axis, [(0, 1), (1, 0)])  2.05 us
  transfers between devices with their start and end apart: 8, of which 4 were waited for; matrix products, arithmetic and copies ran while one was open for 9% of the time, Pallas kernels for 0%

profile of v7, /device:TPU:0, one launch (start us, length us, event | category | flops | bytes accessed | tf_op | source)
XLA Modules:
  0.0 44.6 jit_solution(4824794115473221337)
XLA Ops:
  0.0 0.0 copy-start.1
  0.0 0.7 %copy-done.1 = s32[4]{0:T(128)S(1)} copy-done((s32[4]{0:T(128)S(1)}, s32[4]{0:T(128)}, u32[]{:S(2)}) %copy-start.1) | copy-done | bytes 40
  0.7 0.9 %broadcast_select_fusion.2 = bf16[2,4,2048]{2,0,1:T(2,128)(2,1)S(1)} fusion(pred[4]{0:T(512)(128)(4,1)S(1)} %broadcast_compare_fusion, bf16[1,2,4,2048]{3,2,1,0:T(4,128)(2,1)} %param.7), kind=kLoop, calls=%fused_computation.16 | loop fusion | flops 16384 | bytes 65540 | tf_op jit(solution)/shard_map/jit(_where)/select_n | solution.py:145
  1.5 0.0 copy-start
  1.5 0.1 broadcast_select_fusion
  1.6 0.5 %collective-permute-start.2 = (bf16[2,4,4096]{2,0,1:T(2,128)(2,1)S(1)}, bf16[2,4,4096]{2,0,1:T(2,128)(2,1)S(1)}, u32[]{:S(2)}, u32[]{:S(2)}) collective-permute-start(bf16[2,4,4096]{2,0,1:T(2,128)(2,1)S(1)} %broadcast_select_fusion), channel_id=1, source_target_pairs={{0,2},{1,3},{2,0},{3,1},{4,6},{5,7},{6,4},{7,5},{8,10},{9,11},{10,... | collective-permute-start | bytes 196616 | tf_op jit(solution)/shard_map/ppermute | solution.py:113
  2.1 2.6 %collective-permute-start.3 = (bf16[2,4,4096]{2,0,1:T(2,128)(2,1)S(1)}, bf16[2,4,4096]{2,0,1:T(2,128)(2,1)S(1)}, u32[]{:S(2)}, u32[]{:S(2)}) collective-permute-start(bf16[2,4,4096]{2,0,1:T(2,128)(2,1)S(1)} %broadcast_select_fusion), channel_id=1, source_target_pairs={{0,3},{1,2},{2,1},{3,0},{4,7},{5,6},{6,5},{7,4},{8,11},{9,10},{10,... | collective-permute-start | bytes 196616 | tf_op jit(solution)/shard_map/ppermute | solution.py:113
  4.7 0.0 collective-permute-start.1
  4.8 0.0 copy-done
  4.8 2.0 %collective-permute-start = (bf16[2,4,2048]{2,0,1:T(2,128)(2,1)S(1)}, bf16[2,4,2048]{2,0,1:T(2,128)(2,1)S(1)}, u32[]{:S(2)}, u32[]{:S(2)}) collective-permute-start(bf16[2,4,2048]{2,0,1:T(2,128)(2,1)S(1)} %bitcast.24), channel_id=1, source_target_pairs={{0,1},{1,0},{2,3},{3,2},{4,5},{5,4},{6,7},{7,6},{8,9},{9,8},{10,11... | collective-permute-start | bytes 98312 | tf_op jit(solution)/shard_map/ppermute | solution.py:125
  7.5 0.1 fusion.11
  7.6 0.1 fusion.9
  7.7 0.1 copy.12
  7.8 0.1 copy.11
  7.9 0.9 %multiply_sine_fusion.1 = (f32[128,8]{1,0:T(8,128)}, f32[128,8]{1,0:T(8,128)}) fusion(f32[128,8]{1,0:T(8,128)S(1)} %copy.11), kind=kLoop, calls=%fused_computation.19 | loop fusion | flops 1024 | bytes 12288 | tf_op jit(solution)/shard_map/sin | solution.py:21
  8.8 0.9 %multiply_sine_fusion = (f32[128,16]{1,0:T(8,128)}, f32[128,16]{1,0:T(8,128)}) fusion(f32[128,16]{1,0:T(8,128)S(1)} %copy.12), kind=kLoop, calls=%fused_computation.17 | loop fusion | flops 2048 | bytes 24576 | tf_op jit(solution)/shard_map/sin | solution.py:21
  9.7 1.0 %fusion.7 = (f32[128,128]{1,0:T(8,128)}, f32[128,128]{1,0:T(8,128)}) fusion(s32[128]{0:T(128)S(1)} %iota_add_fusion), kind=kLoop, calls=%fused_computation.22 | loop fusion | flops 229376 | bytes 131584 | tf_op jit(solution)/shard_map/sin | solution.py:21
  11.3 0.0 collective-permute-done.2
  11.3 0.0 collective-permute-done.3
  11.3 0.0 collective-permute-done.1
  11.4 0.2 add_add_fusion.1
  11.5 2.6 %collective-permute-start.6 = (bf16[2,4,4096]{2,0,1:T(2,128)(2,1)S(1)}, bf16[2,4,4096]{2,0,1:T(2,128)(2,1)S(1)}, u32[]{:S(2)}, u32[]{:S(2)}) collective-permute-start(bf16[2,4,4096]{2,0,1:T(2,128)(2,1)S(1)} %add_add_fusion.1), channel_id=1, source_target_pairs={{0,12},{1,13},{2,14},{3,15},{4,8},{5,9},{6,10},{7,11},{8,4},{9,5},... | collective-permute-start | bytes 196616 | tf_op jit(solution)/shard_map/ppermute | solution.py:113
  14.1 0.4 %collective-permute-start.5 = (bf16[2,4,4096]{2,0,1:T(2,128)(2,1)S(1)}, bf16[2,4,4096]{2,0,1:T(2,128)(2,1)S(1)}, u32[]{:S(2)}, u32[]{:S(2)}) collective-permute-start(bf16[2,4,4096]{2,0,1:T(2,128)(2,1)S(1)} %add_add_fusion.1), channel_id=1, source_target_pairs={{0,8},{1,9},{2,10},{3,11},{4,12},{5,13},{6,14},{7,15},{8,0},{9,1},... | collective-permute-start | bytes 196616 | tf_op jit(solution)/shard_map/ppermute | solution.py:113
  14.6 0.5 %collective-permute-start.4 = (bf16[2,4,4096]{2,0,1:T(2,128)(2,1)S(1)}, bf16[2,4,4096]{2,0,1:T(2,128)(2,1)S(1)}, u32[]{:S(2)}, u32[]{:S(2)}) collective-permute-start(bf16[2,4,4096]{2,0,1:T(2,128)(2,1)S(1)} %add_add_fusion.1), channel_id=1, source_target_pairs={{0,4},{1,5},{2,6},{3,7},{4,0},{5,1},{6,2},{7,3},{8,12},{9,13},{10,... | collective-permute-start | bytes 196616 | tf_op jit(solution)/shard_map/ppermute | solution.py:113
  15.1 0.0 collective-permute-done
  15.1 0.1 fusion.3
  15.2 2.2 %collective-permute-done.6 = bf16[2,4,4096]{2,0,1:T(2,128)(2,1)S(1)} collective-permute-done((bf16[2,4,4096]{2,0,1:T(2,128)(2,1)S(1)}, bf16[2,4,4096]{2,0,1:T(2,128)(2,1)S(1)}, u32[]{:S(2)}, u32[]{:S(2)}) %collective-permute-start.6) | collective-permute-done | bytes 65568 | tf_op jit(solution)/shard_map/ppermute | solution.py:113
  17.4 1.0 %collective-permute-done.5 = bf16[2,4,4096]{2,0,1:T(2,128)(2,1)S(1)} collective-permute-done((bf16[2,4,4096]{2,0,1:T(2,128)(2,1)S(1)}, bf16[2,4,4096]{2,0,1:T(2,128)(2,1)S(1)}, u32[]{:S(2)}, u32[]{:S(2)}) %collective-permute-start.5) | collective-permute-done | bytes 65568 | tf_op jit(solution)/shard_map/ppermute | solution.py:113
  18.4 0.4 %collective-permute-done.4 = bf16[2,4,4096]{2,0,1:T(2,128)(2,1)S(1)} collective-permute-done((bf16[2,4,4096]{2,0,1:T(2,128)(2,1)S(1)}, bf16[2,4,4096]{2,0,1:T(2,128)(2,1)S(1)}, u32[]{:S(2)}, u32[]{:S(2)}) %collective-permute-start.4) | collective-permute-done | bytes 65568 | tf_op jit(solution)/shard_map/ppermute | solution.py:113
  18.9 2.7 %collective-permute-start.7 = (bf16[2,4,4096]{2,0,1:T(2,128)(2,1)S(1)}, bf16[2,4,4096]{2,0,1:T(2,128)(2,1)S(1)}, u32[]{:S(2)}, u32[]{:S(2)}) collective-permute-start(bf16[2,4,4096]{2,0,1:T(2,128)(2,1)S(1)} %bitcast.20), channel_id=1, source_target_pairs={{0,16},{1,17},{2,18},{3,19},{4,20},{5,21},{6,22},{7,23},{8,24},{9,... | collective-permute-start | bytes 196616 | tf_op jit(solution)/shard_map/ppermute | solution.py:113
  21.5 0.7 %pad_convert_fusion.wpad_ref = f32[4,2,5248]{2,1,0:T(2,128)} fusion(bf16[4,2,4096]{2,1,0:T(2,128)(2,1)S(1)} %fusion.3), kind=kLoop, calls=%fused_computation.6 | loop fusion | flops 41984 | bytes 233472 | tf_op jit(solution)/shard_map/jit(_pad)/pad | solution.py:156
  22.3 1.8 %collective-permute-done.7 = bf16[2,4,4096]{2,0,1:T(2,128)(2,1)S(1)} collective-permute-done((bf16[2,4,4096]{2,0,1:T(2,128)(2,1)S(1)}, bf16[2,4,4096]{2,0,1:T(2,128)(2,1)S(1)}, u32[]{:S(2)}, u32[]{:S(2)}) %collective-permute-start.7) | collective-permute-done | bytes 65568 | tf_op jit(solution)/shard_map/ppermute | solution.py:113
  24.1 0.1 add.64
  24.2 0.7 %convert_bitcast_fusion.ref_ref = f32[8,2,2048]{2,1,0:T(2,128)} fusion(bf16[2,8,2048]{2,0,1:T(2,128)(2,1)S(1)} %bitcast.22), kind=kLoop, calls=%fused_computation | loop fusion | flops 32768 | bytes 196608 | tf_op jit(solution)/shard_map/convert_element_type | solution.py:157
  24.9 19.8 %shard_map.64 = f32[6,2,128,128]{3,2,1,0:T(8,128)} custom-call(s32[6]{0:T(128)} %bitcast.29, s32[1]{0:T(128)S(6)} %copy.17.count_ref, f32[4,2,5248]{2,1,0:T(2,128)} %pad_convert_fusion.wpad_ref, f32[8,2,2048]{2,1,0:T(2,128)} %convert_bitcast_fusion.ref_ref, f32[128,8]{1,0:T(8,128)} %get-tuple-element.8.ac_ref, f32[128,8]{1,0:T(8,128)} %get-tuple-element.7.as_ref, ...), custom_call_target="tpu_custom_call" | custom-call | tf_op jit(solution)/shard_map/pallas_call | solution.py:169
  (6 shorter events, 0.1 us)
Async XLA Ops:
  0.0 0.7 %copy-start.1 = (s32[4]{0:T(128)S(1)}, s32[4]{0:T(128)}, u32[]{:S(2)}) copy-start(s32[4]{0:T(128)} %param.8) | copy-start | bytes 52
  1.5 3.3 %copy-start = (bf16[1,2,4,2048]{3,2,1,0:T(4,128)(2,1)S(1)}, bf16[1,2,4,2048]{3,2,1,0:T(4,128)(2,1)}, u32[]{:S(2)}) copy-start(bf16[1,2,4,2048]{3,2,1,0:T(4,128)(2,1)} %param.6) | copy-start | bytes 98308
  1.6 9.7 %collective-permute-start.2 = (bf16[2,4,4096]{2,0,1:T(2,128)(2,1)S(1)}, bf16[2,4,4096]{2,0,1:T(2,128)(2,1)S(1)}, u32[]{:S(2)}, u32[]{:S(2)}) collective-permute-start(bf16[2,4,4096]{2,0,1:T(2,128)(2,1)S(1)} %broadcast_select_fusion), channel_id=1, source_target_pairs={{0,2},{1,3},{2,0},{3,1},{4,6},{5,7},{6,4},{7,5},{8,10},{9,11},{10,... | collective-permute-start | bytes 196616 | tf_op jit(solution)/shard_map/ppermute | solution.py:113
  2.1 9.2 %collective-permute-start.3 = (bf16[2,4,4096]{2,0,1:T(2,128)(2,1)S(1)}, bf16[2,4,4096]{2,0,1:T(2,128)(2,1)S(1)}, u32[]{:S(2)}, u32[]{:S(2)}) collective-permute-start(bf16[2,4,4096]{2,0,1:T(2,128)(2,1)S(1)} %broadcast_select_fusion), channel_id=1, source_target_pairs={{0,3},{1,2},{2,1},{3,0},{4,7},{5,6},{6,5},{7,4},{8,11},{9,10},{10,... | collective-permute-start | bytes 196616 | tf_op jit(solution)/shard_map/ppermute | solution.py:113
  4.7 6.6 %collective-permute-start.1 = (bf16[2,4,4096]{2,0,1:T(2,128)(2,1)S(1)}, bf16[2,4,4096]{2,0,1:T(2,128)(2,1)S(1)}, u32[]{:S(2)}, u32[]{:S(2)}) collective-permute-start(bf16[2,4,4096]{2,0,1:T(2,128)(2,1)S(1)} %broadcast_select_fusion), channel_id=1, source_target_pairs={{0,1},{1,0},{2,3},{3,2},{4,5},{5,4},{6,7},{7,6},{8,9},{9,8},{10,11... | collective-permute-start | bytes 196616 | tf_op jit(solution)/shard_map/ppermute | solution.py:113
  4.8 10.3 %collective-permute-start = (bf16[2,4,2048]{2,0,1:T(2,128)(2,1)S(1)}, bf16[2,4,2048]{2,0,1:T(2,128)(2,1)S(1)}, u32[]{:S(2)}, u32[]{:S(2)}) collective-permute-start(bf16[2,4,2048]{2,0,1:T(2,128)(2,1)S(1)} %bitcast.24), channel_id=1, source_target_pairs={{0,1},{1,0},{2,3},{3,2},{4,5},{5,4},{6,7},{7,6},{8,9},{9,8},{10,11... | collective-permute-start | bytes 98312 | tf_op jit(solution)/shard_map/ppermute | solution.py:125
  11.5 5.9 %collective-permute-start.6 = (bf16[2,4,4096]{2,0,1:T(2,128)(2,1)S(1)}, bf16[2,4,4096]{2,0,1:T(2,128)(2,1)S(1)}, u32[]{:S(2)}, u32[]{:S(2)}) collective-permute-start(bf16[2,4,4096]{2,0,1:T(2,128)(2,1)S(1)} %add_add_fusion.1), channel_id=1, source_target_pairs={{0,12},{1,13},{2,14},{3,15},{4,8},{5,9},{6,10},{7,11},{8,4},{9,5},... | collective-permute-start | bytes 196616 | tf_op jit(solution)/shard_map/ppermute | solution.py:113
  14.1 4.3 %collective-permute-start.5 = (bf16[2,4,4096]{2,0,1:T(2,128)(2,1)S(1)}, bf16[2,4,4096]{2,0,1:T(2,128)(2,1)S(1)}, u32[]{:S(2)}, u32[]{:S(2)}) collective-permute-start(bf16[2,4,4096]{2,0,1:T(2,128)(2,1)S(1)} %add_add_fusion.1), channel_id=1, source_target_pairs={{0,8},{1,9},{2,10},{3,11},{4,12},{5,13},{6,14},{7,15},{8,0},{9,1},... | collective-permute-start | bytes 196616 | tf_op jit(solution)/shard_map/ppermute | solution.py:113
  14.6 4.3 %collective-permute-start.4 = (bf16[2,4,4096]{2,0,1:T(2,128)(2,1)S(1)}, bf16[2,4,4096]{2,0,1:T(2,128)(2,1)S(1)}, u32[]{:S(2)}, u32[]{:S(2)}) collective-permute-start(bf16[2,4,4096]{2,0,1:T(2,128)(2,1)S(1)} %add_add_fusion.1), channel_id=1, source_target_pairs={{0,4},{1,5},{2,6},{3,7},{4,0},{5,1},{6,2},{7,3},{8,12},{9,13},{10,... | collective-permute-start | bytes 196616 | tf_op jit(solution)/shard_map/ppermute | solution.py:113
  18.9 5.2 %collective-permute-start.7 = (bf16[2,4,4096]{2,0,1:T(2,128)(2,1)S(1)}, bf16[2,4,4096]{2,0,1:T(2,128)(2,1)S(1)}, u32[]{:S(2)}, u32[]{:S(2)}) collective-permute-start(bf16[2,4,4096]{2,0,1:T(2,128)(2,1)S(1)} %bitcast.20), channel_id=1, source_target_pairs={{0,16},{1,17},{2,18},{3,19},{4,20},{5,21},{6,22},{7,23},{8,24},{9,... | collective-permute-start | bytes 196616 | tf_op jit(solution)/shard_map/ppermute | solution.py:113

commit v8 on v7

--- a/solution.py
+++ b/solution.py
@@ -103,18 +103,21 @@
             out_ref[q, 1] = jnp.where(keep, reverse_rows(im) * norm, 0.0)
 
 
-def butterfly_sum(value, axes):
+def butterfly_sum(value, axes, later=()):
     count = lax.axis_size(axes)
     if count & (count - 1):
-        return lax.psum(value, axes)
+        return lax.psum(value, axes), later
     stride = 1
     while stride < count:
         radix = 4 if stride * 4 <= count else 2
         parts = [lax.ppermute(value, axes, [(i, i ^ (m * stride)) for i in range(count)]) for m in range(1, radix)]
         for part in parts:
             value = value + part
+        if stride == 1:
+            late = (value.reshape(-1)[0] != value.reshape(-1)[0]).astype(jnp.int32)
+            later = jax.tree.map(lambda x: x + late.astype(x.dtype), later)
         stride *= radix
-    return value
+    return value, later
 
 
 def seg_join(half, axis):
@@ -140,23 +143,24 @@
     bins = DOP // segments
     chunks = step_len // CHUNK
 
-    samples = seg_join(surveillance[0], "seg")
     mine = (owner_index == beam_place)[None, :, None]
     local = jnp.where(mine, reference_blocks[0], jnp.zeros_like(reference_blocks[0]))
     if segments == 2:
         first = seg_place == 0
         zero = jnp.zeros_like(local)
         placed = jnp.where(first, jnp.concatenate([local, zero], -1), jnp.concatenate([zero, local], -1))
-        refs = butterfly_sum(placed, ("beam", "seg"))
+        refs, (own_samples, first_bin) = butterfly_sum(placed, ("beam", "seg"), (surveillance[0], doppler_start[0]))
     else:
-        refs = seg_join(butterfly_sum(local, "beam"), "seg")
+        refs, (own_samples, first_bin) = butterfly_sum(local, "beam", (surveillance[0], doppler_start[0]))
+        refs = seg_join(refs, "seg")
+    samples = seg_join(own_samples, "seg")
 
     span = step_len + rim_len
     wpad = jnp.transpose(samples, (1, 0, 2)).astype(jnp.float32)
     wpad = jnp.pad(wpad, ((0, 0), (0, 0), (0, span + LB - step_len)))
     refrows = jnp.transpose(refs.reshape(2, step_count * chunks, CHUNK), (1, 0, 2)).astype(jnp.float32)
 
-    freqs = doppler_start[0] + seg_place * bins + jnp.arange(bins, dtype=jnp.int32)
+    freqs = first_bin + seg_place * bins + jnp.arange(bins, dtype=jnp.int32)
     a_c, a_s = phase_rows(freqs, jnp.arange(step_count * chunks, dtype=jnp.int32) * CHUNK, window_len)
     h_c, h_s = phase_rows(freqs, jnp.arange(CHUNK // LB, dtype=jnp.int32) * LB, window_len)
     l_c, l_s = phase_rows(freqs, jnp.arange(LB, dtype=jnp.int32), window_len)

time: 45 us -> 45.9 us (1.020)
  between operations: 1.39 us -> 2.74 us
  waiting for transfers between devices: 5.49 us -> 4.74 us
  local copies, waits for them, and re-layouts: 0.9 us -> 1.47 us
  starting transfers between devices: 11.4 us -> 10.9 us
    ppermute x7, waiting for transfers between devices: 5.48 us -> 4.74 us  [butterfly_sum(): lax.ppermute(value, axes, [(i, i ^ m * stride) for i in range(count)])]
    slice x0 -> x1, local copies, waits for them, and re-layouts: none -> 0.51 us  [butterfly_sum(): late = (value.reshape(-1)[0] != value.reshape(-1)[0]).astype(jnp.int32)]
    ppermute x1, starting transfers between devices: 2.05 us -> 1.55 us  [seg_join(): other = lax.ppermute(half, axis, [(0, 1), (1, 0)])]
  transfers between devices with their start and end apart: 8 -> 8, of which waited for: 4 -> 3; matrix products, arithmetic and copies ran while one was open for 9% -> 10% of each run, Pallas kernels for 0% -> 0%
where the time goes in v8:
time: 45.9 us; the launch traced here: 45.5 us
  Pallas kernels  20 us (44%)
  starting transfers between devices  10.9 us (24%)
  other arithmetic  5.68 us (12%)
  waiting for transfers between devices  4.74 us (10%)
  between operations  2.74 us (6%)
  local copies, waits for them, and re-layouts  1.47 us (3%)
    pallas_call x1, Pallas kernels, shards(): pl.pallas_call(kernel, out_shape=jax.ShapeDtypeStruct((slot_count, 2, LB,...  20 us
    ppermute x7, starting transfers between devices, butterfly_sum(): lax.ppermute(value, axes, [(i, i ^ m * stride) for i in range(count)])  9.38 us
    ppermute x7, waiting for transfers between devices, butterfly_sum(): lax.ppermute(value, axes, [(i, i ^ m * stride) for i in range(count)])  4.74 us
    sin x3, other arithmetic, phase_rows(): return (jnp.cos(angle), jnp.sin(angle))  2.77 us
    ppermute x1, starting transfers between devices, seg_join(): other = lax.ppermute(half, axis, [(0, 1), (1, 0)])  1.55 us
  transfers between devices with their start and end apart: 8, of which 3 were waited for; matrix products, arithmetic and copies ran while one was open for 10% of the time, Pallas kernels for 0%

profile of v8, /device:TPU:0, one launch (start us, length us, event | category | flops | bytes accessed | tf_op | source)
XLA Modules:
  0.0 45.5 jit_solution(2638076714734461728)
XLA Ops:
  0.0 0.0 copy-start.1
  0.0 0.7 %copy-done.1 = s32[4]{0:T(128)S(1)} copy-done((s32[4]{0:T(128)S(1)}, s32[4]{0:T(128)}, u32[]{:S(2)}) %copy-start.1) | copy-done | bytes 40
  0.7 0.9 %broadcast_select_fusion.2 = bf16[2,4,2048]{2,0,1:T(2,128)(2,1)S(1)} fusion(pred[4]{0:T(512)(128)(4,1)S(1)} %broadcast_compare_fusion, bf16[1,2,4,2048]{3,2,1,0:T(4,128)(2,1)} %param.7), kind=kLoop, calls=%fused_computation.17 | loop fusion | flops 16384 | bytes 65540 | tf_op jit(solution)/shard_map/jit(_where)/select_n | solution.py:147
  1.5 0.1 broadcast_select_fusion.1
  1.6 0.5 %collective-permute-start.1 = (bf16[2,4,4096]{2,0,1:T(2,128)(2,1)S(1)}, bf16[2,4,4096]{2,0,1:T(2,128)(2,1)S(1)}, u32[]{:S(2)}, u32[]{:S(2)}) collective-permute-start(bf16[2,4,4096]{2,0,1:T(2,128)(2,1)S(1)} %broadcast_select_fusion.1), channel_id=1, source_target_pairs={{0,2},{1,3},{2,0},{3,1},{4,6},{5,7},{6,4},{7,5},{8,10},{9,11},{10,... | collective-permute-start | bytes 196616 | tf_op jit(solution)/shard_map/ppermute | solution.py:113
  2.1 2.6 %collective-permute-start.2 = (bf16[2,4,4096]{2,0,1:T(2,128)(2,1)S(1)}, bf16[2,4,4096]{2,0,1:T(2,128)(2,1)S(1)}, u32[]{:S(2)}, u32[]{:S(2)}) collective-permute-start(bf16[2,4,4096]{2,0,1:T(2,128)(2,1)S(1)} %broadcast_select_fusion.1), channel_id=1, source_target_pairs={{0,3},{1,2},{2,1},{3,0},{4,7},{5,6},{6,5},{7,4},{8,11},{9,10},{10,... | collective-permute-start | bytes 196616 | tf_op jit(solution)/shard_map/ppermute | solution.py:113
  4.7 0.0 collective-permute-start
  6.1 0.0 collective-permute-done.1
  6.1 1.1 %collective-permute-done.2 = bf16[2,4,4096]{2,0,1:T(2,128)(2,1)S(1)} collective-permute-done((bf16[2,4,4096]{2,0,1:T(2,128)(2,1)S(1)}, bf16[2,4,4096]{2,0,1:T(2,128)(2,1)S(1)}, u32[]{:S(2)}, u32[]{:S(2)}) %collective-permute-start.2) | collective-permute-done | bytes 65568 | tf_op jit(solution)/shard_map/ppermute | solution.py:113
  7.1 1.8 %collective-permute-done = bf16[2,4,4096]{2,0,1:T(2,128)(2,1)S(1)} collective-permute-done((bf16[2,4,4096]{2,0,1:T(2,128)(2,1)S(1)}, bf16[2,4,4096]{2,0,1:T(2,128)(2,1)S(1)}, u32[]{:S(2)}, u32[]{:S(2)}) %collective-permute-start) | collective-permute-done | bytes 65568 | tf_op jit(solution)/shard_map/ppermute | solution.py:113
  9.0 0.2 add_add_fusion.1
  9.2 0.1 copy.22
  9.2 2.6 %collective-permute-start.6 = (bf16[2,4,4096]{2,0,1:T(2,128)(2,1)S(1)}, bf16[2,4,4096]{2,0,1:T(2,128)(2,1)S(1)}, u32[]{:S(2)}, u32[]{:S(2)}) collective-permute-start(bf16[2,4,4096]{2,0,1:T(2,128)(2,1)S(1)} %add_add_fusion.1), channel_id=1, source_target_pairs={{0,12},{1,13},{2,14},{3,15},{4,8},{5,9},{6,10},{7,11},{8,4},{9,5},... | collective-permute-start | bytes 196616 | tf_op jit(solution)/shard_map/ppermute | solution.py:113
  11.8 0.4 collective-permute-start.5
  12.3 0.5 %collective-permute-start.4 = (bf16[2,4,4096]{2,0,1:T(2,128)(2,1)S(1)}, bf16[2,4,4096]{2,0,1:T(2,128)(2,1)S(1)}, u32[]{:S(2)}, u32[]{:S(2)}) collective-permute-start(bf16[2,4,4096]{2,0,1:T(2,128)(2,1)S(1)} %add_add_fusion.1), channel_id=1, source_target_pairs={{0,4},{1,5},{2,6},{3,7},{4,0},{5,1},{6,2},{7,3},{8,12},{9,13},{10,... | collective-permute-start | bytes 196616 | tf_op jit(solution)/shard_map/ppermute | solution.py:113
  12.8 0.0 copy-start
  12.8 0.5 %slice.5 = bf16[1]{0:T(256)(128)(2,1)} slice(bf16[32768]{0:T(1024)(128)(2,1)S(1)} %bitcast.37), slice={[0:1]} | slice | bytes 4 | tf_op jit(solution)/shard_map/slice | solution.py:117
  14.6 0.1 fusion.11
  14.7 0.1 fusion.9
  14.8 0.0 copy-done
  14.9 1.5 %collective-permute-start.3 = (bf16[2,4,2048]{2,0,1:T(2,128)(2,1)S(1)}, bf16[2,4,2048]{2,0,1:T(2,128)(2,1)S(1)}, u32[]{:S(2)}, u32[]{:S(2)}) collective-permute-start(bf16[2,4,2048]{2,0,1:T(2,128)(2,1)S(1)} %bitcast.32), channel_id=1, source_target_pairs={{0,1},{1,0},{2,3},{3,2},{4,5},{5,4},{6,7},{7,6},{8,9},{9,8},{10,11... | collective-permute-start | bytes 98312 | tf_op jit(solution)/shard_map/ppermute | solution.py:128
  16.4 0.1 copy.16
  16.5 0.1 copy.15
  16.6 0.9 %multiply_sine_fusion.1 = (f32[128,8]{1,0:T(8,128)}, f32[128,8]{1,0:T(8,128)}) fusion(f32[128,8]{1,0:T(8,128)S(1)} %copy.15), kind=kLoop, calls=%fused_computation.20 | loop fusion | flops 1024 | bytes 12288 | tf_op jit(solution)/shard_map/sin | solution.py:21
  17.5 0.9 %multiply_sine_fusion = (f32[128,16]{1,0:T(8,128)}, f32[128,16]{1,0:T(8,128)}) fusion(f32[128,16]{1,0:T(8,128)S(1)} %copy.16), kind=kLoop, calls=%fused_computation.18 | loop fusion | flops 2048 | bytes 24576 | tf_op jit(solution)/shard_map/sin | solution.py:21
  18.4 1.0 %fusion.7 = (f32[128,128]{1,0:T(8,128)}, f32[128,128]{1,0:T(8,128)}) fusion(s32[128]{0:T(128)S(1)} %iota_add_fusion), kind=kLoop, calls=%fused_computation.23 | loop fusion | flops 229376 | bytes 131584 | tf_op jit(solution)/shard_map/sin | solution.py:21
  19.4 0.0 collective-permute-done.3
  19.4 0.1 fusion.3
  19.5 0.0 collective-permute-done.6
  19.5 0.0 collective-permute-done.5
  19.5 0.0 collective-permute-done.4
  19.6 2.7 %collective-permute-start.7 = (bf16[2,4,4096]{2,0,1:T(2,128)(2,1)S(1)}, bf16[2,4,4096]{2,0,1:T(2,128)(2,1)S(1)}, u32[]{:S(2)}, u32[]{:S(2)}) collective-permute-start(bf16[2,4,4096]{2,0,1:T(2,128)(2,1)S(1)} %bitcast.27), channel_id=1, source_target_pairs={{0,16},{1,17},{2,18},{3,19},{4,20},{5,21},{6,22},{7,23},{8,24},{9,... | collective-permute-start | bytes 196616 | tf_op jit(solution)/shard_map/ppermute | solution.py:113
  22.2 0.7 %pad_convert_fusion.wpad_ref = f32[4,2,5248]{2,1,0:T(2,128)} fusion(bf16[4,2,4096]{2,1,0:T(2,128)(2,1)S(1)} %fusion.3), kind=kLoop, calls=%fused_computation.6 | loop fusion | flops 41984 | bytes 233472 | tf_op jit(solution)/shard_map/jit(_pad)/pad | solution.py:160
  23.0 1.8 %collective-permute-done.7 = bf16[2,4,4096]{2,0,1:T(2,128)(2,1)S(1)} collective-permute-done((bf16[2,4,4096]{2,0,1:T(2,128)(2,1)S(1)}, bf16[2,4,4096]{2,0,1:T(2,128)(2,1)S(1)}, u32[]{:S(2)}, u32[]{:S(2)}) %collective-permute-start.7) | collective-permute-done | bytes 65568 | tf_op jit(solution)/shard_map/ppermute | solution.py:113
  24.8 0.1 add.82
  24.9 0.7 %convert_bitcast_fusion.ref_ref = f32[8,2,2048]{2,1,0:T(2,128)} fusion(bf16[2,8,2048]{2,0,1:T(2,128)(2,1)S(1)} %bitcast.29), kind=kLoop, calls=%fused_computation | loop fusion | flops 32768 | bytes 196608 | tf_op jit(solution)/shard_map/convert_element_type | solution.py:161
  25.6 20.0 %shard_map.64 = f32[6,2,128,128]{3,2,1,0:T(8,128)} custom-call(s32[6]{0:T(128)} %bitcast.39, s32[1]{0:T(128)S(6)} %copy.25.count_ref, f32[4,2,5248]{2,1,0:T(2,128)} %pad_convert_fusion.wpad_ref, f32[8,2,2048]{2,1,0:T(2,128)} %convert_bitcast_fusion.ref_ref, f32[128,8]{1,0:T(8,128)} %get-tuple-element.8.ac_ref, f32[128,8]{1,0:T(8,128)} %get-tuple-element.7.as_ref, ...), custom_call_target="tpu_custom_call" | custom-call | tf_op jit(solution)/shard_map/pallas_call | solution.py:173
  (8 shorter events, 0.1 us)
Async XLA Ops:
  0.0 0.7 %copy-start.1 = (s32[4]{0:T(128)S(1)}, s32[4]{0:T(128)}, u32[]{:S(2)}) copy-start(s32[4]{0:T(128)} %param.8) | copy-start | bytes 52
  1.6 4.5 %collective-permute-start.1 = (bf16[2,4,4096]{2,0,1:T(2,128)(2,1)S(1)}, bf16[2,4,4096]{2,0,1:T(2,128)(2,1)S(1)}, u32[]{:S(2)}, u32[]{:S(2)}) collective-permute-start(bf16[2,4,4096]{2,0,1:T(2,128)(2,1)S(1)} %broadcast_select_fusion.1), channel_id=1, source_target_pairs={{0,2},{1,3},{2,0},{3,1},{4,6},{5,7},{6,4},{7,5},{8,10},{9,11},{10,... | collective-permute-start | bytes 196616 | tf_op jit(solution)/shard_map/ppermute | solution.py:113
  2.1 5.0 %collective-permute-start.2 = (bf16[2,4,4096]{2,0,1:T(2,128)(2,1)S(1)}, bf16[2,4,4096]{2,0,1:T(2,128)(2,1)S(1)}, u32[]{:S(2)}, u32[]{:S(2)}) collective-permute-start(bf16[2,4,4096]{2,0,1:T(2,128)(2,1)S(1)} %broadcast_select_fusion.1), channel_id=1, source_target_pairs={{0,3},{1,2},{2,1},{3,0},{4,7},{5,6},{6,5},{7,4},{8,11},{9,10},{10,... | collective-permute-start | bytes 196616 | tf_op jit(solution)/shard_map/ppermute | solution.py:113
  4.7 4.3 %collective-permute-start = (bf16[2,4,4096]{2,0,1:T(2,128)(2,1)S(1)}, bf16[2,4,4096]{2,0,1:T(2,128)(2,1)S(1)}, u32[]{:S(2)}, u32[]{:S(2)}) collective-permute-start(bf16[2,4,4096]{2,0,1:T(2,128)(2,1)S(1)} %broadcast_select_fusion.1), channel_id=1, source_target_pairs={{0,1},{1,0},{2,3},{3,2},{4,5},{5,4},{6,7},{7,6},{8,9},{9,8},{10,11... | collective-permute-start | bytes 196616 | tf_op jit(solution)/shard_map/ppermute | solution.py:113
  9.2 10.3 %collective-permute-start.6 = (bf16[2,4,4096]{2,0,1:T(2,128)(2,1)S(1)}, bf16[2,4,4096]{2,0,1:T(2,128)(2,1)S(1)}, u32[]{:S(2)}, u32[]{:S(2)}) collective-permute-start(bf16[2,4,4096]{2,0,1:T(2,128)(2,1)S(1)} %add_add_fusion.1), channel_id=1, source_target_pairs={{0,12},{1,13},{2,14},{3,15},{4,8},{5,9},{6,10},{7,11},{8,4},{9,5},... | collective-permute-start | bytes 196616 | tf_op jit(solution)/shard_map/ppermute | solution.py:113
  11.8 7.7 %collective-permute-start.5 = (bf16[2,4,4096]{2,0,1:T(2,128)(2,1)S(1)}, bf16[2,4,4096]{2,0,1:T(2,128)(2,1)S(1)}, u32[]{:S(2)}, u32[]{:S(2)}) collective-permute-start(bf16[2,4,4096]{2,0,1:T(2,128)(2,1)S(1)} %add_add_fusion.1), channel_id=1, source_target_pairs={{0,8},{1,9},{2,10},{3,11},{4,12},{5,13},{6,14},{7,15},{8,0},{9,1},... | collective-permute-start | bytes 196616 | tf_op jit(solution)/shard_map/ppermute | solution.py:113
  12.3 7.2 %collective-permute-start.4 = (bf16[2,4,4096]{2,0,1:T(2,128)(2,1)S(1)}, bf16[2,4,4096]{2,0,1:T(2,128)(2,1)S(1)}, u32[]{:S(2)}, u32[]{:S(2)}) collective-permute-start(bf16[2,4,4096]{2,0,1:T(2,128)(2,1)S(1)} %add_add_fusion.1), channel_id=1, source_target_pairs={{0,4},{1,5},{2,6},{3,7},{4,0},{5,1},{6,2},{7,3},{8,12},{9,13},{10,... | collective-permute-start | bytes 196616 | tf_op jit(solution)/shard_map/ppermute | solution.py:113
  12.8 2.0 %copy-start = (bf16[1,2,4,2048]{3,2,1,0:T(4,128)(2,1)S(1)}, bf16[1,2,4,2048]{3,2,1,0:T(4,128)(2,1)}, u32[]{:S(2)}) copy-start(bf16[1,2,4,2048]{3,2,1,0:T(4,128)(2,1)} %param.6) | copy-start | bytes 98308
  14.9 4.5 %collective-permute-start.3 = (bf16[2,4,2048]{2,0,1:T(2,128)(2,1)S(1)}, bf16[2,4,2048]{2,0,1:T(2,128)(2,1)S(1)}, u32[]{:S(2)}, u32[]{:S(2)}) collective-permute-start(bf16[2,4,2048]{2,0,1:T(2,128)(2,1)S(1)} %bitcast.32), channel_id=1, source_target_pairs={{0,1},{1,0},{2,3},{3,2},{4,5},{5,4},{6,7},{7,6},{8,9},{9,8},{10,11... | collective-permute-start | bytes 98312 | tf_op jit(solution)/shard_map/ppermute | solution.py:128
  19.6 5.2 %collective-permute-start.7 = (bf16[2,4,4096]{2,0,1:T(2,128)(2,1)S(1)}, bf16[2,4,4096]{2,0,1:T(2,128)(2,1)S(1)}, u32[]{:S(2)}, u32[]{:S(2)}) collective-permute-start(bf16[2,4,4096]{2,0,1:T(2,128)(2,1)S(1)} %bitcast.27), channel_id=1, source_target_pairs={{0,16},{1,17},{2,18},{3,19},{4,20},{5,21},{6,22},{7,23},{8,24},{9,... | collective-permute-start | bytes 196616 | tf_op jit(solution)/shard_map/ppermute | solution.py:113

commit v9 on v8

--- a/solution.py
+++ b/solution.py
@@ -34,8 +34,13 @@
     return (turn(high) + turn(mid)) + turn(low)
 
 
-def caf_kernel(blocks_ref, count_ref, wpad_ref, ref_ref, ac_ref, as_ref, hc_ref, hs_ref, lc_ref, ls_ref,
-               out_ref, first_buf, second_buf, acc, bc_ref, bs_ref, *, chunks, slots, span, steps, norm):
+def caf_kernel(blocks_ref, count_ref, wpad_ref, ref_ref, cos_ref, sin_ref,
+               out_ref, first_buf, second_buf, acc, bc_ref, bs_ref, *, chunks, slots, span, steps, groups, norm):
+    def column(ref, lane):
+        tail = ref[:, LB:]
+        pick = lax.broadcasted_iota(jnp.int32, tail.shape, 1) == lane
+        return jnp.sum(jnp.where(pick, tail, 0.0), axis=1, keepdims=True)
+
     pair = pl.program_id(0)
     lanes = PIECE + LB
     pieces = [(comp, i) for comp in range(2) for i in range(span // PIECE)]
@@ -51,11 +56,11 @@
     @pl.when(pair == 0)
     def _():
         acc[...] = jnp.zeros_like(acc)
-        l_c = lc_ref[...]
-        l_s = ls_ref[...]
+        l_c = cos_ref[:, :LB]
+        l_s = sin_ref[:, :LB]
         for i in range(CHUNK // LB):
-            h_c = jnp.broadcast_to(hc_ref[:, i:i + 1], (LB, LB))
-            h_s = jnp.broadcast_to(hs_ref[:, i:i + 1], (LB, LB))
+            h_c = jnp.broadcast_to(column(cos_ref, groups + i), (LB, LB))
+            h_s = jnp.broadcast_to(column(sin_ref, groups + i), (LB, LB))
             bc_ref[:, i * LB:(i + 1) * LB] = h_c * l_c - h_s * l_s
             bs_ref[:, i * LB:(i + 1) * LB] = h_s * l_c + h_c * l_s
         for comp, i in pieces:
@@ -69,9 +74,8 @@
             rr = ref_ref[g]
             r_re = rr[0:1, :]
             r_im = rr[1:2, :]
-            pick = lax.broadcasted_iota(jnp.int32, ac_ref.shape, 1) == g
-            a_c = jnp.broadcast_to(jnp.sum(jnp.where(pick, ac_ref[...], 0.0), axis=1, keepdims=True), (LB, CHUNK))
-            a_s = jnp.broadcast_to(jnp.sum(jnp.where(pick, as_ref[...], 0.0), axis=1, keepdims=True), (LB, CHUNK))
+            a_c = jnp.broadcast_to(column(cos_ref, g), (LB, CHUNK))
+            a_s = jnp.broadcast_to(column(sin_ref, g), (LB, CHUNK))
             b_c = bc_ref[...]
             b_s = bs_ref[...]
             cos_part = a_c * b_c - a_s * b_s
@@ -103,21 +107,28 @@
             out_ref[q, 1] = jnp.where(keep, reverse_rows(im) * norm, 0.0)
 
 
-def butterfly_sum(value, axes, later=()):
+def butterfly_sum(value, axes, later=(), rider=None):
     count = lax.axis_size(axes)
-    if count & (count - 1):
-        return lax.psum(value, axes), later
     stride = 1
+    carried = None
     while stride < count:
         radix = 4 if stride * 4 <= count else 2
-        parts = [lax.ppermute(value, axes, [(i, i ^ (m * stride)) for i in range(count)]) for m in range(1, radix)]
+        parts = []
+        for m in range(1, radix):
+            pairs = [(i, i ^ (m * stride)) for i in range(count)]
+            if stride == 1 and m == 1 and rider is not None:
+                both = lax.ppermute(jnp.concatenate([value, rider], -1), axes, pairs)
+                parts.append(both[..., :value.shape[-1]])
+                carried = both[..., value.shape[-1]:]
+            else:
+                parts.append(lax.ppermute(value, axes, pairs))
         for part in parts:
             value = value + part
         if stride == 1:
             late = (value.reshape(-1)[0] != value.reshape(-1)[0]).astype(jnp.int32)
             later = jax.tree.map(lambda x: x + late.astype(x.dtype), later)
         stride *= radix
-    return value, later
+    return value, later, carried
 
 
 def seg_join(half, axis):
@@ -145,15 +156,18 @@
 
     mine = (owner_index == beam_place)[None, :, None]
     local = jnp.where(mine, reference_blocks[0], jnp.zeros_like(reference_blocks[0]))
-    if segments == 2:
+    group = lax.axis_size(("beam", "seg"))
+    if segments == 2 and group >= 4 and not group & (group - 1):
         first = seg_place == 0
         zero = jnp.zeros_like(local)
         placed = jnp.where(first, jnp.concatenate([local, zero], -1), jnp.concatenate([zero, local], -1))
-        refs, (own_samples, first_bin) = butterfly_sum(placed, ("beam", "seg"), (surveillance[0], doppler_start[0]))
+        refs, (first_bin,), other = butterfly_sum(placed, ("beam", "seg"), (doppler_start[0],), surveillance[0])
+        samples = jnp.where(first, jnp.concatenate([surveillance[0], other], -1),
+                            jnp.concatenate([other, surveillance[0]], -1))
     else:
-        refs, (own_samples, first_bin) = butterfly_sum(local, "beam", (surveillance[0], doppler_start[0]))
-        refs = seg_join(refs, "seg")
-    samples = seg_join(own_samples, "seg")
+        refs = seg_join(lax.psum(local, "beam"), "seg")
+        samples = seg_join(surveillance[0], "seg")
+        first_bin = doppler_start[0]
 
     span = step_len + rim_len
     wpad = jnp.transpose(samples, (1, 0, 2)).astype(jnp.float32)
@@ -161,13 +175,14 @@
     refrows = jnp.transpose(refs.reshape(2, step_count * chunks, CHUNK), (1, 0, 2)).astype(jnp.float32)
 
     freqs = first_bin + seg_place * bins + jnp.arange(bins, dtype=jnp.int32)
-    a_c, a_s = phase_rows(freqs, jnp.arange(step_count * chunks, dtype=jnp.int32) * CHUNK, window_len)
-    h_c, h_s = phase_rows(freqs, jnp.arange(CHUNK // LB, dtype=jnp.int32) * LB, window_len)
-    l_c, l_s = phase_rows(freqs, jnp.arange(LB, dtype=jnp.int32), window_len)
-
-    tables = (a_c, a_s, h_c, h_s, l_c, l_s)
+    times = jnp.concatenate([jnp.arange(LB, dtype=jnp.int32),
+                             jnp.arange(step_count * chunks, dtype=jnp.int32) * CHUNK,
+                             jnp.arange(CHUNK // LB, dtype=jnp.int32) * LB])
+    cos_rows, sin_rows = phase_rows(freqs, times, window_len)
+    tables = (cos_rows, sin_rows)
     assert step_count % 2 == 0
     kernel = functools.partial(caf_kernel, chunks=chunks, slots=slot_count, span=span, steps=step_count,
+                               groups=step_count * chunks,
                                norm=1.0 / math.sqrt(window_len))
     full = lambda shape: pl.BlockSpec(shape, lambda k, *_: (0,) * len(shape))
     out = pl.pallas_call(

time: 45.9 us -> 43.7 us (0.952)
  other arithmetic: 5.68 us -> 4.19 us
  starting transfers between devices: 10.9 us -> 9.89 us
  waiting for transfers between devices: 4.74 us -> 5.2 us
    sin x3 -> x1, other arithmetic: 2.77 us -> 1.31 us  [phase_rows(): return (jnp.cos(angle), jnp.sin(angle))]
    ppermute x8 -> x7, starting transfers between devices: 10.9 us -> 9.89 us  [the longest x6 9.34 us: butterfly_sum(): parts.append(lax.ppermute(value, axes, pairs))]
    ppermute x8 -> x7, waiting for transfers between devices: 4.74 us -> 5.2 us  [the longest x6 2.66 us: butterfly_sum(): parts.append(lax.ppermute(value, axes, pairs))]
  transfers between devices with their start and end apart: 8 -> 7, of which waited for: 3 -> 5; matrix products, arithmetic and copies ran while one was open for 10% -> 7% of each run, Pallas kernels for 0% -> 0%
where the time goes in v9:
time: 43.7 us; the launch traced here: 43.6 us
  Pallas kernels  20.3 us (46%)
  starting transfers between devices  9.89 us (23%)
  waiting for transfers between devices  5.2 us (12%)
  other arithmetic  4.19 us (10%)
  between operations  2.69 us (6%)
  local copies, waits for them, and re-layouts  1.3 us (3%)
    pallas_call x1, Pallas kernels, shards(): pl.pallas_call(kernel, out_shape=jax.ShapeDtypeStruct((slot_count, 2, LB,...  20.3 us
    ppermute x6, starting transfers between devices, butterfly_sum(): parts.append(lax.ppermute(value, axes, pairs))  9.34 us
    ppermute x6, waiting for transfers between devices, butterfly_sum(): parts.append(lax.ppermute(value, axes, pairs))  2.66 us
    ppermute x1, waiting for transfers between devices, butterfly_sum(): both = lax.ppermute(jnp.concatenate([value, rider], -1), axes, pairs)  2.54 us
    sin x1, other arithmetic, phase_rows(): return (jnp.cos(angle), jnp.sin(angle))  1.31 us
  transfers between devices with their start and end apart: 7, of which 5 were waited for; matrix products, arithmetic and copies ran while one was open for 7% of the time, Pallas kernels for 0%

profile of v9, /device:TPU:0, one launch (start us, length us, event | category | flops | bytes accessed | tf_op | source)
XLA Modules:
  0.0 43.6 jit_solution(16515194082964405118)
XLA Ops:
  0.0 0.0 copy-start.1
  0.0 0.7 %copy-done.1 = s32[4]{0:T(128)S(1)} copy-done((s32[4]{0:T(128)S(1)}, s32[4]{0:T(128)}, u32[]{:S(2)}) %copy-start.1) | copy-done | bytes 40
  0.7 0.9 %broadcast_select_fusion.2 = bf16[2,4,2048]{2,0,1:T(2,128)(2,1)S(1)} fusion(pred[4]{0:T(512)(128)(4,1)S(1)} %broadcast_compare_fusion, bf16[1,2,4,2048]{3,2,1,0:T(4,128)(2,1)} %param.7), kind=kLoop, calls=%fused_computation.21 | loop fusion | flops 16384 | bytes 65540 | tf_op jit(solution)/shard_map/jit(_where)/select_n | solution.py:158
  1.5 0.0 copy-start
  1.5 0.1 broadcast_select_fusion.1
  1.6 0.5 %collective-permute-start.1 = (bf16[2,4,4096]{2,0,1:T(2,128)(2,1)S(1)}, bf16[2,4,4096]{2,0,1:T(2,128)(2,1)S(1)}, u32[]{:S(2)}, u32[]{:S(2)}) collective-permute-start(bf16[2,4,4096]{2,0,1:T(2,128)(2,1)S(1)} %broadcast_select_fusion.1), channel_id=1, source_target_pairs={{0,2},{1,3},{2,0},{3,1},{4,6},{5,7},{6,4},{7,5},{8,10},{9,11},{10,... | collective-permute-start | bytes 196616 | tf_op jit(solution)/shard_map/ppermute | solution.py:124
  2.1 2.6 %collective-permute-start.2 = (bf16[2,4,4096]{2,0,1:T(2,128)(2,1)S(1)}, bf16[2,4,4096]{2,0,1:T(2,128)(2,1)S(1)}, u32[]{:S(2)}, u32[]{:S(2)}) collective-permute-start(bf16[2,4,4096]{2,0,1:T(2,128)(2,1)S(1)} %broadcast_select_fusion.1), channel_id=1, source_target_pairs={{0,3},{1,2},{2,1},{3,0},{4,7},{5,6},{6,5},{7,4},{8,11},{9,10},{10,... | collective-permute-start | bytes 196616 | tf_op jit(solution)/shard_map/ppermute | solution.py:124
  4.7 0.0 copy-done
  4.8 0.1 pad_maximum_fusion
  4.9 0.6 %collective-permute-start = (bf16[2,4,6144]{2,0,1:T(2,128)(2,1)S(1)}, bf16[2,4,6144]{2,0,1:T(2,128)(2,1)S(1)}, u32[]{:S(2)}, u32[]{:S(2)}) collective-permute-start(bf16[2,4,6144]{2,0,1:T(2,128)(2,1)S(1)} %pad_maximum_fusion), channel_id=1, source_target_pairs={{0,1},{1,0},{2,3},{3,2},{4,5},{5,4},{6,7},{7,6},{8,9},{9,8},{10,11... | collective-permute-start | bytes 294920 | tf_op jit(solution)/shard_map/ppermute | solution.py:120
  6.7 0.1 pad_add_fusion
  6.8 0.0 collective-permute-done.1
  6.8 0.3 collective-permute-done.2
  7.2 2.5 %collective-permute-done = bf16[2,4,6144]{2,0,1:T(2,128)(2,1)S(1)} collective-permute-done((bf16[2,4,6144]{2,0,1:T(2,128)(2,1)S(1)}, bf16[2,4,6144]{2,0,1:T(2,128)(2,1)S(1)}, u32[]{:S(2)}, u32[]{:S(2)}) %collective-permute-start) | collective-permute-done | bytes 98336 | tf_op jit(solution)/shard_map/ppermute | solution.py:120
  9.7 0.2 fusion.5
  9.9 0.1 copy.16
  9.9 2.6 %collective-permute-start.5 = (bf16[2,4,4096]{2,0,1:T(2,128)(2,1)S(1)}, bf16[2,4,4096]{2,0,1:T(2,128)(2,1)S(1)}, u32[]{:S(2)}, u32[]{:S(2)}) collective-permute-start(bf16[2,4,4096]{2,0,1:T(2,128)(2,1)S(1)} %fusion.5), channel_id=1, source_target_pairs={{0,12},{1,13},{2,14},{3,15},{4,8},{5,9},{6,10},{7,11},{8,4},{9,5},... | collective-permute-start | bytes 196616 | tf_op jit(solution)/shard_map/ppermute | solution.py:124
  12.5 0.4 %collective-permute-start.4 = (bf16[2,4,4096]{2,0,1:T(2,128)(2,1)S(1)}, bf16[2,4,4096]{2,0,1:T(2,128)(2,1)S(1)}, u32[]{:S(2)}, u32[]{:S(2)}) collective-permute-start(bf16[2,4,4096]{2,0,1:T(2,128)(2,1)S(1)} %fusion.5), channel_id=1, source_target_pairs={{0,8},{1,9},{2,10},{3,11},{4,12},{5,13},{6,14},{7,15},{8,0},{9,1},... | collective-permute-start | bytes 196616 | tf_op jit(solution)/shard_map/ppermute | solution.py:124
  13.0 0.5 %collective-permute-start.3 = (bf16[2,4,4096]{2,0,1:T(2,128)(2,1)S(1)}, bf16[2,4,4096]{2,0,1:T(2,128)(2,1)S(1)}, u32[]{:S(2)}, u32[]{:S(2)}) collective-permute-start(bf16[2,4,4096]{2,0,1:T(2,128)(2,1)S(1)} %fusion.5), channel_id=1, source_target_pairs={{0,4},{1,5},{2,6},{3,7},{4,0},{5,1},{6,2},{7,3},{8,12},{9,13},{10,... | collective-permute-start | bytes 196616 | tf_op jit(solution)/shard_map/ppermute | solution.py:124
  13.5 0.1 fusion.3
  13.7 0.5 %slice.15 = bf16[1]{0:T(256)(128)(2,1)} slice(bf16[32768]{0:T(1024)(128)(2,1)S(1)} %bitcast.33), slice={[0:1]} | slice | bytes 4 | tf_op jit(solution)/shard_map/slice | solution.py:128
  15.5 0.7 %pad_convert_fusion.wpad_ref = f32[4,2,5248]{2,1,0:T(2,128)} fusion(bf16[4,2,4096]{2,1,0:T(2,128)(2,1)S(1)} %fusion.3), kind=kLoop, calls=%fused_computation.12 | loop fusion | flops 41984 | bytes 233472 | tf_op jit(solution)/shard_map/jit(_pad)/pad | solution.py:174
  16.2 0.0 collective-permute-done.5
  16.2 0.6 %collective-permute-done.4 = bf16[2,4,4096]{2,0,1:T(2,128)(2,1)S(1)} collective-permute-done((bf16[2,4,4096]{2,0,1:T(2,128)(2,1)S(1)}, bf16[2,4,4096]{2,0,1:T(2,128)(2,1)S(1)}, u32[]{:S(2)}, u32[]{:S(2)}) %collective-permute-start.4) | collective-permute-done | bytes 65568 | tf_op jit(solution)/shard_map/ppermute | solution.py:124
  16.8 0.4 %collective-permute-done.3 = bf16[2,4,4096]{2,0,1:T(2,128)(2,1)S(1)} collective-permute-done((bf16[2,4,4096]{2,0,1:T(2,128)(2,1)S(1)}, bf16[2,4,4096]{2,0,1:T(2,128)(2,1)S(1)}, u32[]{:S(2)}, u32[]{:S(2)}) %collective-permute-start.3) | collective-permute-done | bytes 65568 | tf_op jit(solution)/shard_map/ppermute | solution.py:124
  17.3 2.7 %collective-permute-start.6 = (bf16[2,4,4096]{2,0,1:T(2,128)(2,1)S(1)}, bf16[2,4,4096]{2,0,1:T(2,128)(2,1)S(1)}, u32[]{:S(2)}, u32[]{:S(2)}) collective-permute-start(bf16[2,4,4096]{2,0,1:T(2,128)(2,1)S(1)} %bitcast.26), channel_id=1, source_target_pairs={{0,16},{1,17},{2,18},{3,19},{4,20},{5,21},{6,22},{7,23},{8,24},{9,... | collective-permute-start | bytes 196616 | tf_op jit(solution)/shard_map/ppermute | solution.py:124
  19.9 1.3 %fusion.6 = (f32[128,152]{1,0:T(8,128)}, f32[128,152]{1,0:T(8,128)}) fusion(s32[152]{0:T(256)S(1)} %pad_add_fusion, s32[128]{0:T(128)S(1)} %iota_add_fusion), kind=kLoop, calls=%fused_computation.18 | loop fusion | flops 272384 | bytes 156768 | tf_op jit(solution)/shard_map/sin | solution.py:21
  21.2 1.3 %collective-permute-done.6 = bf16[2,4,4096]{2,0,1:T(2,128)(2,1)S(1)} collective-permute-done((bf16[2,4,4096]{2,0,1:T(2,128)(2,1)S(1)}, bf16[2,4,4096]{2,0,1:T(2,128)(2,1)S(1)}, u32[]{:S(2)}, u32[]{:S(2)}) %collective-permute-start.6) | collective-permute-done | bytes 65568 | tf_op jit(solution)/shard_map/ppermute | solution.py:124
  22.5 0.1 add.58
  22.6 0.7 %convert_bitcast_fusion.ref_ref = f32[8,2,2048]{2,1,0:T(2,128)} fusion(bf16[2,8,2048]{2,0,1:T(2,128)(2,1)S(1)} %bitcast.28), kind=kLoop, calls=%fused_computation.8 | loop fusion | flops 32768 | bytes 196608 | tf_op jit(solution)/shard_map/convert_element_type | solution.py:175
  23.3 20.3 %shard_map.64 = f32[6,2,128,128]{3,2,1,0:T(8,128)} custom-call(s32[6]{0:T(128)} %bitcast.34, s32[1]{0:T(128)S(6)} %copy.19.count_ref, f32[4,2,5248]{2,1,0:T(2,128)} %pad_convert_fusion.wpad_ref, f32[8,2,2048]{2,1,0:T(2,128)} %convert_bitcast_fusion.ref_ref, f32[128,152]{1,0:T(8,128)} %get-tuple-element.6.cos_ref, f32[128,152]{1,0:T(8,128)} %get-tuple-element.5.sin_ref), custom_call_target="tpu_custom_call" | custom-call | tf_op jit(solution)/shard_map/pallas_call | solution.py:188
  (9 shorter events, 0.1 us)
Async XLA Ops:
  0.0 0.7 %copy-start.1 = (s32[4]{0:T(128)S(1)}, s32[4]{0:T(128)}, u32[]{:S(2)}) copy-start(s32[4]{0:T(128)} %param.8) | copy-start | bytes 52
  1.5 3.2 %copy-start = (bf16[1,2,4,2048]{3,2,1,0:T(4,128)(2,1)S(1)}, bf16[1,2,4,2048]{3,2,1,0:T(4,128)(2,1)}, u32[]{:S(2)}) copy-start(bf16[1,2,4,2048]{3,2,1,0:T(4,128)(2,1)} %param.6) | copy-start | bytes 98308
  1.6 5.2 %collective-permute-start.1 = (bf16[2,4,4096]{2,0,1:T(2,128)(2,1)S(1)}, bf16[2,4,4096]{2,0,1:T(2,128)(2,1)S(1)}, u32[]{:S(2)}, u32[]{:S(2)}) collective-permute-start(bf16[2,4,4096]{2,0,1:T(2,128)(2,1)S(1)} %broadcast_select_fusion.1), channel_id=1, source_target_pairs={{0,2},{1,3},{2,0},{3,1},{4,6},{5,7},{6,4},{7,5},{8,10},{9,11},{10,... | collective-permute-start | bytes 196616 | tf_op jit(solution)/shard_map/ppermute | solution.py:124
  2.1 5.0 %collective-permute-start.2 = (bf16[2,4,4096]{2,0,1:T(2,128)(2,1)S(1)}, bf16[2,4,4096]{2,0,1:T(2,128)(2,1)S(1)}, u32[]{:S(2)}, u32[]{:S(2)}) collective-permute-start(bf16[2,4,4096]{2,0,1:T(2,128)(2,1)S(1)} %broadcast_select_fusion.1), channel_id=1, source_target_pairs={{0,3},{1,2},{2,1},{3,0},{4,7},{5,6},{6,5},{7,4},{8,11},{9,10},{10,... | collective-permute-start | bytes 196616 | tf_op jit(solution)/shard_map/ppermute | solution.py:124
  4.9 4.8 %collective-permute-start = (bf16[2,4,6144]{2,0,1:T(2,128)(2,1)S(1)}, bf16[2,4,6144]{2,0,1:T(2,128)(2,1)S(1)}, u32[]{:S(2)}, u32[]{:S(2)}) collective-permute-start(bf16[2,4,6144]{2,0,1:T(2,128)(2,1)S(1)} %pad_maximum_fusion), channel_id=1, source_target_pairs={{0,1},{1,0},{2,3},{3,2},{4,5},{5,4},{6,7},{7,6},{8,9},{9,8},{10,11... | collective-permute-start | bytes 294920 | tf_op jit(solution)/shard_map/ppermute | solution.py:120
  9.9 6.3 %collective-permute-start.5 = (bf16[2,4,4096]{2,0,1:T(2,128)(2,1)S(1)}, bf16[2,4,4096]{2,0,1:T(2,128)(2,1)S(1)}, u32[]{:S(2)}, u32[]{:S(2)}) collective-permute-start(bf16[2,4,4096]{2,0,1:T(2,128)(2,1)S(1)} %fusion.5), channel_id=1, source_target_pairs={{0,12},{1,13},{2,14},{3,15},{4,8},{5,9},{6,10},{7,11},{8,4},{9,5},... | collective-permute-start | bytes 196616 | tf_op jit(solution)/shard_map/ppermute | solution.py:124
  12.5 4.3 %collective-permute-start.4 = (bf16[2,4,4096]{2,0,1:T(2,128)(2,1)S(1)}, bf16[2,4,4096]{2,0,1:T(2,128)(2,1)S(1)}, u32[]{:S(2)}, u32[]{:S(2)}) collective-permute-start(bf16[2,4,4096]{2,0,1:T(2,128)(2,1)S(1)} %fusion.5), channel_id=1, source_target_pairs={{0,8},{1,9},{2,10},{3,11},{4,12},{5,13},{6,14},{7,15},{8,0},{9,1},... | collective-permute-start | bytes 196616 | tf_op jit(solution)/shard_map/ppermute | solution.py:124
  13.0 4.3 %collective-permute-start.3 = (bf16[2,4,4096]{2,0,1:T(2,128)(2,1)S(1)}, bf16[2,4,4096]{2,0,1:T(2,128)(2,1)S(1)}, u32[]{:S(2)}, u32[]{:S(2)}) collective-permute-start(bf16[2,4,4096]{2,0,1:T(2,128)(2,1)S(1)} %fusion.5), channel_id=1, source_target_pairs={{0,4},{1,5},{2,6},{3,7},{4,0},{5,1},{6,2},{7,3},{8,12},{9,13},{10,... | collective-permute-start | bytes 196616 | tf_op jit(solution)/shard_map/ppermute | solution.py:124
  17.3 5.2 %collective-permute-start.6 = (bf16[2,4,4096]{2,0,1:T(2,128)(2,1)S(1)}, bf16[2,4,4096]{2,0,1:T(2,128)(2,1)S(1)}, u32[]{:S(2)}, u32[]{:S(2)}) collective-permute-start(bf16[2,4,4096]{2,0,1:T(2,128)(2,1)S(1)} %bitcast.26), channel_id=1, source_target_pairs={{0,16},{1,17},{2,18},{3,19},{4,20},{5,21},{6,22},{7,23},{8,24},{9,... | collective-permute-start | bytes 196616 | tf_op jit(solution)/shard_map/ppermute | solution.py:124

commit v10 on v9

--- a/solution.py
+++ b/solution.py
@@ -71,7 +71,7 @@
     def one_step(step, cur, nxt, next_step):
         for c in range(chunks):
             g = step * chunks + c
-            rr = ref_ref[g]
+            rr = ref_ref[g].astype(jnp.float32)
             r_re = rr[0:1, :]
             r_im = rr[1:2, :]
             a_c = jnp.broadcast_to(column(cos_ref, g), (LB, CHUNK))
@@ -117,9 +117,9 @@
         for m in range(1, radix):
             pairs = [(i, i ^ (m * stride)) for i in range(count)]
             if stride == 1 and m == 1 and rider is not None:
-                both = lax.ppermute(jnp.concatenate([value, rider], -1), axes, pairs)
-                parts.append(both[..., :value.shape[-1]])
-                carried = both[..., value.shape[-1]:]
+                both = lax.ppermute(jnp.concatenate([value, rider], 0), axes, pairs)
+                parts.append(both[:value.shape[0]])
+                carried = both[value.shape[0]:]
             else:
                 parts.append(lax.ppermute(value, axes, pairs))
         for part in parts:
@@ -157,22 +157,24 @@
     mine = (owner_index == beam_place)[None, :, None]
     local = jnp.where(mine, reference_blocks[0], jnp.zeros_like(reference_blocks[0]))
     group = lax.axis_size(("beam", "seg"))
-    if segments == 2 and group >= 4 and not group & (group - 1):
+    if segments == 2 and group >= 4 and not group & (group - 1) and seg_len == CHUNK:
         first = seg_place == 0
-        zero = jnp.zeros_like(local)
-        placed = jnp.where(first, jnp.concatenate([local, zero], -1), jnp.concatenate([zero, local], -1))
-        refs, (first_bin,), other = butterfly_sum(placed, ("beam", "seg"), (doppler_start[0],), surveillance[0])
-        samples = jnp.where(first, jnp.concatenate([surveillance[0], other], -1),
-                            jnp.concatenate([other, surveillance[0]], -1))
+        own = jnp.transpose(local, (1, 0, 2))
+        zero = jnp.zeros_like(own)
+        placed = jnp.where(first, jnp.stack([own, zero], 1), jnp.stack([zero, own], 1)).reshape(-1, 2, seg_len)
+        mine_samples = jnp.transpose(surveillance[0], (1, 0, 2))
+        refrows, (first_bin,), other = butterfly_sum(placed, ("beam", "seg"), (doppler_start[0],), mine_samples)
+        samples = jnp.where(first, jnp.concatenate([mine_samples, other], -1),
+                            jnp.concatenate([other, mine_samples], -1))
     else:
         refs = seg_join(lax.psum(local, "beam"), "seg")
-        samples = seg_join(surveillance[0], "seg")
+        refrows = jnp.transpose(refs.reshape(2, step_count * chunks, CHUNK), (1, 0, 2))
+        samples = jnp.transpose(seg_join(surveillance[0], "seg"), (1, 0, 2))
         first_bin = doppler_start[0]
 
     span = step_len + rim_len
-    wpad = jnp.transpose(samples, (1, 0, 2)).astype(jnp.float32)
+    wpad = samples.astype(jnp.float32)
     wpad = jnp.pad(wpad, ((0, 0), (0, 0), (0, span + LB - step_len)))
-    refrows = jnp.transpose(refs.reshape(2, step_count * chunks, CHUNK), (1, 0, 2)).astype(jnp.float32)
 
     freqs = first_bin + seg_place * bins + jnp.arange(bins, dtype=jnp.int32)
     times = jnp.concatenate([jnp.arange(LB, dtype=jnp.int32),

time: 43.7 us -> 43.1 us (0.986)
  Pallas kernels: 20.3 us -> 19.8 us
    another operation x0 -> x1, other arithmetic: none -> 0.84 us  [shards(): jnp.stack([own, zero], 1)]
    convert_element_type x2 -> x0, other arithmetic: 0.8 us -> none  [the longest x1 0.7 us: shards(): jnp.transpose(refs.reshape(2, step_count * chunks, CHUNK), (1, 0, 2))]
    select_n x2, other arithmetic: 0.91 us -> 0.14 us  [the longest x1 0.11 us: shards(): jnp.where(first, jnp.concatenate([mine_samples, other], -1), jnp.concaten...]
    add x3, other arithmetic: 0.26 us -> 0.84 us  [butterfly_sum(): value = value + part]
    pallas_call x1, Pallas kernels: 20.3 us -> 19.8 us  [shards(): pl.pallas_call(kernel, out_shape=jax.ShapeDtypeStruct((slot_count, 2, LB,...]
where the time goes in v10:
time: 43.1 us; the launch traced here: 43 us
  Pallas kernels  19.8 us (46%)
  starting transfers between devices  9.88 us (23%)
  waiting for transfers between devices  5.23 us (12%)
  other arithmetic  4.07 us (9%)
  between operations  2.68 us (6%)
  local copies, waits for them, and re-layouts  1.32 us (3%)
    pallas_call x1, Pallas kernels, shards(): pl.pallas_call(kernel, out_shape=jax.ShapeDtypeStruct((slot_count, 2, LB,...  19.8 us
    ppermute x6, starting transfers between devices, butterfly_sum(): parts.append(lax.ppermute(value, axes, pairs))  9.34 us
    ppermute x6, waiting for transfers between devices, butterfly_sum(): parts.append(lax.ppermute(value, axes, pairs))  2.65 us
    ppermute x1, waiting for transfers between devices, butterfly_sum(): both = lax.ppermute(jnp.concatenate([value, rider], 0), axes, pairs)  2.58 us
    sin x1, other arithmetic, phase_rows(): return (jnp.cos(angle), jnp.sin(angle))  1.3 us
  transfers between devices with their start and end apart: 7, of which 5 were waited for; matrix products, arithmetic and copies ran while one was open for 7% of the time, Pallas kernels for 0%

profile of v10, /device:TPU:0, one launch (start us, length us, event | category | flops | bytes accessed | tf_op | source)
XLA Modules:
  0.0 43.0 jit_solution(3251229058432971278)
XLA Ops:
  0.0 0.0 copy-start.1
  0.0 0.7 %copy-done.1 = s32[4]{0:T(128)S(1)} copy-done((s32[4]{0:T(128)S(1)}, s32[4]{0:T(128)}, u32[]{:S(2)}) %copy-start.1) | copy-done | bytes 40
  0.7 0.8 %fusion.7 = bf16[4,1,2,2048]{3,0,2,1:T(4,128)(2,1)S(1)} fusion(bf16[1,2,4,2048]{3,2,1,0:T(4,128)(2,1)} %param.7, pred[4]{0:T(512)(128)(4,1)S(1)} %broadcast_compare_fusion), kind=kLoop, calls=%fused_computation.19 | loop fusion | flops 16384 | bytes 65540 | tf_op jit(solution)/shard_map/stack | solution.py:164
  1.6 0.0 copy-start
  1.6 0.1 copy.8
  1.6 0.5 %collective-permute-start.1 = (bf16[8,2,2048]{2,1,0:T(2,128)(2,1)S(1)}, bf16[8,2,2048]{2,1,0:T(2,128)(2,1)S(1)}, u32[]{:S(2)}, u32[]{:S(2)}) collective-permute-start(bf16[8,2,2048]{2,1,0:T(2,128)(2,1)S(1)} %bitcast.27), channel_id=1, source_target_pairs={{0,2},{1,3},{2,0},{3,1},{4,6},{5,7},{6,4},{7,5},{8,10},{9,11},{10,... | collective-permute-start | bytes 196616 | tf_op jit(solution)/shard_map/ppermute | solution.py:124
  2.2 2.6 %collective-permute-start.2 = (bf16[8,2,2048]{2,1,0:T(2,128)(2,1)S(1)}, bf16[8,2,2048]{2,1,0:T(2,128)(2,1)S(1)}, u32[]{:S(2)}, u32[]{:S(2)}) collective-permute-start(bf16[8,2,2048]{2,1,0:T(2,128)(2,1)S(1)} %bitcast.28), channel_id=1, source_target_pairs={{0,3},{1,2},{2,1},{3,0},{4,7},{5,6},{6,5},{7,4},{8,11},{9,10},{10,... | collective-permute-start | bytes 196616 | tf_op jit(solution)/shard_map/ppermute | solution.py:124
  4.8 0.0 copy-done
  4.8 0.1 pad_maximum_fusion
  5.0 0.5 %collective-permute-start = (bf16[12,2,2048]{2,1,0:T(2,128)(2,1)S(1)}, bf16[12,2,2048]{2,1,0:T(2,128)(2,1)S(1)}, u32[]{:S(2)}, u32[]{:S(2)}) collective-permute-start(bf16[12,2,2048]{2,1,0:T(2,128)(2,1)S(1)} %pad_maximum_fusion), channel_id=1, source_target_pairs={{0,1},{1,0},{2,3},{3,2},{4,5},{5,4},{6,7},{7,6},{8,9},{9,8},{10,11... | collective-permute-start | bytes 294920 | tf_op jit(solution)/shard_map/ppermute | solution.py:120
  6.8 0.1 pad_add_fusion
  6.9 0.0 collective-permute-done.1
  6.9 0.3 collective-permute-done.2
  7.2 2.6 %collective-permute-done = bf16[12,2,2048]{2,1,0:T(2,128)(2,1)S(1)} collective-permute-done((bf16[12,2,2048]{2,1,0:T(2,128)(2,1)S(1)}, bf16[12,2,2048]{2,1,0:T(2,128)(2,1)S(1)}, u32[]{:S(2)}, u32[]{:S(2)}) %collective-permute-start) | collective-permute-done | bytes 98336 | tf_op jit(solution)/shard_map/ppermute | solution.py:120
  9.8 0.1 fusion.4
  9.9 2.6 %collective-permute-start.5 = (bf16[8,2,2048]{2,1,0:T(2,128)(2,1)S(1)}, bf16[8,2,2048]{2,1,0:T(2,128)(2,1)S(1)}, u32[]{:S(2)}, u32[]{:S(2)}) collective-permute-start(bf16[8,2,2048]{2,1,0:T(2,128)(2,1)S(1)} %fusion.4), channel_id=1, source_target_pairs={{0,12},{1,13},{2,14},{3,15},{4,8},{5,9},{6,10},{7,11},{8,4},{9,5},... | collective-permute-start | bytes 196616 | tf_op jit(solution)/shard_map/ppermute | solution.py:124
  12.5 0.4 %collective-permute-start.4 = (bf16[8,2,2048]{2,1,0:T(2,128)(2,1)S(1)}, bf16[8,2,2048]{2,1,0:T(2,128)(2,1)S(1)}, u32[]{:S(2)}, u32[]{:S(2)}) collective-permute-start(bf16[8,2,2048]{2,1,0:T(2,128)(2,1)S(1)} %fusion.4), channel_id=1, source_target_pairs={{0,8},{1,9},{2,10},{3,11},{4,12},{5,13},{6,14},{7,15},{8,0},{9,1},... | collective-permute-start | bytes 196616 | tf_op jit(solution)/shard_map/ppermute | solution.py:124
  13.0 0.5 %collective-permute-start.3 = (bf16[8,2,2048]{2,1,0:T(2,128)(2,1)S(1)}, bf16[8,2,2048]{2,1,0:T(2,128)(2,1)S(1)}, u32[]{:S(2)}, u32[]{:S(2)}) collective-permute-start(bf16[8,2,2048]{2,1,0:T(2,128)(2,1)S(1)} %fusion.4), channel_id=1, source_target_pairs={{0,4},{1,5},{2,6},{3,7},{4,0},{5,1},{6,2},{7,3},{8,12},{9,13},{10,... | collective-permute-start | bytes 196616 | tf_op jit(solution)/shard_map/ppermute | solution.py:124
  13.5 0.1 broadcast_select_fusion
  13.6 0.5 %slice.15 = bf16[1]{0:T(256)(128)(2,1)} slice(bf16[32768]{0:T(1024)(128)(2,1)S(1)} %bitcast.37), slice={[0:1]} | slice | bytes 4 | tf_op jit(solution)/shard_map/slice | solution.py:128
  15.4 0.7 %pad_convert_fusion.wpad_ref = f32[4,2,5248]{2,1,0:T(2,128)} fusion(bf16[4,2,4096]{2,1,0:T(2,128)(2,1)S(1)} %broadcast_select_fusion), kind=kLoop, calls=%fused_computation.10 | loop fusion | flops 41984 | bytes 233472 | tf_op jit(solution)/shard_map/jit(_pad)/pad | solution.py:177
  16.2 0.0 collective-permute-done.5
  16.2 0.6 %collective-permute-done.4 = bf16[8,2,2048]{2,1,0:T(2,128)(2,1)S(1)} collective-permute-done((bf16[8,2,2048]{2,1,0:T(2,128)(2,1)S(1)}, bf16[8,2,2048]{2,1,0:T(2,128)(2,1)S(1)}, u32[]{:S(2)}, u32[]{:S(2)}) %collective-permute-start.4) | collective-permute-done | bytes 65568 | tf_op jit(solution)/shard_map/ppermute | solution.py:124
  16.8 0.4 %collective-permute-done.3 = bf16[8,2,2048]{2,1,0:T(2,128)(2,1)S(1)} collective-permute-done((bf16[8,2,2048]{2,1,0:T(2,128)(2,1)S(1)}, bf16[8,2,2048]{2,1,0:T(2,128)(2,1)S(1)}, u32[]{:S(2)}, u32[]{:S(2)}) %collective-permute-start.3) | collective-permute-done | bytes 65568 | tf_op jit(solution)/shard_map/ppermute | solution.py:124
  17.2 2.7 %collective-permute-start.6 = (bf16[8,2,2048]{2,1,0:T(2,128)(2,1)S(1)}, bf16[8,2,2048]{2,1,0:T(2,128)(2,1)S(1)}, u32[]{:S(2)}, u32[]{:S(2)}) collective-permute-start(bf16[8,2,2048]{2,1,0:T(2,128)(2,1)S(1)} %bitcast.32), channel_id=1, source_target_pairs={{0,16},{1,17},{2,18},{3,19},{4,20},{5,21},{6,22},{7,23},{8,24},{9,... | collective-permute-start | bytes 196616 | tf_op jit(solution)/shard_map/ppermute | solution.py:124
  19.9 1.3 %fusion.5 = (f32[128,152]{1,0:T(8,128)}, f32[128,152]{1,0:T(8,128)}) fusion(s32[152]{0:T(256)S(1)} %pad_add_fusion, s32[128]{0:T(128)S(1)} %iota_add_fusion), kind=kLoop, calls=%fused_computation.14 | loop fusion | flops 272384 | bytes 156768 | tf_op jit(solution)/shard_map/sin | solution.py:21
  21.2 1.3 %collective-permute-done.6 = bf16[8,2,2048]{2,1,0:T(2,128)(2,1)S(1)} collective-permute-done((bf16[8,2,2048]{2,1,0:T(2,128)(2,1)S(1)}, bf16[8,2,2048]{2,1,0:T(2,128)(2,1)S(1)}, u32[]{:S(2)}, u32[]{:S(2)}) %collective-permute-start.6) | collective-permute-done | bytes 65568 | tf_op jit(solution)/shard_map/ppermute | solution.py:124
  22.5 0.7 %add.58.ref_ref = bf16[8,2,2048]{2,1,0:T(2,128)(2,1)} add(bf16[8,2,2048]{2,1,0:T(2,128)(2,1)S(1)} %bitcast.33, bf16[8,2,2048]{2,1,0:T(2,128)(2,1)S(1)} %collective-permute-done.6) | non-fusion elementwise | flops 32768 | bytes 196608 | tf_op jit(solution)/shard_map/add | solution.py:126
  23.2 19.8 %shard_map.64 = f32[6,2,128,128]{3,2,1,0:T(8,128)} custom-call(s32[6]{0:T(128)} %bitcast.38, s32[1]{0:T(128)S(6)} %copy.13.count_ref, f32[4,2,5248]{2,1,0:T(2,128)} %pad_convert_fusion.wpad_ref, bf16[8,2,2048]{2,1,0:T(2,128)(2,1)} %add.58.ref_ref, f32[128,152]{1,0:T(8,128)} %get-tuple-element.6.cos_ref, f32[128,152]{1,0:T(8,128)} %get-tuple-element.5.sin_ref), custom_call_target="tpu_custom_call" | custom-call | tf_op jit(solution)/shard_map/pallas_call | solution.py:190
  (10 shorter events, 0.1 us)
Async XLA Ops:
  0.0 0.7 %copy-start.1 = (s32[4]{0:T(128)S(1)}, s32[4]{0:T(128)}, u32[]{:S(2)}) copy-start(s32[4]{0:T(128)} %param.8) | copy-start | bytes 52
  1.6 3.2 %copy-start = (bf16[1,2,4,2048]{3,2,1,0:T(4,128)(2,1)S(1)}, bf16[1,2,4,2048]{3,2,1,0:T(4,128)(2,1)}, u32[]{:S(2)}) copy-start(bf16[1,2,4,2048]{3,2,1,0:T(4,128)(2,1)} %param.6) | copy-start | bytes 98308
  1.6 5.2 %collective-permute-start.1 = (bf16[8,2,2048]{2,1,0:T(2,128)(2,1)S(1)}, bf16[8,2,2048]{2,1,0:T(2,128)(2,1)S(1)}, u32[]{:S(2)}, u32[]{:S(2)}) collective-permute-start(bf16[8,2,2048]{2,1,0:T(2,128)(2,1)S(1)} %bitcast.27), channel_id=1, source_target_pairs={{0,2},{1,3},{2,0},{3,1},{4,6},{5,7},{6,4},{7,5},{8,10},{9,11},{10,... | collective-permute-start | bytes 196616 | tf_op jit(solution)/shard_map/ppermute | solution.py:124
  2.2 5.0 %collective-permute-start.2 = (bf16[8,2,2048]{2,1,0:T(2,128)(2,1)S(1)}, bf16[8,2,2048]{2,1,0:T(2,128)(2,1)S(1)}, u32[]{:S(2)}, u32[]{:S(2)}) collective-permute-start(bf16[8,2,2048]{2,1,0:T(2,128)(2,1)S(1)} %bitcast.28), channel_id=1, source_target_pairs={{0,3},{1,2},{2,1},{3,0},{4,7},{5,6},{6,5},{7,4},{8,11},{9,10},{10,... | collective-permute-start | bytes 196616 | tf_op jit(solution)/shard_map/ppermute | solution.py:124
  5.0 4.8 %collective-permute-start = (bf16[12,2,2048]{2,1,0:T(2,128)(2,1)S(1)}, bf16[12,2,2048]{2,1,0:T(2,128)(2,1)S(1)}, u32[]{:S(2)}, u32[]{:S(2)}) collective-permute-start(bf16[12,2,2048]{2,1,0:T(2,128)(2,1)S(1)} %pad_maximum_fusion), channel_id=1, source_target_pairs={{0,1},{1,0},{2,3},{3,2},{4,5},{5,4},{6,7},{7,6},{8,9},{9,8},{10,11... | collective-permute-start | bytes 294920 | tf_op jit(solution)/shard_map/ppermute | solution.py:120
  9.9 6.3 %collective-permute-start.5 = (bf16[8,2,2048]{2,1,0:T(2,128)(2,1)S(1)}, bf16[8,2,2048]{2,1,0:T(2,128)(2,1)S(1)}, u32[]{:S(2)}, u32[]{:S(2)}) collective-permute-start(bf16[8,2,2048]{2,1,0:T(2,128)(2,1)S(1)} %fusion.4), channel_id=1, source_target_pairs={{0,12},{1,13},{2,14},{3,15},{4,8},{5,9},{6,10},{7,11},{8,4},{9,5},... | collective-permute-start | bytes 196616 | tf_op jit(solution)/shard_map/ppermute | solution.py:124
  12.5 4.3 %collective-permute-start.4 = (bf16[8,2,2048]{2,1,0:T(2,128)(2,1)S(1)}, bf16[8,2,2048]{2,1,0:T(2,128)(2,1)S(1)}, u32[]{:S(2)}, u32[]{:S(2)}) collective-permute-start(bf16[8,2,2048]{2,1,0:T(2,128)(2,1)S(1)} %fusion.4), channel_id=1, source_target_pairs={{0,8},{1,9},{2,10},{3,11},{4,12},{5,13},{6,14},{7,15},{8,0},{9,1},... | collective-permute-start | bytes 196616 | tf_op jit(solution)/shard_map/ppermute | solution.py:124
  13.0 4.3 %collective-permute-start.3 = (bf16[8,2,2048]{2,1,0:T(2,128)(2,1)S(1)}, bf16[8,2,2048]{2,1,0:T(2,128)(2,1)S(1)}, u32[]{:S(2)}, u32[]{:S(2)}) collective-permute-start(bf16[8,2,2048]{2,1,0:T(2,128)(2,1)S(1)} %fusion.4), channel_id=1, source_target_pairs={{0,4},{1,5},{2,6},{3,7},{4,0},{5,1},{6,2},{7,3},{8,12},{9,13},{10,... | collective-permute-start | bytes 196616 | tf_op jit(solution)/shard_map/ppermute | solution.py:124
  17.2 5.2 %collective-permute-start.6 = (bf16[8,2,2048]{2,1,0:T(2,128)(2,1)S(1)}, bf16[8,2,2048]{2,1,0:T(2,128)(2,1)S(1)}, u32[]{:S(2)}, u32[]{:S(2)}) collective-permute-start(bf16[8,2,2048]{2,1,0:T(2,128)(2,1)S(1)} %bitcast.32), channel_id=1, source_target_pairs={{0,16},{1,17},{2,18},{3,19},{4,20},{5,21},{6,22},{7,23},{8,24},{9,... | collective-permute-start | bytes 196616 | tf_op jit(solution)/shard_map/ppermute | solution.py:124

commit v11 on v10

--- a/solution.py
+++ b/solution.py
@@ -34,8 +34,10 @@
     return (turn(high) + turn(mid)) + turn(low)
 
 
-def caf_kernel(blocks_ref, count_ref, wpad_ref, ref_ref, cos_ref, sin_ref,
-               out_ref, first_buf, second_buf, acc, bc_ref, bs_ref, *, chunks, slots, span, steps, groups, norm):
+def caf_kernel(blocks_ref, count_ref, wpad_ref, cos_ref, sin_ref, *rest, parts, chunks, slots, span, steps,
+               groups, norm):
+    ref_refs = rest[:parts]
+    out_ref, first_buf, second_buf, acc, bc_ref, bs_ref = rest[parts:]
     def column(ref, lane):
         tail = ref[:, LB:]
         pick = lax.broadcasted_iota(jnp.int32, tail.shape, 1) == lane
@@ -71,7 +73,9 @@
     def one_step(step, cur, nxt, next_step):
         for c in range(chunks):
             g = step * chunks + c
-            rr = ref_ref[g].astype(jnp.float32)
+            rr = ref_refs[0][g].astype(jnp.float32)
+            for extra in ref_refs[1:]:
+                rr = rr + extra[g].astype(jnp.float32)
             r_re = rr[0:1, :]
             r_im = rr[1:2, :]
             a_c = jnp.broadcast_to(column(cos_ref, g), (LB, CHUNK))
@@ -122,13 +126,15 @@
                 carried = both[value.shape[0]:]
             else:
                 parts.append(lax.ppermute(value, axes, pairs))
+        if stride * radix >= count:
+            return [value] + parts, later, carried
         for part in parts:
             value = value + part
         if stride == 1:
             late = (value.reshape(-1)[0] != value.reshape(-1)[0]).astype(jnp.int32)
             later = jax.tree.map(lambda x: x + late.astype(x.dtype), later)
         stride *= radix
-    return value, later, carried
+    return [value], later, carried
 
 
 def seg_join(half, axis):
@@ -163,12 +169,12 @@
         zero = jnp.zeros_like(own)
         placed = jnp.where(first, jnp.stack([own, zero], 1), jnp.stack([zero, own], 1)).reshape(-1, 2, seg_len)
         mine_samples = jnp.transpose(surveillance[0], (1, 0, 2))
-        refrows, (first_bin,), other = butterfly_sum(placed, ("beam", "seg"), (doppler_start[0],), mine_samples)
+        refparts, (first_bin,), other = butterfly_sum(placed, ("beam", "seg"), (doppler_start[0],), mine_samples)
         samples = jnp.where(first, jnp.concatenate([mine_samples, other], -1),
                             jnp.concatenate([other, mine_samples], -1))
     else:
         refs = seg_join(lax.psum(local, "beam"), "seg")
-        refrows = jnp.transpose(refs.reshape(2, step_count * chunks, CHUNK), (1, 0, 2))
+        refparts = [jnp.transpose(refs.reshape(2, step_count * chunks, CHUNK), (1, 0, 2))]
         samples = jnp.transpose(seg_join(surveillance[0], "seg"), (1, 0, 2))
         first_bin = doppler_start[0]
 
@@ -184,7 +190,7 @@
     tables = (cos_rows, sin_rows)
     assert step_count % 2 == 0
     kernel = functools.partial(caf_kernel, chunks=chunks, slots=slot_count, span=span, steps=step_count,
-                               groups=step_count * chunks,
+                               groups=step_count * chunks, parts=len(refparts),
                                norm=1.0 / math.sqrt(window_len))
     full = lambda shape: pl.BlockSpec(shape, lambda k, *_: (0,) * len(shape))
     out = pl.pallas_call(
@@ -193,14 +199,14 @@
         grid_spec=pltpu.PrefetchScalarGridSpec(
             num_scalar_prefetch=2,
             grid=(step_count // 2,),
-            in_specs=[full(wpad.shape), full(refrows.shape)] + [full(t.shape) for t in tables],
+            in_specs=[full(wpad.shape)] + [full(t.shape) for t in tables] + [full(p.shape) for p in refparts],
             out_specs=full((slot_count, 2, LB, bins)),
             scratch_shapes=[pltpu.VMEM((2 * LB, span), jnp.bfloat16), pltpu.VMEM((2 * LB, span), jnp.bfloat16),
                             pltpu.VMEM((slot_count, 2 * LB, 2 * bins), jnp.float32),
                             pltpu.VMEM((bins, CHUNK), jnp.float32), pltpu.VMEM((bins, CHUNK), jnp.float32)],
         ),
         compiler_params=pltpu.CompilerParams(dimension_semantics=("arbitrary",)),
-    )(lag_blocks[0], block_count, wpad, refrows, *tables)
+    )(lag_blocks[0], block_count, wpad, *tables, *refparts)
     return out[None]
 
 

time: 43.1 us -> 43.5 us (level)
  other arithmetic: 4.07 us -> 3.37 us
  local copies, waits for them, and re-layouts: 1.32 us -> 1.94 us
    add x3 -> x2, other arithmetic: 0.84 us -> 0.14 us  [butterfly_sum(): value = value + part]
    unnamed x6 -> x10, local copies, waits for them, and re-layouts: 0.71 us -> 1.33 us
where the time goes in v11:
time: 43.5 us; the launch traced here: 43.3 us
  Pallas kernels  20.2 us (46%)
  starting transfers between devices  9.88 us (23%)
  waiting for transfers between devices  5.22 us (12%)
  other arithmetic  3.37 us (8%)
  between operations  2.69 us (6%)
  local copies, waits for them, and re-layouts  1.94 us (4%)
    pallas_call x1, Pallas kernels, shards(): pl.pallas_call(kernel, out_shape=jax.ShapeDtypeStruct((slot_count, 2, LB,...  20.2 us
    ppermute x6, starting transfers between devices, butterfly_sum(): parts.append(lax.ppermute(value, axes, pairs))  9.34 us
    ppermute x6, waiting for transfers between devices, butterfly_sum(): parts.append(lax.ppermute(value, axes, pairs))  2.64 us
    ppermute x1, waiting for transfers between devices, butterfly_sum(): both = lax.ppermute(jnp.concatenate([value, rider], 0), axes, pairs)  2.58 us
    unnamed x10, local copies, waits for them, and re-layouts  1.33 us
    sin x1, other arithmetic, phase_rows(): return (jnp.cos(angle), jnp.sin(angle))  1.29 us
  transfers between devices with their start and end apart: 7, of which 5 were waited for; matrix products, arithmetic and copies ran while one was open for 7% of the time, Pallas kernels for 0%

profile of v11, /device:TPU:0, one launch (start us, length us, event | category | flops | bytes accessed | tf_op | source)
XLA Modules:
  0.0 43.3 jit_solution(15290791588090655508)
XLA Ops:
  0.0 0.0 copy-start.3
  0.0 0.7 %copy-done.3 = s32[4]{0:T(128)S(1)} copy-done((s32[4]{0:T(128)S(1)}, s32[4]{0:T(128)}, u32[]{:S(2)}) %copy-start.3) | copy-done | bytes 40
  0.7 0.8 %fusion.7 = bf16[4,1,2,2048]{3,0,2,1:T(4,128)(2,1)S(1)} fusion(bf16[1,2,4,2048]{3,2,1,0:T(4,128)(2,1)} %param.7, pred[4]{0:T(512)(128)(4,1)S(1)} %broadcast_compare_fusion), kind=kLoop, calls=%fused_computation.19 | loop fusion | flops 16384 | bytes 65540 | tf_op jit(solution)/shard_map/stack | solution.py:170
  1.6 0.0 copy-start.2
  1.6 0.1 copy.8
  1.6 0.5 %collective-permute-start.1 = (bf16[8,2,2048]{2,1,0:T(2,128)(2,1)S(1)}, bf16[8,2,2048]{2,1,0:T(2,128)(2,1)S(1)}, u32[]{:S(2)}, u32[]{:S(2)}) collective-permute-start(bf16[8,2,2048]{2,1,0:T(2,128)(2,1)S(1)} %bitcast.27), channel_id=1, source_target_pairs={{0,2},{1,3},{2,0},{3,1},{4,6},{5,7},{6,4},{7,5},{8,10},{9,11},{10,... | collective-permute-start | bytes 196616 | tf_op jit(solution)/shard_map/ppermute | solution.py:128
  2.2 2.6 %collective-permute-start.2 = (bf16[8,2,2048]{2,1,0:T(2,128)(2,1)S(1)}, bf16[8,2,2048]{2,1,0:T(2,128)(2,1)S(1)}, u32[]{:S(2)}, u32[]{:S(2)}) collective-permute-start(bf16[8,2,2048]{2,1,0:T(2,128)(2,1)S(1)} %bitcast.28), channel_id=1, source_target_pairs={{0,3},{1,2},{2,1},{3,0},{4,7},{5,6},{6,5},{7,4},{8,11},{9,10},{10,... | collective-permute-start | bytes 196616 | tf_op jit(solution)/shard_map/ppermute | solution.py:128
  4.8 0.0 copy-done.2
  4.8 0.1 pad_maximum_fusion
  5.0 0.5 %collective-permute-start = (bf16[12,2,2048]{2,1,0:T(2,128)(2,1)S(1)}, bf16[12,2,2048]{2,1,0:T(2,128)(2,1)S(1)}, u32[]{:S(2)}, u32[]{:S(2)}) collective-permute-start(bf16[12,2,2048]{2,1,0:T(2,128)(2,1)S(1)} %pad_maximum_fusion), channel_id=1, source_target_pairs={{0,1},{1,0},{2,3},{3,2},{4,5},{5,4},{6,7},{7,6},{8,9},{9,8},{10,11... | collective-permute-start | bytes 294920 | tf_op jit(solution)/shard_map/ppermute | solution.py:124
  6.8 0.1 pad_add_fusion
  6.9 0.0 collective-permute-done.1
  6.9 0.3 collective-permute-done.2
  7.2 2.6 %collective-permute-done = bf16[12,2,2048]{2,1,0:T(2,128)(2,1)S(1)} collective-permute-done((bf16[12,2,2048]{2,1,0:T(2,128)(2,1)S(1)}, bf16[12,2,2048]{2,1,0:T(2,128)(2,1)S(1)}, u32[]{:S(2)}, u32[]{:S(2)}) %collective-permute-start) | collective-permute-done | bytes 98336 | tf_op jit(solution)/shard_map/ppermute | solution.py:124
  9.8 0.1 fusion.4
  9.9 2.6 %collective-permute-start.5 = (bf16[8,2,2048]{2,1,0:T(2,128)(2,1)S(1)}, bf16[8,2,2048]{2,1,0:T(2,128)(2,1)S(1)}, u32[]{:S(2)}, u32[]{:S(2)}) collective-permute-start(bf16[8,2,2048]{2,1,0:T(2,128)(2,1)S(1)} %fusion.4), channel_id=1, source_target_pairs={{0,12},{1,13},{2,14},{3,15},{4,8},{5,9},{6,10},{7,11},{8,4},{9,5},... | collective-permute-start | bytes 196616 | tf_op jit(solution)/shard_map/ppermute | solution.py:128
  12.5 0.4 %collective-permute-start.4 = (bf16[8,2,2048]{2,1,0:T(2,128)(2,1)S(1)}, bf16[8,2,2048]{2,1,0:T(2,128)(2,1)S(1)}, u32[]{:S(2)}, u32[]{:S(2)}) collective-permute-start(bf16[8,2,2048]{2,1,0:T(2,128)(2,1)S(1)} %fusion.4), channel_id=1, source_target_pairs={{0,8},{1,9},{2,10},{3,11},{4,12},{5,13},{6,14},{7,15},{8,0},{9,1},... | collective-permute-start | bytes 196616 | tf_op jit(solution)/shard_map/ppermute | solution.py:128
  13.0 0.5 %collective-permute-start.3 = (bf16[8,2,2048]{2,1,0:T(2,128)(2,1)S(1)}, bf16[8,2,2048]{2,1,0:T(2,128)(2,1)S(1)}, u32[]{:S(2)}, u32[]{:S(2)}) collective-permute-start(bf16[8,2,2048]{2,1,0:T(2,128)(2,1)S(1)} %fusion.4), channel_id=1, source_target_pairs={{0,4},{1,5},{2,6},{3,7},{4,0},{5,1},{6,2},{7,3},{8,12},{9,13},{10,... | collective-permute-start | bytes 196616 | tf_op jit(solution)/shard_map/ppermute | solution.py:128
  13.5 0.1 broadcast_select_fusion
  13.6 0.5 %slice.15 = bf16[1]{0:T(256)(128)(2,1)} slice(bf16[32768]{0:T(1024)(128)(2,1)S(1)} %bitcast.37), slice={[0:1]} | slice | bytes 4 | tf_op jit(solution)/shard_map/slice | solution.py:134
  15.4 0.7 %pad_convert_fusion.wpad_ref = f32[4,2,5248]{2,1,0:T(2,128)} fusion(bf16[4,2,4096]{2,1,0:T(2,128)(2,1)S(1)} %broadcast_select_fusion), kind=kLoop, calls=%fused_computation.10 | loop fusion | flops 41984 | bytes 233472 | tf_op jit(solution)/shard_map/jit(_pad)/pad | solution.py:183
  16.2 0.0 collective-permute-done.5
  16.2 0.6 %collective-permute-done.4 = bf16[8,2,2048]{2,1,0:T(2,128)(2,1)S(1)} collective-permute-done((bf16[8,2,2048]{2,1,0:T(2,128)(2,1)S(1)}, bf16[8,2,2048]{2,1,0:T(2,128)(2,1)S(1)}, u32[]{:S(2)}, u32[]{:S(2)}) %collective-permute-start.4) | collective-permute-done | bytes 65568 | tf_op jit(solution)/shard_map/ppermute | solution.py:128
  16.8 0.4 %collective-permute-done.3 = bf16[8,2,2048]{2,1,0:T(2,128)(2,1)S(1)} collective-permute-done((bf16[8,2,2048]{2,1,0:T(2,128)(2,1)S(1)}, bf16[8,2,2048]{2,1,0:T(2,128)(2,1)S(1)}, u32[]{:S(2)}, u32[]{:S(2)}) %collective-permute-start.3) | collective-permute-done | bytes 65568 | tf_op jit(solution)/shard_map/ppermute | solution.py:128
  17.2 0.0 copy-start
  17.3 2.7 %collective-permute-start.6 = (bf16[8,2,2048]{2,1,0:T(2,128)(2,1)S(1)}, bf16[8,2,2048]{2,1,0:T(2,128)(2,1)S(1)}, u32[]{:S(2)}, u32[]{:S(2)}) collective-permute-start(bf16[8,2,2048]{2,1,0:T(2,128)(2,1)S(1)} %bitcast.32), channel_id=1, source_target_pairs={{0,16},{1,17},{2,18},{3,19},{4,20},{5,21},{6,22},{7,23},{8,24},{9,... | collective-permute-start | bytes 196616 | tf_op jit(solution)/shard_map/ppermute | solution.py:128
  19.9 1.3 %fusion.5 = (f32[128,152]{1,0:T(8,128)}, f32[128,152]{1,0:T(8,128)}) fusion(s32[152]{0:T(256)S(1)} %pad_add_fusion, s32[128]{0:T(128)S(1)} %iota_add_fusion), kind=kLoop, calls=%fused_computation.15 | loop fusion | flops 272384 | bytes 156768 | tf_op jit(solution)/shard_map/sin | solution.py:21
  21.2 0.0 copy-done
  21.2 1.3 %collective-permute-done.6.rest_1_ = bf16[8,2,2048]{2,1,0:T(2,128)(2,1)S(1)} collective-permute-done((bf16[8,2,2048]{2,1,0:T(2,128)(2,1)S(1)}, bf16[8,2,2048]{2,1,0:T(2,128)(2,1)S(1)}, u32[]{:S(2)}, u32[]{:S(2)}) %collective-permute-start.6) | collective-permute-done | bytes 65568 | tf_op jit(solution)/shard_map/ppermute | solution.py:128
  22.5 0.0 copy-start.1
  22.5 0.6 %copy-done.1 = bf16[8,2,2048]{2,1,0:T(2,128)(2,1)} copy-done((bf16[8,2,2048]{2,1,0:T(2,128)(2,1)}, bf16[8,2,2048]{2,1,0:T(2,128)(2,1)S(1)}, u32[]{:S(2)}) %copy-start.1) | copy-done | bytes 65560
  23.1 20.2 %shard_map.64 = f32[6,2,128,128]{3,2,1,0:T(8,128)} custom-call(s32[6]{0:T(128)} %bitcast.38, s32[1]{0:T(128)S(6)} %copy.13.count_ref, f32[4,2,5248]{2,1,0:T(2,128)} %pad_convert_fusion.wpad_ref, f32[128,152]{1,0:T(8,128)} %get-tuple-element.6.cos_ref, f32[128,152]{1,0:T(8,128)} %get-tuple-element.5.sin_ref, bf16[8,2,2048]{2,1,0:T(2,128)(2,1)} %bitcast.33, ...), custom_call_target="tpu_custom_call" | custom-call | tf_op jit(solution)/shard_map/pallas_call | solution.py:196
  (10 shorter events, 0.1 us)
Async XLA Ops:
  0.0 0.7 %copy-start.3 = (s32[4]{0:T(128)S(1)}, s32[4]{0:T(128)}, u32[]{:S(2)}) copy-start(s32[4]{0:T(128)} %param.8) | copy-start | bytes 52
  1.6 3.2 %copy-start.2 = (bf16[1,2,4,2048]{3,2,1,0:T(4,128)(2,1)S(1)}, bf16[1,2,4,2048]{3,2,1,0:T(4,128)(2,1)}, u32[]{:S(2)}) copy-start(bf16[1,2,4,2048]{3,2,1,0:T(4,128)(2,1)} %param.6) | copy-start | bytes 98308
  1.6 5.2 %collective-permute-start.1 = (bf16[8,2,2048]{2,1,0:T(2,128)(2,1)S(1)}, bf16[8,2,2048]{2,1,0:T(2,128)(2,1)S(1)}, u32[]{:S(2)}, u32[]{:S(2)}) collective-permute-start(bf16[8,2,2048]{2,1,0:T(2,128)(2,1)S(1)} %bitcast.27), channel_id=1, source_target_pairs={{0,2},{1,3},{2,0},{3,1},{4,6},{5,7},{6,4},{7,5},{8,10},{9,11},{10,... | collective-permute-start | bytes 196616 | tf_op jit(solution)/shard_map/ppermute | solution.py:128
  2.2 5.0 %collective-permute-start.2 = (bf16[8,2,2048]{2,1,0:T(2,128)(2,1)S(1)}, bf16[8,2,2048]{2,1,0:T(2,128)(2,1)S(1)}, u32[]{:S(2)}, u32[]{:S(2)}) collective-permute-start(bf16[8,2,2048]{2,1,0:T(2,128)(2,1)S(1)} %bitcast.28), channel_id=1, source_target_pairs={{0,3},{1,2},{2,1},{3,0},{4,7},{5,6},{6,5},{7,4},{8,11},{9,10},{10,... | collective-permute-start | bytes 196616 | tf_op jit(solution)/shard_map/ppermute | solution.py:128
  5.0 4.8 %collective-permute-start = (bf16[12,2,2048]{2,1,0:T(2,128)(2,1)S(1)}, bf16[12,2,2048]{2,1,0:T(2,128)(2,1)S(1)}, u32[]{:S(2)}, u32[]{:S(2)}) collective-permute-start(bf16[12,2,2048]{2,1,0:T(2,128)(2,1)S(1)} %pad_maximum_fusion), channel_id=1, source_target_pairs={{0,1},{1,0},{2,3},{3,2},{4,5},{5,4},{6,7},{7,6},{8,9},{9,8},{10,11... | collective-permute-start | bytes 294920 | tf_op jit(solution)/shard_map/ppermute | solution.py:124
  9.9 6.3 %collective-permute-start.5 = (bf16[8,2,2048]{2,1,0:T(2,128)(2,1)S(1)}, bf16[8,2,2048]{2,1,0:T(2,128)(2,1)S(1)}, u32[]{:S(2)}, u32[]{:S(2)}) collective-permute-start(bf16[8,2,2048]{2,1,0:T(2,128)(2,1)S(1)} %fusion.4), channel_id=1, source_target_pairs={{0,12},{1,13},{2,14},{3,15},{4,8},{5,9},{6,10},{7,11},{8,4},{9,5},... | collective-permute-start | bytes 196616 | tf_op jit(solution)/shard_map/ppermute | solution.py:128
  12.5 4.3 %collective-permute-start.4 = (bf16[8,2,2048]{2,1,0:T(2,128)(2,1)S(1)}, bf16[8,2,2048]{2,1,0:T(2,128)(2,1)S(1)}, u32[]{:S(2)}, u32[]{:S(2)}) collective-permute-start(bf16[8,2,2048]{2,1,0:T(2,128)(2,1)S(1)} %fusion.4), channel_id=1, source_target_pairs={{0,8},{1,9},{2,10},{3,11},{4,12},{5,13},{6,14},{7,15},{8,0},{9,1},... | collective-permute-start | bytes 196616 | tf_op jit(solution)/shard_map/ppermute | solution.py:128
  13.0 4.3 %collective-permute-start.3 = (bf16[8,2,2048]{2,1,0:T(2,128)(2,1)S(1)}, bf16[8,2,2048]{2,1,0:T(2,128)(2,1)S(1)}, u32[]{:S(2)}, u32[]{:S(2)}) collective-permute-start(bf16[8,2,2048]{2,1,0:T(2,128)(2,1)S(1)} %fusion.4), channel_id=1, source_target_pairs={{0,4},{1,5},{2,6},{3,7},{4,0},{5,1},{6,2},{7,3},{8,12},{9,13},{10,... | collective-permute-start | bytes 196616 | tf_op jit(solution)/shard_map/ppermute | solution.py:128
  17.2 4.0 %copy-start = (bf16[2,8,2048]{2,1,0:T(8,128)(2,1)}, bf16[2,8,2048]{2,1,0:T(8,128)(2,1)S(1)}, u32[]{:S(2)}) copy-start(bf16[2,8,2048]{2,1,0:T(8,128)(2,1)S(1)} %add_add_fusion) | copy-start | bytes 196612
  17.3 5.2 %collective-permute-start.6 = (bf16[8,2,2048]{2,1,0:T(2,128)(2,1)S(1)}, bf16[8,2,2048]{2,1,0:T(2,128)(2,1)S(1)}, u32[]{:S(2)}, u32[]{:S(2)}) collective-permute-start(bf16[8,2,2048]{2,1,0:T(2,128)(2,1)S(1)} %bitcast.32), channel_id=1, source_target_pairs={{0,16},{1,17},{2,18},{3,19},{4,20},{5,21},{6,22},{7,23},{8,24},{9,... | collective-permute-start | bytes 196616 | tf_op jit(solution)/shard_map/ppermute | solution.py:128
  22.5 0.6 %copy-start.1 = (bf16[8,2,2048]{2,1,0:T(2,128)(2,1)}, bf16[8,2,2048]{2,1,0:T(2,128)(2,1)S(1)}, u32[]{:S(2)}) copy-start(bf16[8,2,2048]{2,1,0:T(2,128)(2,1)S(1)} %collective-permute-done.6.rest_1_) | copy-start | bytes 196612

commit v12 on v11

--- a/solution.py
+++ b/solution.py
@@ -55,6 +55,10 @@
         rolled = pltpu.roll(tile, lanes - LB + 1, 1, stride=1, stride_axis=0)
         dst[comp * LB:(comp + 1) * LB, v0:v0 + PIECE] = rolled[:, :PIECE].astype(jnp.bfloat16)
 
+    early = -(-(CHUNK + span - CHUNK * chunks - LB) // PIECE)
+    head = [(comp, i) for comp, i in pieces if i < early]
+    tail = [(comp, i) for comp, i in pieces if i >= early]
+
     @pl.when(pair == 0)
     def _():
         acc[...] = jnp.zeros_like(acc)
@@ -65,12 +69,12 @@
             h_s = jnp.broadcast_to(column(sin_ref, groups + i), (LB, LB))
             bc_ref[:, i * LB:(i + 1) * LB] = h_c * l_c - h_s * l_s
             bs_ref[:, i * LB:(i + 1) * LB] = h_s * l_c + h_c * l_s
-        for comp, i in pieces:
+        for comp, i in head:
             build_piece(0, comp, i, first_buf)
 
     offsets = [jnp.maximum(blocks_ref[q], 0) * LB for q in range(slots)]
 
-    def one_step(step, cur, nxt, next_step):
+    def one_step(step, cur, nxt, next_step, fill=()):
         for c in range(chunks):
             g = step * chunks + c
             rr = ref_refs[0][g].astype(jnp.float32)
@@ -92,11 +96,14 @@
                 hank = cur[:, pl.ds(off, CHUNK)]
                 acc[q] += lax.dot_general(hank, coef, (((1,), (1,)), ((), ())),
                                           preferred_element_type=jnp.float32)
+            if c == 0:
+                for comp, i in fill:
+                    build_piece(step, comp, i, cur)
             for comp, i in pieces[c * share:(c + 1) * share]:
                 build_piece(next_step, comp, i, nxt)
 
     step = 2 * pair
-    one_step(step, first_buf, second_buf, step + 1)
+    one_step(step, first_buf, second_buf, step + 1, tail)
     one_step(step + 1, second_buf, first_buf, jnp.minimum(step + 2, steps - 1))
 
     @pl.when(pair == pl.num_programs(0) - 1)

time: 43.5 us -> 43.5 us (level)
  no operation moved by 1% of the time
where the time goes in v12:
time: 43.5 us; the launch traced here: 43.7 us
  Pallas kernels  20.5 us (47%)
  starting transfers between devices  9.88 us (23%)
  waiting for transfers between devices  5.22 us (12%)
  other arithmetic  3.37 us (8%)
  between operations  2.69 us (6%)
  local copies, waits for them, and re-layouts  1.94 us (4%)
    pallas_call x1, Pallas kernels, shards(): pl.pallas_call(kernel, out_shape=jax.ShapeDtypeStruct((slot_count, 2, LB,...  20.5 us
    ppermute x6, starting transfers between devices, butterfly_sum(): parts.append(lax.ppermute(value, axes, pairs))  9.34 us
    ppermute x6, waiting for transfers between devices, butterfly_sum(): parts.append(lax.ppermute(value, axes, pairs))  2.64 us
    ppermute x1, waiting for transfers between devices, butterfly_sum(): both = lax.ppermute(jnp.concatenate([value, rider], 0), axes, pairs)  2.58 us
    unnamed x10, local copies, waits for them, and re-layouts  1.33 us
    sin x1, other arithmetic, phase_rows(): return (jnp.cos(angle), jnp.sin(angle))  1.29 us
  transfers between devices with their start and end apart: 7, of which 5 were waited for; matrix products, arithmetic and copies ran while one was open for 7% of the time, Pallas kernels for 0%

profile of v12, /device:TPU:0, one launch (start us, length us, event | category | flops | bytes accessed | tf_op | source)
XLA Modules:
  0.0 43.7 jit_solution(12289693326514961031)
XLA Ops:
  0.0 0.0 copy-start.3
  0.0 0.7 %copy-done.3 = s32[4]{0:T(128)S(1)} copy-done((s32[4]{0:T(128)S(1)}, s32[4]{0:T(128)}, u32[]{:S(2)}) %copy-start.3) | copy-done | bytes 40
  0.7 0.8 %fusion.7 = bf16[4,1,2,2048]{3,0,2,1:T(4,128)(2,1)S(1)} fusion(bf16[1,2,4,2048]{3,2,1,0:T(4,128)(2,1)} %param.7, pred[4]{0:T(512)(128)(4,1)S(1)} %broadcast_compare_fusion), kind=kLoop, calls=%fused_computation.19 | loop fusion | flops 16384 | bytes 65540 | tf_op jit(solution)/shard_map/stack | solution.py:177
  1.6 0.0 copy-start.2
  1.6 0.1 copy.8
  1.6 0.5 %collective-permute-start.1 = (bf16[8,2,2048]{2,1,0:T(2,128)(2,1)S(1)}, bf16[8,2,2048]{2,1,0:T(2,128)(2,1)S(1)}, u32[]{:S(2)}, u32[]{:S(2)}) collective-permute-start(bf16[8,2,2048]{2,1,0:T(2,128)(2,1)S(1)} %bitcast.27), channel_id=1, source_target_pairs={{0,2},{1,3},{2,0},{3,1},{4,6},{5,7},{6,4},{7,5},{8,10},{9,11},{10,... | collective-permute-start | bytes 196616 | tf_op jit(solution)/shard_map/ppermute | solution.py:135
  2.2 2.6 %collective-permute-start.2 = (bf16[8,2,2048]{2,1,0:T(2,128)(2,1)S(1)}, bf16[8,2,2048]{2,1,0:T(2,128)(2,1)S(1)}, u32[]{:S(2)}, u32[]{:S(2)}) collective-permute-start(bf16[8,2,2048]{2,1,0:T(2,128)(2,1)S(1)} %bitcast.28), channel_id=1, source_target_pairs={{0,3},{1,2},{2,1},{3,0},{4,7},{5,6},{6,5},{7,4},{8,11},{9,10},{10,... | collective-permute-start | bytes 196616 | tf_op jit(solution)/shard_map/ppermute | solution.py:135
  4.8 0.0 copy-done.2
  4.8 0.1 pad_maximum_fusion
  5.0 0.5 %collective-permute-start = (bf16[12,2,2048]{2,1,0:T(2,128)(2,1)S(1)}, bf16[12,2,2048]{2,1,0:T(2,128)(2,1)S(1)}, u32[]{:S(2)}, u32[]{:S(2)}) collective-permute-start(bf16[12,2,2048]{2,1,0:T(2,128)(2,1)S(1)} %pad_maximum_fusion), channel_id=1, source_target_pairs={{0,1},{1,0},{2,3},{3,2},{4,5},{5,4},{6,7},{7,6},{8,9},{9,8},{10,11... | collective-permute-start | bytes 294920 | tf_op jit(solution)/shard_map/ppermute | solution.py:131
  6.8 0.1 pad_add_fusion
  6.9 0.0 collective-permute-done.1
  6.9 0.3 collective-permute-done.2
  7.2 2.6 %collective-permute-done = bf16[12,2,2048]{2,1,0:T(2,128)(2,1)S(1)} collective-permute-done((bf16[12,2,2048]{2,1,0:T(2,128)(2,1)S(1)}, bf16[12,2,2048]{2,1,0:T(2,128)(2,1)S(1)}, u32[]{:S(2)}, u32[]{:S(2)}) %collective-permute-start) | collective-permute-done | bytes 98336 | tf_op jit(solution)/shard_map/ppermute | solution.py:131
  9.8 0.1 fusion.4
  9.9 2.6 %collective-permute-start.5 = (bf16[8,2,2048]{2,1,0:T(2,128)(2,1)S(1)}, bf16[8,2,2048]{2,1,0:T(2,128)(2,1)S(1)}, u32[]{:S(2)}, u32[]{:S(2)}) collective-permute-start(bf16[8,2,2048]{2,1,0:T(2,128)(2,1)S(1)} %fusion.4), channel_id=1, source_target_pairs={{0,12},{1,13},{2,14},{3,15},{4,8},{5,9},{6,10},{7,11},{8,4},{9,5},... | collective-permute-start | bytes 196616 | tf_op jit(solution)/shard_map/ppermute | solution.py:135
  12.5 0.4 %collective-permute-start.4 = (bf16[8,2,2048]{2,1,0:T(2,128)(2,1)S(1)}, bf16[8,2,2048]{2,1,0:T(2,128)(2,1)S(1)}, u32[]{:S(2)}, u32[]{:S(2)}) collective-permute-start(bf16[8,2,2048]{2,1,0:T(2,128)(2,1)S(1)} %fusion.4), channel_id=1, source_target_pairs={{0,8},{1,9},{2,10},{3,11},{4,12},{5,13},{6,14},{7,15},{8,0},{9,1},... | collective-permute-start | bytes 196616 | tf_op jit(solution)/shard_map/ppermute | solution.py:135
  13.0 0.5 %collective-permute-start.3 = (bf16[8,2,2048]{2,1,0:T(2,128)(2,1)S(1)}, bf16[8,2,2048]{2,1,0:T(2,128)(2,1)S(1)}, u32[]{:S(2)}, u32[]{:S(2)}) collective-permute-start(bf16[8,2,2048]{2,1,0:T(2,128)(2,1)S(1)} %fusion.4), channel_id=1, source_target_pairs={{0,4},{1,5},{2,6},{3,7},{4,0},{5,1},{6,2},{7,3},{8,12},{9,13},{10,... | collective-permute-start | bytes 196616 | tf_op jit(solution)/shard_map/ppermute | solution.py:135
  13.5 0.1 broadcast_select_fusion
  13.6 0.5 %slice.15 = bf16[1]{0:T(256)(128)(2,1)} slice(bf16[32768]{0:T(1024)(128)(2,1)S(1)} %bitcast.37), slice={[0:1]} | slice | bytes 4 | tf_op jit(solution)/shard_map/slice | solution.py:141
  15.4 0.7 %pad_convert_fusion.wpad_ref = f32[4,2,5248]{2,1,0:T(2,128)} fusion(bf16[4,2,4096]{2,1,0:T(2,128)(2,1)S(1)} %broadcast_select_fusion), kind=kLoop, calls=%fused_computation.10 | loop fusion | flops 41984 | bytes 233472 | tf_op jit(solution)/shard_map/jit(_pad)/pad | solution.py:190
  16.2 0.0 collective-permute-done.5
  16.2 0.6 %collective-permute-done.4 = bf16[8,2,2048]{2,1,0:T(2,128)(2,1)S(1)} collective-permute-done((bf16[8,2,2048]{2,1,0:T(2,128)(2,1)S(1)}, bf16[8,2,2048]{2,1,0:T(2,128)(2,1)S(1)}, u32[]{:S(2)}, u32[]{:S(2)}) %collective-permute-start.4) | collective-permute-done | bytes 65568 | tf_op jit(solution)/shard_map/ppermute | solution.py:135
  16.8 0.4 %collective-permute-done.3 = bf16[8,2,2048]{2,1,0:T(2,128)(2,1)S(1)} collective-permute-done((bf16[8,2,2048]{2,1,0:T(2,128)(2,1)S(1)}, bf16[8,2,2048]{2,1,0:T(2,128)(2,1)S(1)}, u32[]{:S(2)}, u32[]{:S(2)}) %collective-permute-start.3) | collective-permute-done | bytes 65568 | tf_op jit(solution)/shard_map/ppermute | solution.py:135
  17.2 0.0 copy-start
  17.3 2.7 %collective-permute-start.6 = (bf16[8,2,2048]{2,1,0:T(2,128)(2,1)S(1)}, bf16[8,2,2048]{2,1,0:T(2,128)(2,1)S(1)}, u32[]{:S(2)}, u32[]{:S(2)}) collective-permute-start(bf16[8,2,2048]{2,1,0:T(2,128)(2,1)S(1)} %bitcast.32), channel_id=1, source_target_pairs={{0,16},{1,17},{2,18},{3,19},{4,20},{5,21},{6,22},{7,23},{8,24},{9,... | collective-permute-start | bytes 196616 | tf_op jit(solution)/shard_map/ppermute | solution.py:135
  19.9 1.3 %fusion.5 = (f32[128,152]{1,0:T(8,128)}, f32[128,152]{1,0:T(8,128)}) fusion(s32[152]{0:T(256)S(1)} %pad_add_fusion, s32[128]{0:T(128)S(1)} %iota_add_fusion), kind=kLoop, calls=%fused_computation.15 | loop fusion | flops 272384 | bytes 156768 | tf_op jit(solution)/shard_map/sin | solution.py:21
  21.2 0.0 copy-done
  21.2 1.3 %collective-permute-done.6.rest_1_ = bf16[8,2,2048]{2,1,0:T(2,128)(2,1)S(1)} collective-permute-done((bf16[8,2,2048]{2,1,0:T(2,128)(2,1)S(1)}, bf16[8,2,2048]{2,1,0:T(2,128)(2,1)S(1)}, u32[]{:S(2)}, u32[]{:S(2)}) %collective-permute-start.6) | collective-permute-done | bytes 65568 | tf_op jit(solution)/shard_map/ppermute | solution.py:135
  22.5 0.0 copy-start.1
  22.5 0.6 %copy-done.1 = bf16[8,2,2048]{2,1,0:T(2,128)(2,1)} copy-done((bf16[8,2,2048]{2,1,0:T(2,128)(2,1)}, bf16[8,2,2048]{2,1,0:T(2,128)(2,1)S(1)}, u32[]{:S(2)}) %copy-start.1) | copy-done | bytes 65560
  23.1 20.5 %shard_map.64 = f32[6,2,128,128]{3,2,1,0:T(8,128)} custom-call(s32[6]{0:T(128)} %bitcast.38, s32[1]{0:T(128)S(6)} %copy.13.count_ref, f32[4,2,5248]{2,1,0:T(2,128)} %pad_convert_fusion.wpad_ref, f32[128,152]{1,0:T(8,128)} %get-tuple-element.6.cos_ref, f32[128,152]{1,0:T(8,128)} %get-tuple-element.5.sin_ref, bf16[8,2,2048]{2,1,0:T(2,128)(2,1)} %bitcast.33, ...), custom_call_target="tpu_custom_call" | custom-call | tf_op jit(solution)/shard_map/pallas_call | solution.py:203
  (10 shorter events, 0.1 us)
Async XLA Ops:
  0.0 0.7 %copy-start.3 = (s32[4]{0:T(128)S(1)}, s32[4]{0:T(128)}, u32[]{:S(2)}) copy-start(s32[4]{0:T(128)} %param.8) | copy-start | bytes 52
  1.6 3.2 %copy-start.2 = (bf16[1,2,4,2048]{3,2,1,0:T(4,128)(2,1)S(1)}, bf16[1,2,4,2048]{3,2,1,0:T(4,128)(2,1)}, u32[]{:S(2)}) copy-start(bf16[1,2,4,2048]{3,2,1,0:T(4,128)(2,1)} %param.6) | copy-start | bytes 98308
  1.6 5.2 %collective-permute-start.1 = (bf16[8,2,2048]{2,1,0:T(2,128)(2,1)S(1)}, bf16[8,2,2048]{2,1,0:T(2,128)(2,1)S(1)}, u32[]{:S(2)}, u32[]{:S(2)}) collective-permute-start(bf16[8,2,2048]{2,1,0:T(2,128)(2,1)S(1)} %bitcast.27), channel_id=1, source_target_pairs={{0,2},{1,3},{2,0},{3,1},{4,6},{5,7},{6,4},{7,5},{8,10},{9,11},{10,... | collective-permute-start | bytes 196616 | tf_op jit(solution)/shard_map/ppermute | solution.py:135
  2.2 5.0 %collective-permute-start.2 = (bf16[8,2,2048]{2,1,0:T(2,128)(2,1)S(1)}, bf16[8,2,2048]{2,1,0:T(2,128)(2,1)S(1)}, u32[]{:S(2)}, u32[]{:S(2)}) collective-permute-start(bf16[8,2,2048]{2,1,0:T(2,128)(2,1)S(1)} %bitcast.28), channel_id=1, source_target_pairs={{0,3},{1,2},{2,1},{3,0},{4,7},{5,6},{6,5},{7,4},{8,11},{9,10},{10,... | collective-permute-start | bytes 196616 | tf_op jit(solution)/shard_map/ppermute | solution.py:135
  5.0 4.8 %collective-permute-start = (bf16[12,2,2048]{2,1,0:T(2,128)(2,1)S(1)}, bf16[12,2,2048]{2,1,0:T(2,128)(2,1)S(1)}, u32[]{:S(2)}, u32[]{:S(2)}) collective-permute-start(bf16[12,2,2048]{2,1,0:T(2,128)(2,1)S(1)} %pad_maximum_fusion), channel_id=1, source_target_pairs={{0,1},{1,0},{2,3},{3,2},{4,5},{5,4},{6,7},{7,6},{8,9},{9,8},{10,11... | collective-permute-start | bytes 294920 | tf_op jit(solution)/shard_map/ppermute | solution.py:131
  9.9 6.3 %collective-permute-start.5 = (bf16[8,2,2048]{2,1,0:T(2,128)(2,1)S(1)}, bf16[8,2,2048]{2,1,0:T(2,128)(2,1)S(1)}, u32[]{:S(2)}, u32[]{:S(2)}) collective-permute-start(bf16[8,2,2048]{2,1,0:T(2,128)(2,1)S(1)} %fusion.4), channel_id=1, source_target_pairs={{0,12},{1,13},{2,14},{3,15},{4,8},{5,9},{6,10},{7,11},{8,4},{9,5},... | collective-permute-start | bytes 196616 | tf_op jit(solution)/shard_map/ppermute | solution.py:135
  12.5 4.3 %collective-permute-start.4 = (bf16[8,2,2048]{2,1,0:T(2,128)(2,1)S(1)}, bf16[8,2,2048]{2,1,0:T(2,128)(2,1)S(1)}, u32[]{:S(2)}, u32[]{:S(2)}) collective-permute-start(bf16[8,2,2048]{2,1,0:T(2,128)(2,1)S(1)} %fusion.4), channel_id=1, source_target_pairs={{0,8},{1,9},{2,10},{3,11},{4,12},{5,13},{6,14},{7,15},{8,0},{9,1},... | collective-permute-start | bytes 196616 | tf_op jit(solution)/shard_map/ppermute | solution.py:135
  13.0 4.3 %collective-permute-start.3 = (bf16[8,2,2048]{2,1,0:T(2,128)(2,1)S(1)}, bf16[8,2,2048]{2,1,0:T(2,128)(2,1)S(1)}, u32[]{:S(2)}, u32[]{:S(2)}) collective-permute-start(bf16[8,2,2048]{2,1,0:T(2,128)(2,1)S(1)} %fusion.4), channel_id=1, source_target_pairs={{0,4},{1,5},{2,6},{3,7},{4,0},{5,1},{6,2},{7,3},{8,12},{9,13},{10,... | collective-permute-start | bytes 196616 | tf_op jit(solution)/shard_map/ppermute | solution.py:135
  17.2 4.0 %copy-start = (bf16[2,8,2048]{2,1,0:T(8,128)(2,1)}, bf16[2,8,2048]{2,1,0:T(8,128)(2,1)S(1)}, u32[]{:S(2)}) copy-start(bf16[2,8,2048]{2,1,0:T(8,128)(2,1)S(1)} %add_add_fusion) | copy-start | bytes 196612
  17.3 5.2 %collective-permute-start.6 = (bf16[8,2,2048]{2,1,0:T(2,128)(2,1)S(1)}, bf16[8,2,2048]{2,1,0:T(2,128)(2,1)S(1)}, u32[]{:S(2)}, u32[]{:S(2)}) collective-permute-start(bf16[8,2,2048]{2,1,0:T(2,128)(2,1)S(1)} %bitcast.32), channel_id=1, source_target_pairs={{0,16},{1,17},{2,18},{3,19},{4,20},{5,21},{6,22},{7,23},{8,24},{9,... | collective-permute-start | bytes 196616 | tf_op jit(solution)/shard_map/ppermute | solution.py:135
  22.5 0.6 %copy-start.1 = (bf16[8,2,2048]{2,1,0:T(2,128)(2,1)}, bf16[8,2,2048]{2,1,0:T(2,128)(2,1)S(1)}, u32[]{:S(2)}) copy-start(bf16[8,2,2048]{2,1,0:T(2,128)(2,1)S(1)} %collective-permute-done.6.rest_1_) | copy-start | bytes 196612

commit v13 on v11

--- a/solution.py
+++ b/solution.py
@@ -12,7 +12,6 @@
 NLB = 8
 DOP = 256
 CHUNK = 2048
-PIECE = 1024
 
 
 def phase_rows(freqs, times, window_len):
@@ -44,16 +43,17 @@
         return jnp.sum(jnp.where(pick, tail, 0.0), axis=1, keepdims=True)
 
     pair = pl.program_id(0)
-    lanes = PIECE + LB
-    pieces = [(comp, i) for comp in range(2) for i in range(span // PIECE)]
+    piece = span
+    lanes = piece + LB
+    pieces = [(comp, i) for comp in range(2) for i in range(span // piece)]
     share = -(-len(pieces) // chunks)
 
     def build_piece(step, comp, i, dst):
-        v0 = i * PIECE
+        v0 = i * piece
         win = wpad_ref[step, comp:comp + 1, v0:v0 + lanes]
         tile = jnp.broadcast_to(win, (LB, lanes))
         rolled = pltpu.roll(tile, lanes - LB + 1, 1, stride=1, stride_axis=0)
-        dst[comp * LB:(comp + 1) * LB, v0:v0 + PIECE] = rolled[:, :PIECE].astype(jnp.bfloat16)
+        dst[comp * LB:(comp + 1) * LB, v0:v0 + piece] = rolled[:, :piece].astype(jnp.bfloat16)
 
     @pl.when(pair == 0)
     def _():

time: 43.5 us -> 43.4 us (level)
  no operation moved by 1% of the time
where the time goes in v13:
time: 43.4 us; the launch traced here: 42.9 us
  Pallas kernels  19.8 us (46%)
  starting transfers between devices  9.88 us (23%)
  waiting for transfers between devices  5.22 us (12%)
  other arithmetic  3.37 us (8%)
  between operations  2.69 us (6%)
  local copies, waits for them, and re-layouts  1.94 us (4%)
    pallas_call x1, Pallas kernels, shards(): pl.pallas_call(kernel, out_shape=jax.ShapeDtypeStruct((slot_count, 2, LB,...  19.8 us
    ppermute x6, starting transfers between devices, butterfly_sum(): parts.append(lax.ppermute(value, axes, pairs))  9.34 us
    ppermute x6, waiting for transfers between devices, butterfly_sum(): parts.append(lax.ppermute(value, axes, pairs))  2.64 us
    ppermute x1, waiting for transfers between devices, butterfly_sum(): both = lax.ppermute(jnp.concatenate([value, rider], 0), axes, pairs)  2.58 us
    unnamed x10, local copies, waits for them, and re-layouts  1.33 us
    sin x1, other arithmetic, phase_rows(): return (jnp.cos(angle), jnp.sin(angle))  1.29 us
  transfers between devices with their start and end apart: 7, of which 5 were waited for; matrix products, arithmetic and copies ran while one was open for 7% of the time, Pallas kernels for 0%

profile of v13, /device:TPU:0, one launch (start us, length us, event | category | flops | bytes accessed | tf_op | source)
XLA Modules:
  0.0 42.9 jit_solution(11826112269376373174)
XLA Ops:
  0.0 0.0 copy-start.3
  0.0 0.7 %copy-done.3 = s32[4]{0:T(128)S(1)} copy-done((s32[4]{0:T(128)S(1)}, s32[4]{0:T(128)}, u32[]{:S(2)}) %copy-start.3) | copy-done | bytes 40
  0.7 0.8 %fusion.7 = bf16[4,1,2,2048]{3,0,2,1:T(4,128)(2,1)S(1)} fusion(bf16[1,2,4,2048]{3,2,1,0:T(4,128)(2,1)} %param.7, pred[4]{0:T(512)(128)(4,1)S(1)} %broadcast_compare_fusion), kind=kLoop, calls=%fused_computation.19 | loop fusion | flops 16384 | bytes 65540 | tf_op jit(solution)/shard_map/stack | solution.py:170
  1.6 0.0 copy-start.2
  1.6 0.1 copy.8
  1.6 0.5 %collective-permute-start.1 = (bf16[8,2,2048]{2,1,0:T(2,128)(2,1)S(1)}, bf16[8,2,2048]{2,1,0:T(2,128)(2,1)S(1)}, u32[]{:S(2)}, u32[]{:S(2)}) collective-permute-start(bf16[8,2,2048]{2,1,0:T(2,128)(2,1)S(1)} %bitcast.27), channel_id=1, source_target_pairs={{0,2},{1,3},{2,0},{3,1},{4,6},{5,7},{6,4},{7,5},{8,10},{9,11},{10,... | collective-permute-start | bytes 196616 | tf_op jit(solution)/shard_map/ppermute | solution.py:128
  2.2 2.6 %collective-permute-start.2 = (bf16[8,2,2048]{2,1,0:T(2,128)(2,1)S(1)}, bf16[8,2,2048]{2,1,0:T(2,128)(2,1)S(1)}, u32[]{:S(2)}, u32[]{:S(2)}) collective-permute-start(bf16[8,2,2048]{2,1,0:T(2,128)(2,1)S(1)} %bitcast.28), channel_id=1, source_target_pairs={{0,3},{1,2},{2,1},{3,0},{4,7},{5,6},{6,5},{7,4},{8,11},{9,10},{10,... | collective-permute-start | bytes 196616 | tf_op jit(solution)/shard_map/ppermute | solution.py:128
  4.8 0.0 copy-done.2
  4.8 0.1 pad_maximum_fusion
  5.0 0.5 %collective-permute-start = (bf16[12,2,2048]{2,1,0:T(2,128)(2,1)S(1)}, bf16[12,2,2048]{2,1,0:T(2,128)(2,1)S(1)}, u32[]{:S(2)}, u32[]{:S(2)}) collective-permute-start(bf16[12,2,2048]{2,1,0:T(2,128)(2,1)S(1)} %pad_maximum_fusion), channel_id=1, source_target_pairs={{0,1},{1,0},{2,3},{3,2},{4,5},{5,4},{6,7},{7,6},{8,9},{9,8},{10,11... | collective-permute-start | bytes 294920 | tf_op jit(solution)/shard_map/ppermute | solution.py:124
  6.8 0.1 pad_add_fusion
  6.9 0.0 collective-permute-done.1
  6.9 0.3 collective-permute-done.2
  7.2 2.6 %collective-permute-done = bf16[12,2,2048]{2,1,0:T(2,128)(2,1)S(1)} collective-permute-done((bf16[12,2,2048]{2,1,0:T(2,128)(2,1)S(1)}, bf16[12,2,2048]{2,1,0:T(2,128)(2,1)S(1)}, u32[]{:S(2)}, u32[]{:S(2)}) %collective-permute-start) | collective-permute-done | bytes 98336 | tf_op jit(solution)/shard_map/ppermute | solution.py:124
  9.8 0.1 fusion.4
  9.9 2.6 %collective-permute-start.5 = (bf16[8,2,2048]{2,1,0:T(2,128)(2,1)S(1)}, bf16[8,2,2048]{2,1,0:T(2,128)(2,1)S(1)}, u32[]{:S(2)}, u32[]{:S(2)}) collective-permute-start(bf16[8,2,2048]{2,1,0:T(2,128)(2,1)S(1)} %fusion.4), channel_id=1, source_target_pairs={{0,12},{1,13},{2,14},{3,15},{4,8},{5,9},{6,10},{7,11},{8,4},{9,5},... | collective-permute-start | bytes 196616 | tf_op jit(solution)/shard_map/ppermute | solution.py:128
  12.5 0.4 %collective-permute-start.4 = (bf16[8,2,2048]{2,1,0:T(2,128)(2,1)S(1)}, bf16[8,2,2048]{2,1,0:T(2,128)(2,1)S(1)}, u32[]{:S(2)}, u32[]{:S(2)}) collective-permute-start(bf16[8,2,2048]{2,1,0:T(2,128)(2,1)S(1)} %fusion.4), channel_id=1, source_target_pairs={{0,8},{1,9},{2,10},{3,11},{4,12},{5,13},{6,14},{7,15},{8,0},{9,1},... | collective-permute-start | bytes 196616 | tf_op jit(solution)/shard_map/ppermute | solution.py:128
  13.0 0.5 %collective-permute-start.3 = (bf16[8,2,2048]{2,1,0:T(2,128)(2,1)S(1)}, bf16[8,2,2048]{2,1,0:T(2,128)(2,1)S(1)}, u32[]{:S(2)}, u32[]{:S(2)}) collective-permute-start(bf16[8,2,2048]{2,1,0:T(2,128)(2,1)S(1)} %fusion.4), channel_id=1, source_target_pairs={{0,4},{1,5},{2,6},{3,7},{4,0},{5,1},{6,2},{7,3},{8,12},{9,13},{10,... | collective-permute-start | bytes 196616 | tf_op jit(solution)/shard_map/ppermute | solution.py:128
  13.5 0.1 broadcast_select_fusion
  13.6 0.5 %slice.15 = bf16[1]{0:T(256)(128)(2,1)} slice(bf16[32768]{0:T(1024)(128)(2,1)S(1)} %bitcast.37), slice={[0:1]} | slice | bytes 4 | tf_op jit(solution)/shard_map/slice | solution.py:134
  15.4 0.7 %pad_convert_fusion.wpad_ref = f32[4,2,5248]{2,1,0:T(2,128)} fusion(bf16[4,2,4096]{2,1,0:T(2,128)(2,1)S(1)} %broadcast_select_fusion), kind=kLoop, calls=%fused_computation.10 | loop fusion | flops 41984 | bytes 233472 | tf_op jit(solution)/shard_map/jit(_pad)/pad | solution.py:183
  16.2 0.0 collective-permute-done.5
  16.2 0.6 %collective-permute-done.4 = bf16[8,2,2048]{2,1,0:T(2,128)(2,1)S(1)} collective-permute-done((bf16[8,2,2048]{2,1,0:T(2,128)(2,1)S(1)}, bf16[8,2,2048]{2,1,0:T(2,128)(2,1)S(1)}, u32[]{:S(2)}, u32[]{:S(2)}) %collective-permute-start.4) | collective-permute-done | bytes 65568 | tf_op jit(solution)/shard_map/ppermute | solution.py:128
  16.8 0.4 %collective-permute-done.3 = bf16[8,2,2048]{2,1,0:T(2,128)(2,1)S(1)} collective-permute-done((bf16[8,2,2048]{2,1,0:T(2,128)(2,1)S(1)}, bf16[8,2,2048]{2,1,0:T(2,128)(2,1)S(1)}, u32[]{:S(2)}, u32[]{:S(2)}) %collective-permute-start.3) | collective-permute-done | bytes 65568 | tf_op jit(solution)/shard_map/ppermute | solution.py:128
  17.2 0.0 copy-start
  17.3 2.7 %collective-permute-start.6 = (bf16[8,2,2048]{2,1,0:T(2,128)(2,1)S(1)}, bf16[8,2,2048]{2,1,0:T(2,128)(2,1)S(1)}, u32[]{:S(2)}, u32[]{:S(2)}) collective-permute-start(bf16[8,2,2048]{2,1,0:T(2,128)(2,1)S(1)} %bitcast.32), channel_id=1, source_target_pairs={{0,16},{1,17},{2,18},{3,19},{4,20},{5,21},{6,22},{7,23},{8,24},{9,... | collective-permute-start | bytes 196616 | tf_op jit(solution)/shard_map/ppermute | solution.py:128
  19.9 1.3 %fusion.5 = (f32[128,152]{1,0:T(8,128)}, f32[128,152]{1,0:T(8,128)}) fusion(s32[152]{0:T(256)S(1)} %pad_add_fusion, s32[128]{0:T(128)S(1)} %iota_add_fusion), kind=kLoop, calls=%fused_computation.15 | loop fusion | flops 272384 | bytes 156768 | tf_op jit(solution)/shard_map/sin | solution.py:20
  21.2 0.0 copy-done
  21.2 1.3 %collective-permute-done.6.rest_1_ = bf16[8,2,2048]{2,1,0:T(2,128)(2,1)S(1)} collective-permute-done((bf16[8,2,2048]{2,1,0:T(2,128)(2,1)S(1)}, bf16[8,2,2048]{2,1,0:T(2,128)(2,1)S(1)}, u32[]{:S(2)}, u32[]{:S(2)}) %collective-permute-start.6) | collective-permute-done | bytes 65568 | tf_op jit(solution)/shard_map/ppermute | solution.py:128
  22.5 0.0 copy-start.1
  22.5 0.6 %copy-done.1 = bf16[8,2,2048]{2,1,0:T(2,128)(2,1)} copy-done((bf16[8,2,2048]{2,1,0:T(2,128)(2,1)}, bf16[8,2,2048]{2,1,0:T(2,128)(2,1)S(1)}, u32[]{:S(2)}) %copy-start.1) | copy-done | bytes 65560
  23.1 19.8 %shard_map.64 = f32[6,2,128,128]{3,2,1,0:T(8,128)} custom-call(s32[6]{0:T(128)} %bitcast.38, s32[1]{0:T(128)S(6)} %copy.13.count_ref, f32[4,2,5248]{2,1,0:T(2,128)} %pad_convert_fusion.wpad_ref, f32[128,152]{1,0:T(8,128)} %get-tuple-element.6.cos_ref, f32[128,152]{1,0:T(8,128)} %get-tuple-element.5.sin_ref, bf16[8,2,2048]{2,1,0:T(2,128)(2,1)} %bitcast.33, ...), custom_call_target="tpu_custom_call" | custom-call | tf_op jit(solution)/shard_map/pallas_call | solution.py:196
  (10 shorter events, 0.1 us)
Async XLA Ops:
  0.0 0.7 %copy-start.3 = (s32[4]{0:T(128)S(1)}, s32[4]{0:T(128)}, u32[]{:S(2)}) copy-start(s32[4]{0:T(128)} %param.8) | copy-start | bytes 52
  1.6 3.2 %copy-start.2 = (bf16[1,2,4,2048]{3,2,1,0:T(4,128)(2,1)S(1)}, bf16[1,2,4,2048]{3,2,1,0:T(4,128)(2,1)}, u32[]{:S(2)}) copy-start(bf16[1,2,4,2048]{3,2,1,0:T(4,128)(2,1)} %param.6) | copy-start | bytes 98308
  1.6 5.2 %collective-permute-start.1 = (bf16[8,2,2048]{2,1,0:T(2,128)(2,1)S(1)}, bf16[8,2,2048]{2,1,0:T(2,128)(2,1)S(1)}, u32[]{:S(2)}, u32[]{:S(2)}) collective-permute-start(bf16[8,2,2048]{2,1,0:T(2,128)(2,1)S(1)} %bitcast.27), channel_id=1, source_target_pairs={{0,2},{1,3},{2,0},{3,1},{4,6},{5,7},{6,4},{7,5},{8,10},{9,11},{10,... | collective-permute-start | bytes 196616 | tf_op jit(solution)/shard_map/ppermute | solution.py:128
  2.2 5.0 %collective-permute-start.2 = (bf16[8,2,2048]{2,1,0:T(2,128)(2,1)S(1)}, bf16[8,2,2048]{2,1,0:T(2,128)(2,1)S(1)}, u32[]{:S(2)}, u32[]{:S(2)}) collective-permute-start(bf16[8,2,2048]{2,1,0:T(2,128)(2,1)S(1)} %bitcast.28), channel_id=1, source_target_pairs={{0,3},{1,2},{2,1},{3,0},{4,7},{5,6},{6,5},{7,4},{8,11},{9,10},{10,... | collective-permute-start | bytes 196616 | tf_op jit(solution)/shard_map/ppermute | solution.py:128
  5.0 4.8 %collective-permute-start = (bf16[12,2,2048]{2,1,0:T(2,128)(2,1)S(1)}, bf16[12,2,2048]{2,1,0:T(2,128)(2,1)S(1)}, u32[]{:S(2)}, u32[]{:S(2)}) collective-permute-start(bf16[12,2,2048]{2,1,0:T(2,128)(2,1)S(1)} %pad_maximum_fusion), channel_id=1, source_target_pairs={{0,1},{1,0},{2,3},{3,2},{4,5},{5,4},{6,7},{7,6},{8,9},{9,8},{10,11... | collective-permute-start | bytes 294920 | tf_op jit(solution)/shard_map/ppermute | solution.py:124
  9.9 6.3 %collective-permute-start.5 = (bf16[8,2,2048]{2,1,0:T(2,128)(2,1)S(1)}, bf16[8,2,2048]{2,1,0:T(2,128)(2,1)S(1)}, u32[]{:S(2)}, u32[]{:S(2)}) collective-permute-start(bf16[8,2,2048]{2,1,0:T(2,128)(2,1)S(1)} %fusion.4), channel_id=1, source_target_pairs={{0,12},{1,13},{2,14},{3,15},{4,8},{5,9},{6,10},{7,11},{8,4},{9,5},... | collective-permute-start | bytes 196616 | tf_op jit(solution)/shard_map/ppermute | solution.py:128
  12.5 4.3 %collective-permute-start.4 = (bf16[8,2,2048]{2,1,0:T(2,128)(2,1)S(1)}, bf16[8,2,2048]{2,1,0:T(2,128)(2,1)S(1)}, u32[]{:S(2)}, u32[]{:S(2)}) collective-permute-start(bf16[8,2,2048]{2,1,0:T(2,128)(2,1)S(1)} %fusion.4), channel_id=1, source_target_pairs={{0,8},{1,9},{2,10},{3,11},{4,12},{5,13},{6,14},{7,15},{8,0},{9,1},... | collective-permute-start | bytes 196616 | tf_op jit(solution)/shard_map/ppermute | solution.py:128
  13.0 4.3 %collective-permute-start.3 = (bf16[8,2,2048]{2,1,0:T(2,128)(2,1)S(1)}, bf16[8,2,2048]{2,1,0:T(2,128)(2,1)S(1)}, u32[]{:S(2)}, u32[]{:S(2)}) collective-permute-start(bf16[8,2,2048]{2,1,0:T(2,128)(2,1)S(1)} %fusion.4), channel_id=1, source_target_pairs={{0,4},{1,5},{2,6},{3,7},{4,0},{5,1},{6,2},{7,3},{8,12},{9,13},{10,... | collective-permute-start | bytes 196616 | tf_op jit(solution)/shard_map/ppermute | solution.py:128
  17.2 4.0 %copy-start = (bf16[2,8,2048]{2,1,0:T(8,128)(2,1)}, bf16[2,8,2048]{2,1,0:T(8,128)(2,1)S(1)}, u32[]{:S(2)}) copy-start(bf16[2,8,2048]{2,1,0:T(8,128)(2,1)S(1)} %add_add_fusion) | copy-start | bytes 196612
  17.3 5.2 %collective-permute-start.6 = (bf16[8,2,2048]{2,1,0:T(2,128)(2,1)S(1)}, bf16[8,2,2048]{2,1,0:T(2,128)(2,1)S(1)}, u32[]{:S(2)}, u32[]{:S(2)}) collective-permute-start(bf16[8,2,2048]{2,1,0:T(2,128)(2,1)S(1)} %bitcast.32), channel_id=1, source_target_pairs={{0,16},{1,17},{2,18},{3,19},{4,20},{5,21},{6,22},{7,23},{8,24},{9,... | collective-permute-start | bytes 196616 | tf_op jit(solution)/shard_map/ppermute | solution.py:128
  22.5 0.6 %copy-start.1 = (bf16[8,2,2048]{2,1,0:T(2,128)(2,1)}, bf16[8,2,2048]{2,1,0:T(2,128)(2,1)S(1)}, u32[]{:S(2)}) copy-start(bf16[8,2,2048]{2,1,0:T(2,128)(2,1)S(1)} %collective-permute-done.6.rest_1_) | copy-start | bytes 196612

commit v14 on v13

--- a/solution.py
+++ b/solution.py
@@ -11,7 +11,7 @@
 LB = 128
 NLB = 8
 DOP = 256
-CHUNK = 2048
+CHUNK = 4096
 
 
 def phase_rows(freqs, times, window_len):
@@ -121,9 +121,10 @@
         for m in range(1, radix):
             pairs = [(i, i ^ (m * stride)) for i in range(count)]
             if stride == 1 and m == 1 and rider is not None:
-                both = lax.ppermute(jnp.concatenate([value, rider], 0), axes, pairs)
-                parts.append(both[:value.shape[0]])
-                carried = both[value.shape[0]:]
+                axis = -1 if value.shape[:-1] == rider.shape[:-1] else 0
+                both = lax.ppermute(jnp.concatenate([value, rider], axis), axes, pairs)
+                parts.append(lax.slice_in_dim(both, 0, value.shape[axis], axis=axis))
+                carried = lax.slice_in_dim(both, value.shape[axis], both.shape[axis], axis=axis)
             else:
                 parts.append(lax.ppermute(value, axes, pairs))
         if stride * radix >= count:
@@ -163,11 +164,12 @@
     mine = (owner_index == beam_place)[None, :, None]
     local = jnp.where(mine, reference_blocks[0], jnp.zeros_like(reference_blocks[0]))
     group = lax.axis_size(("beam", "seg"))
-    if segments == 2 and group >= 4 and not group & (group - 1) and seg_len == CHUNK:
+    if segments == 2 and group >= 4 and not group & (group - 1):
         first = seg_place == 0
         own = jnp.transpose(local, (1, 0, 2))
         zero = jnp.zeros_like(own)
-        placed = jnp.where(first, jnp.stack([own, zero], 1), jnp.stack([zero, own], 1)).reshape(-1, 2, seg_len)
+        placed = jnp.where(first, jnp.concatenate([own, zero], -1), jnp.concatenate([zero, own], -1))
+        placed = jnp.transpose(placed.reshape(step_count, 2, chunks, CHUNK), (0, 2, 1, 3)).reshape(-1, 2, CHUNK)
         mine_samples = jnp.transpose(surveillance[0], (1, 0, 2))
         refparts, (first_bin,), other = butterfly_sum(placed, ("beam", "seg"), (doppler_start[0],), mine_samples)
         samples = jnp.where(first, jnp.concatenate([mine_samples, other], -1),

time: 43.4 us -> 43.6 us (level)
  Pallas kernels: 19.8 us -> 20.5 us
    transpose x0 -> x1, other arithmetic: none -> 0.85 us  [shards(): own = jnp.transpose(local, (1, 0, 2))]
    another operation x1 -> x0, other arithmetic: 0.84 us -> none  [shards(): jnp.stack([own, zero], 1)]
    pallas_call x1, Pallas kernels: 19.8 us -> 20.5 us  [shards(): pl.pallas_call(kernel, out_shape=jax.ShapeDtypeStruct((slot_count, 2, LB,...]
where the time goes in v14:
time: 43.6 us; the launch traced here: 43.5 us
  Pallas kernels  20.5 us (47%)
  starting transfers between devices  9.89 us (23%)
  waiting for transfers between devices  5.21 us (12%)
  other arithmetic  3.41 us (8%)
  between operations  2.69 us (6%)
  local copies, waits for them, and re-layouts  1.88 us (4%)
    pallas_call x1, Pallas kernels, shards(): pl.pallas_call(kernel, out_shape=jax.ShapeDtypeStruct((slot_count, 2, LB,...  20.5 us
    ppermute x6, starting transfers between devices, butterfly_sum(): parts.append(lax.ppermute(value, axes, pairs))  9.34 us
    ppermute x6, waiting for transfers between devices, butterfly_sum(): parts.append(lax.ppermute(value, axes, pairs))  2.67 us
    ppermute x1, waiting for transfers between devices, butterfly_sum(): both = lax.ppermute(jnp.concatenate([value, rider], axis), axes, pairs)  2.54 us
    unnamed x10, local copies, waits for them, and re-layouts  1.33 us
    sin x1, other arithmetic, phase_rows(): return (jnp.cos(angle), jnp.sin(angle))  1.29 us
  transfers between devices with their start and end apart: 7, of which 5 were waited for; matrix products, arithmetic and copies ran while one was open for 7% of the time, Pallas kernels for 0%

profile of v14, /device:TPU:0, one launch (start us, length us, event | category | flops | bytes accessed | tf_op | source)
XLA Modules:
  0.0 43.5 jit_solution(8006419466161338627)
XLA Ops:
  0.0 0.0 copy-start.3
  0.0 0.7 %copy-done.3 = s32[4]{0:T(128)S(1)} copy-done((s32[4]{0:T(128)S(1)}, s32[4]{0:T(128)}, u32[]{:S(2)}) %copy-start.3) | copy-done | bytes 40
  0.7 0.9 %fusion.7 = bf16[4,2,2048]{2,1,0:T(2,128)(2,1)S(1)} fusion(bf16[1,2,4,2048]{3,2,1,0:T(4,128)(2,1)} %param.7, pred[4]{0:T(512)(128)(4,1)S(1)} %broadcast_compare_fusion), kind=kLoop, calls=%fused_computation.20 | loop fusion | flops 16384 | bytes 65540 | tf_op jit(solution)/shard_map/transpose | solution.py:169
  1.5 0.0 copy-start.2
  1.5 0.1 broadcast_select_fusion.1
  1.6 0.5 %collective-permute-start.1 = (bf16[4,2,4096]{2,1,0:T(2,128)(2,1)S(1)}, bf16[4,2,4096]{2,1,0:T(2,128)(2,1)S(1)}, u32[]{:S(2)}, u32[]{:S(2)}) collective-permute-start(bf16[4,2,4096]{2,1,0:T(2,128)(2,1)S(1)} %broadcast_select_fusion.1), channel_id=1, source_target_pairs={{0,2},{1,3},{2,0},{3,1},{4,6},{5,7},{6,4},{7,5},{8,10},{9,11},{10,... | collective-permute-start | bytes 196616 | tf_op jit(solution)/shard_map/ppermute | solution.py:129
  2.1 2.6 %collective-permute-start.2 = (bf16[4,2,4096]{2,1,0:T(2,128)(2,1)S(1)}, bf16[4,2,4096]{2,1,0:T(2,128)(2,1)S(1)}, u32[]{:S(2)}, u32[]{:S(2)}) collective-permute-start(bf16[4,2,4096]{2,1,0:T(2,128)(2,1)S(1)} %broadcast_select_fusion.1), channel_id=1, source_target_pairs={{0,3},{1,2},{2,1},{3,0},{4,7},{5,6},{6,5},{7,4},{8,11},{9,10},{10,... | collective-permute-start | bytes 196616 | tf_op jit(solution)/shard_map/ppermute | solution.py:129
  4.7 0.0 copy-done.2
  4.8 0.1 pad_maximum_fusion
  4.9 0.6 %collective-permute-start = (bf16[4,2,6144]{2,1,0:T(2,128)(2,1)S(1)}, bf16[4,2,6144]{2,1,0:T(2,128)(2,1)S(1)}, u32[]{:S(2)}, u32[]{:S(2)}) collective-permute-start(bf16[4,2,6144]{2,1,0:T(2,128)(2,1)S(1)} %pad_maximum_fusion), channel_id=1, source_target_pairs={{0,1},{1,0},{2,3},{3,2},{4,5},{5,4},{6,7},{7,6},{8,9},{9,8},{10,11... | collective-permute-start | bytes 294920 | tf_op jit(solution)/shard_map/ppermute | solution.py:125
  6.7 0.1 pad_add_fusion
  6.8 0.0 collective-permute-done.1
  6.8 0.3 collective-permute-done.2
  7.2 2.5 %collective-permute-done = bf16[4,2,6144]{2,1,0:T(2,128)(2,1)S(1)} collective-permute-done((bf16[4,2,6144]{2,1,0:T(2,128)(2,1)S(1)}, bf16[4,2,6144]{2,1,0:T(2,128)(2,1)S(1)}, u32[]{:S(2)}, u32[]{:S(2)}) %collective-permute-start) | collective-permute-done | bytes 98336 | tf_op jit(solution)/shard_map/ppermute | solution.py:125
  9.7 0.2 fusion.4
  9.9 2.6 %collective-permute-start.5 = (bf16[4,2,4096]{2,1,0:T(2,128)(2,1)S(1)}, bf16[4,2,4096]{2,1,0:T(2,128)(2,1)S(1)}, u32[]{:S(2)}, u32[]{:S(2)}) collective-permute-start(bf16[4,2,4096]{2,1,0:T(2,128)(2,1)S(1)} %fusion.4), channel_id=1, source_target_pairs={{0,12},{1,13},{2,14},{3,15},{4,8},{5,9},{6,10},{7,11},{8,4},{9,5},... | collective-permute-start | bytes 196616 | tf_op jit(solution)/shard_map/ppermute | solution.py:129
  12.5 0.4 %collective-permute-start.4 = (bf16[4,2,4096]{2,1,0:T(2,128)(2,1)S(1)}, bf16[4,2,4096]{2,1,0:T(2,128)(2,1)S(1)}, u32[]{:S(2)}, u32[]{:S(2)}) collective-permute-start(bf16[4,2,4096]{2,1,0:T(2,128)(2,1)S(1)} %fusion.4), channel_id=1, source_target_pairs={{0,8},{1,9},{2,10},{3,11},{4,12},{5,13},{6,14},{7,15},{8,0},{9,1},... | collective-permute-start | bytes 196616 | tf_op jit(solution)/shard_map/ppermute | solution.py:129
  12.9 0.5 %collective-permute-start.3 = (bf16[4,2,4096]{2,1,0:T(2,128)(2,1)S(1)}, bf16[4,2,4096]{2,1,0:T(2,128)(2,1)S(1)}, u32[]{:S(2)}, u32[]{:S(2)}) collective-permute-start(bf16[4,2,4096]{2,1,0:T(2,128)(2,1)S(1)} %fusion.4), channel_id=1, source_target_pairs={{0,4},{1,5},{2,6},{3,7},{4,0},{5,1},{6,2},{7,3},{8,12},{9,13},{10,... | collective-permute-start | bytes 196616 | tf_op jit(solution)/shard_map/ppermute | solution.py:129
  13.5 0.1 broadcast_select_fusion
  13.6 0.5 %slice.15 = bf16[1]{0:T(256)(128)(2,1)} slice(bf16[32768]{0:T(1024)(128)(2,1)S(1)} %bitcast.30), slice={[0:1]} | slice | bytes 4 | tf_op jit(solution)/shard_map/slice | solution.py:135
  15.4 0.7 %pad_convert_fusion.wpad_ref = f32[4,2,5248]{2,1,0:T(2,128)} fusion(bf16[4,2,4096]{2,1,0:T(2,128)(2,1)S(1)} %broadcast_select_fusion), kind=kLoop, calls=%fused_computation.11 | loop fusion | flops 41984 | bytes 233472 | tf_op jit(solution)/shard_map/jit(_pad)/pad | solution.py:185
  16.1 0.0 collective-permute-done.5
  16.1 0.6 %collective-permute-done.4 = bf16[4,2,4096]{2,1,0:T(2,128)(2,1)S(1)} collective-permute-done((bf16[4,2,4096]{2,1,0:T(2,128)(2,1)S(1)}, bf16[4,2,4096]{2,1,0:T(2,128)(2,1)S(1)}, u32[]{:S(2)}, u32[]{:S(2)}) %collective-permute-start.4) | collective-permute-done | bytes 65568 | tf_op jit(solution)/shard_map/ppermute | solution.py:129
  16.7 0.4 %collective-permute-done.3 = bf16[4,2,4096]{2,1,0:T(2,128)(2,1)S(1)} collective-permute-done((bf16[4,2,4096]{2,1,0:T(2,128)(2,1)S(1)}, bf16[4,2,4096]{2,1,0:T(2,128)(2,1)S(1)}, u32[]{:S(2)}, u32[]{:S(2)}) %collective-permute-start.3) | collective-permute-done | bytes 65568 | tf_op jit(solution)/shard_map/ppermute | solution.py:129
  17.2 0.0 copy-start
  17.2 2.7 %collective-permute-start.6 = (bf16[4,2,4096]{2,1,0:T(2,128)(2,1)S(1)}, bf16[4,2,4096]{2,1,0:T(2,128)(2,1)S(1)}, u32[]{:S(2)}, u32[]{:S(2)}) collective-permute-start(bf16[4,2,4096]{2,1,0:T(2,128)(2,1)S(1)} %bitcast.25), channel_id=1, source_target_pairs={{0,16},{1,17},{2,18},{3,19},{4,20},{5,21},{6,22},{7,23},{8,24},{9,... | collective-permute-start | bytes 196616 | tf_op jit(solution)/shard_map/ppermute | solution.py:129
  19.9 1.3 %fusion.5 = (f32[128,164]{1,0:T(8,128)}, f32[128,164]{1,0:T(8,128)}) fusion(s32[164]{0:T(256)S(1)} %pad_add_fusion, s32[128]{0:T(128)S(1)} %iota_add_fusion), kind=kLoop, calls=%fused_computation.16 | loop fusion | flops 293888 | bytes 169104 | tf_op jit(solution)/shard_map/sin | solution.py:20
  21.2 0.0 copy-done
  21.2 1.3 %collective-permute-done.6.rest_1_ = bf16[4,2,4096]{2,1,0:T(2,128)(2,1)S(1)} collective-permute-done((bf16[4,2,4096]{2,1,0:T(2,128)(2,1)S(1)}, bf16[4,2,4096]{2,1,0:T(2,128)(2,1)S(1)}, u32[]{:S(2)}, u32[]{:S(2)}) %collective-permute-start.6) | collective-permute-done | bytes 65568 | tf_op jit(solution)/shard_map/ppermute | solution.py:129
  22.4 0.0 copy-start.1
  22.5 0.6 %copy-done.1 = bf16[4,2,4096]{2,1,0:T(2,128)(2,1)} copy-done((bf16[4,2,4096]{2,1,0:T(2,128)(2,1)}, bf16[4,2,4096]{2,1,0:T(2,128)(2,1)S(1)}, u32[]{:S(2)}) %copy-start.1) | copy-done | bytes 65560
  23.1 20.5 %shard_map.64 = f32[6,2,128,128]{3,2,1,0:T(8,128)} custom-call(s32[6]{0:T(128)} %bitcast.31, s32[1]{0:T(128)S(6)} %copy.16.count_ref, f32[4,2,5248]{2,1,0:T(2,128)} %pad_convert_fusion.wpad_ref, f32[128,164]{1,0:T(8,128)} %get-tuple-element.6.cos_ref, f32[128,164]{1,0:T(8,128)} %get-tuple-element.5.sin_ref, bf16[4,2,4096]{2,1,0:T(2,128)(2,1)} %bitcast.26, ...), custom_call_target="tpu_custom_call" | custom-call | tf_op jit(solution)/shard_map/pallas_call | solution.py:198
  (9 shorter events, 0.1 us)
Async XLA Ops:
  0.0 0.7 %copy-start.3 = (s32[4]{0:T(128)S(1)}, s32[4]{0:T(128)}, u32[]{:S(2)}) copy-start(s32[4]{0:T(128)} %param.8) | copy-start | bytes 52
  1.5 3.2 %copy-start.2 = (bf16[1,2,4,2048]{3,2,1,0:T(4,128)(2,1)S(1)}, bf16[1,2,4,2048]{3,2,1,0:T(4,128)(2,1)}, u32[]{:S(2)}) copy-start(bf16[1,2,4,2048]{3,2,1,0:T(4,128)(2,1)} %param.6) | copy-start | bytes 98308
  1.6 5.2 %collective-permute-start.1 = (bf16[4,2,4096]{2,1,0:T(2,128)(2,1)S(1)}, bf16[4,2,4096]{2,1,0:T(2,128)(2,1)S(1)}, u32[]{:S(2)}, u32[]{:S(2)}) collective-permute-start(bf16[4,2,4096]{2,1,0:T(2,128)(2,1)S(1)} %broadcast_select_fusion.1), channel_id=1, source_target_pairs={{0,2},{1,3},{2,0},{3,1},{4,6},{5,7},{6,4},{7,5},{8,10},{9,11},{10,... | collective-permute-start | bytes 196616 | tf_op jit(solution)/shard_map/ppermute | solution.py:129
  2.1 5.0 %collective-permute-start.2 = (bf16[4,2,4096]{2,1,0:T(2,128)(2,1)S(1)}, bf16[4,2,4096]{2,1,0:T(2,128)(2,1)S(1)}, u32[]{:S(2)}, u32[]{:S(2)}) collective-permute-start(bf16[4,2,4096]{2,1,0:T(2,128)(2,1)S(1)} %broadcast_select_fusion.1), channel_id=1, source_target_pairs={{0,3},{1,2},{2,1},{3,0},{4,7},{5,6},{6,5},{7,4},{8,11},{9,10},{10,... | collective-permute-start | bytes 196616 | tf_op jit(solution)/shard_map/ppermute | solution.py:129
  4.9 4.8 %collective-permute-start = (bf16[4,2,6144]{2,1,0:T(2,128)(2,1)S(1)}, bf16[4,2,6144]{2,1,0:T(2,128)(2,1)S(1)}, u32[]{:S(2)}, u32[]{:S(2)}) collective-permute-start(bf16[4,2,6144]{2,1,0:T(2,128)(2,1)S(1)} %pad_maximum_fusion), channel_id=1, source_target_pairs={{0,1},{1,0},{2,3},{3,2},{4,5},{5,4},{6,7},{7,6},{8,9},{9,8},{10,11... | collective-permute-start | bytes 294920 | tf_op jit(solution)/shard_map/ppermute | solution.py:125
  9.9 6.3 %collective-permute-start.5 = (bf16[4,2,4096]{2,1,0:T(2,128)(2,1)S(1)}, bf16[4,2,4096]{2,1,0:T(2,128)(2,1)S(1)}, u32[]{:S(2)}, u32[]{:S(2)}) collective-permute-start(bf16[4,2,4096]{2,1,0:T(2,128)(2,1)S(1)} %fusion.4), channel_id=1, source_target_pairs={{0,12},{1,13},{2,14},{3,15},{4,8},{5,9},{6,10},{7,11},{8,4},{9,5},... | collective-permute-start | bytes 196616 | tf_op jit(solution)/shard_map/ppermute | solution.py:129
  12.5 4.3 %collective-permute-start.4 = (bf16[4,2,4096]{2,1,0:T(2,128)(2,1)S(1)}, bf16[4,2,4096]{2,1,0:T(2,128)(2,1)S(1)}, u32[]{:S(2)}, u32[]{:S(2)}) collective-permute-start(bf16[4,2,4096]{2,1,0:T(2,128)(2,1)S(1)} %fusion.4), channel_id=1, source_target_pairs={{0,8},{1,9},{2,10},{3,11},{4,12},{5,13},{6,14},{7,15},{8,0},{9,1},... | collective-permute-start | bytes 196616 | tf_op jit(solution)/shard_map/ppermute | solution.py:129
  12.9 4.3 %collective-permute-start.3 = (bf16[4,2,4096]{2,1,0:T(2,128)(2,1)S(1)}, bf16[4,2,4096]{2,1,0:T(2,128)(2,1)S(1)}, u32[]{:S(2)}, u32[]{:S(2)}) collective-permute-start(bf16[4,2,4096]{2,1,0:T(2,128)(2,1)S(1)} %fusion.4), channel_id=1, source_target_pairs={{0,4},{1,5},{2,6},{3,7},{4,0},{5,1},{6,2},{7,3},{8,12},{9,13},{10,... | collective-permute-start | bytes 196616 | tf_op jit(solution)/shard_map/ppermute | solution.py:129
  17.2 4.0 %copy-start = (bf16[1,8,4096]{2,1,0:T(8,128)(2,1)}, bf16[1,8,4096]{2,1,0:T(8,128)(2,1)S(1)}, u32[]{:S(2)}) copy-start(bf16[1,8,4096]{2,1,0:T(8,128)(2,1)S(1)} %add_add_fusion) | copy-start | bytes 196612
  17.2 5.2 %collective-permute-start.6 = (bf16[4,2,4096]{2,1,0:T(2,128)(2,1)S(1)}, bf16[4,2,4096]{2,1,0:T(2,128)(2,1)S(1)}, u32[]{:S(2)}, u32[]{:S(2)}) collective-permute-start(bf16[4,2,4096]{2,1,0:T(2,128)(2,1)S(1)} %bitcast.25), channel_id=1, source_target_pairs={{0,16},{1,17},{2,18},{3,19},{4,20},{5,21},{6,22},{7,23},{8,24},{9,... | collective-permute-start | bytes 196616 | tf_op jit(solution)/shard_map/ppermute | solution.py:129
  22.4 0.6 %copy-start.1 = (bf16[4,2,4096]{2,1,0:T(2,128)(2,1)}, bf16[4,2,4096]{2,1,0:T(2,128)(2,1)S(1)}, u32[]{:S(2)}) copy-start(bf16[4,2,4096]{2,1,0:T(2,128)(2,1)S(1)} %collective-permute-done.6.rest_1_) | copy-start | bytes 196612

commit v15 on v11

--- a/solution.py
+++ b/solution.py
@@ -160,7 +160,7 @@
     bins = DOP // segments
     chunks = step_len // CHUNK
 
-    mine = (owner_index == beam_place)[None, :, None]
+    mine = jnp.stack([owner_index[k] == beam_place for k in range(step_count)])[None, :, None]
     local = jnp.where(mine, reference_blocks[0], jnp.zeros_like(reference_blocks[0]))
     group = lax.axis_size(("beam", "seg"))
     if segments == 2 and group >= 4 and not group & (group - 1) and seg_len == CHUNK:

time: 43.5 us -> 46 us (1.057)
  between operations: 2.69 us -> 5.17 us
  local copies, waits for them, and re-layouts: 1.94 us -> 2.74 us
  other arithmetic: 3.37 us -> 2.7 us
    slice x0 -> x1, local copies, waits for them, and re-layouts: none -> 1.45 us  [shards(): owner_index[k] == beam_place]
    another operation x1, other arithmetic: 0.84 us -> 0.09 us  [shards(): jnp.stack([own, zero], 1)]
    unnamed x10, local copies, waits for them, and re-layouts: 1.33 us -> 0.68 us
  transfers between devices with their start and end apart: 7 -> 7, of which waited for: 5 -> 5; matrix products, arithmetic and copies ran while one was open for 7% -> 6% of each run, Pallas kernels for 0% -> 0%
where the time goes in v15:
time: 46 us; the launch traced here: 45.6 us
  Pallas kernels  19.9 us (43%)
  starting transfers between devices  9.88 us (21%)
  waiting for transfers between devices  5.21 us (11%)
  between operations  5.17 us (11%)
  local copies, waits for them, and re-layouts  2.74 us (6%)
  other arithmetic  2.7 us (6%)
    pallas_call x1, Pallas kernels, shards(): pl.pallas_call(kernel, out_shape=jax.ShapeDtypeStruct((slot_count, 2, LB,...  19.9 us
    ppermute x6, starting transfers between devices, butterfly_sum(): parts.append(lax.ppermute(value, axes, pairs))  9.34 us
    ppermute x6, waiting for transfers between devices, butterfly_sum(): parts.append(lax.ppermute(value, axes, pairs))  2.62 us
    ppermute x1, waiting for transfers between devices, butterfly_sum(): both = lax.ppermute(jnp.concatenate([value, rider], 0), axes, pairs)  2.58 us
    slice x1, local copies, waits for them, and re-layouts, shards(): owner_index[k] == beam_place  1.45 us
    sin x1, other arithmetic, phase_rows(): return (jnp.cos(angle), jnp.sin(angle))  1.29 us
  transfers between devices with their start and end apart: 7, of which 5 were waited for; matrix products, arithmetic and copies ran while one was open for 6% of the time, Pallas kernels for 0%

profile of v15, /device:TPU:0, one launch (start us, length us, event | category | flops | bytes accessed | tf_op | source)
XLA Modules:
  0.0 45.6 jit_solution(10770170650323891437)
XLA Ops:
  0.0 0.0 copy-start.2
  0.0 1.5 %fusion.8 = (s32[1]{0:T(128)}, s32[1]{0:T(128)}, s32[1]{0:T(128)}, s32[1]{0:T(128)}) fusion(s32[4]{0:T(128)} %param.8), kind=kLoop, calls=%fused_computation.26 | loop fusion | bytes 32 | tf_op jit(solution)/shard_map/slice | solution.py:163
  3.9 0.1 pad_add_fusion
  4.0 0.0 copy-done.2
  4.0 0.1 fusion.7
  4.1 0.0 copy-start.3
  4.2 0.1 copy.8
  4.2 0.5 %collective-permute-start.1 = (bf16[8,2,2048]{2,1,0:T(2,128)(2,1)S(1)}, bf16[8,2,2048]{2,1,0:T(2,128)(2,1)S(1)}, u32[]{:S(2)}, u32[]{:S(2)}) collective-permute-start(bf16[8,2,2048]{2,1,0:T(2,128)(2,1)S(1)} %bitcast.35), channel_id=1, source_target_pairs={{0,2},{1,3},{2,0},{3,1},{4,6},{5,7},{6,4},{7,5},{8,10},{9,11},{10,... | collective-permute-start | bytes 196616 | tf_op jit(solution)/shard_map/ppermute | solution.py:128
  4.8 2.6 %collective-permute-start.2 = (bf16[8,2,2048]{2,1,0:T(2,128)(2,1)S(1)}, bf16[8,2,2048]{2,1,0:T(2,128)(2,1)S(1)}, u32[]{:S(2)}, u32[]{:S(2)}) collective-permute-start(bf16[8,2,2048]{2,1,0:T(2,128)(2,1)S(1)} %bitcast.36), channel_id=1, source_target_pairs={{0,3},{1,2},{2,1},{3,0},{4,7},{5,6},{6,5},{7,4},{8,11},{9,10},{10,... | collective-permute-start | bytes 196616 | tf_op jit(solution)/shard_map/ppermute | solution.py:128
  7.4 0.0 copy-done.3
  7.4 0.1 pad_maximum_fusion
  7.6 0.5 %collective-permute-start = (bf16[12,2,2048]{2,1,0:T(2,128)(2,1)S(1)}, bf16[12,2,2048]{2,1,0:T(2,128)(2,1)S(1)}, u32[]{:S(2)}, u32[]{:S(2)}) collective-permute-start(bf16[12,2,2048]{2,1,0:T(2,128)(2,1)S(1)} %pad_maximum_fusion), channel_id=1, source_target_pairs={{0,1},{1,0},{2,3},{3,2},{4,5},{5,4},{6,7},{7,6},{8,9},{9,8},{10,11... | collective-permute-start | bytes 294920 | tf_op jit(solution)/shard_map/ppermute | solution.py:124
  9.4 0.1 pad_add_fusion.1
  9.5 0.0 collective-permute-done.1
  9.5 0.3 collective-permute-done.2
  9.8 2.6 %collective-permute-done = bf16[12,2,2048]{2,1,0:T(2,128)(2,1)S(1)} collective-permute-done((bf16[12,2,2048]{2,1,0:T(2,128)(2,1)S(1)}, bf16[12,2,2048]{2,1,0:T(2,128)(2,1)S(1)}, u32[]{:S(2)}, u32[]{:S(2)}) %collective-permute-start) | collective-permute-done | bytes 98336 | tf_op jit(solution)/shard_map/ppermute | solution.py:124
  12.4 0.1 fusion.4
  12.5 2.6 %collective-permute-start.5 = (bf16[8,2,2048]{2,1,0:T(2,128)(2,1)S(1)}, bf16[8,2,2048]{2,1,0:T(2,128)(2,1)S(1)}, u32[]{:S(2)}, u32[]{:S(2)}) collective-permute-start(bf16[8,2,2048]{2,1,0:T(2,128)(2,1)S(1)} %fusion.4), channel_id=1, source_target_pairs={{0,12},{1,13},{2,14},{3,15},{4,8},{5,9},{6,10},{7,11},{8,4},{9,5},... | collective-permute-start | bytes 196616 | tf_op jit(solution)/shard_map/ppermute | solution.py:128
  15.1 0.4 collective-permute-start.4
  15.6 0.5 %collective-permute-start.3 = (bf16[8,2,2048]{2,1,0:T(2,128)(2,1)S(1)}, bf16[8,2,2048]{2,1,0:T(2,128)(2,1)S(1)}, u32[]{:S(2)}, u32[]{:S(2)}) collective-permute-start(bf16[8,2,2048]{2,1,0:T(2,128)(2,1)S(1)} %fusion.4), channel_id=1, source_target_pairs={{0,4},{1,5},{2,6},{3,7},{4,0},{5,1},{6,2},{7,3},{8,12},{9,13},{10,... | collective-permute-start | bytes 196616 | tf_op jit(solution)/shard_map/ppermute | solution.py:128
  16.1 0.1 broadcast_select_fusion
  16.2 0.5 %slice.31 = bf16[1]{0:T(256)(128)(2,1)} slice(bf16[32768]{0:T(1024)(128)(2,1)S(1)} %bitcast.45), slice={[0:1]} | slice | bytes 4 | tf_op jit(solution)/shard_map/slice | solution.py:134
  18.0 0.7 %pad_convert_fusion.wpad_ref = f32[4,2,5248]{2,1,0:T(2,128)} fusion(bf16[4,2,4096]{2,1,0:T(2,128)(2,1)S(1)} %broadcast_select_fusion), kind=kLoop, calls=%fused_computation.10 | loop fusion | flops 41984 | bytes 233472 | tf_op jit(solution)/shard_map/jit(_pad)/pad | solution.py:183
  18.8 0.0 collective-permute-done.5
  18.8 0.6 %collective-permute-done.4 = bf16[8,2,2048]{2,1,0:T(2,128)(2,1)S(1)} collective-permute-done((bf16[8,2,2048]{2,1,0:T(2,128)(2,1)S(1)}, bf16[8,2,2048]{2,1,0:T(2,128)(2,1)S(1)}, u32[]{:S(2)}, u32[]{:S(2)}) %collective-permute-start.4) | collective-permute-done | bytes 65568 | tf_op jit(solution)/shard_map/ppermute | solution.py:128
  19.4 0.4 collective-permute-done.3
  19.8 0.0 copy-start
  19.9 2.7 %collective-permute-start.6 = (bf16[8,2,2048]{2,1,0:T(2,128)(2,1)S(1)}, bf16[8,2,2048]{2,1,0:T(2,128)(2,1)S(1)}, u32[]{:S(2)}, u32[]{:S(2)}) collective-permute-start(bf16[8,2,2048]{2,1,0:T(2,128)(2,1)S(1)} %bitcast.40), channel_id=1, source_target_pairs={{0,16},{1,17},{2,18},{3,19},{4,20},{5,21},{6,22},{7,23},{8,24},{9,... | collective-permute-start | bytes 196616 | tf_op jit(solution)/shard_map/ppermute | solution.py:128
  22.5 1.3 %fusion.5 = (f32[128,152]{1,0:T(8,128)}, f32[128,152]{1,0:T(8,128)}) fusion(s32[152]{0:T(256)S(1)} %pad_add_fusion.1, s32[128]{0:T(128)S(1)} %iota_add_fusion), kind=kLoop, calls=%fused_computation.15 | loop fusion | flops 272384 | bytes 156768 | tf_op jit(solution)/shard_map/sin | solution.py:21
  23.8 0.0 copy-done
  23.8 1.3 %collective-permute-done.6.rest_1_ = bf16[8,2,2048]{2,1,0:T(2,128)(2,1)S(1)} collective-permute-done((bf16[8,2,2048]{2,1,0:T(2,128)(2,1)S(1)}, bf16[8,2,2048]{2,1,0:T(2,128)(2,1)S(1)}, u32[]{:S(2)}, u32[]{:S(2)}) %collective-permute-start.6) | collective-permute-done | bytes 65568 | tf_op jit(solution)/shard_map/ppermute | solution.py:128
  25.1 0.0 copy-start.1
  25.1 0.6 %copy-done.1 = bf16[8,2,2048]{2,1,0:T(2,128)(2,1)} copy-done((bf16[8,2,2048]{2,1,0:T(2,128)(2,1)}, bf16[8,2,2048]{2,1,0:T(2,128)(2,1)S(1)}, u32[]{:S(2)}) %copy-start.1) | copy-done | bytes 65560
  25.7 19.9 %shard_map.64 = f32[6,2,128,128]{3,2,1,0:T(8,128)} custom-call(s32[6]{0:T(128)} %bitcast.46, s32[1]{0:T(128)S(6)} %copy.13.count_ref, f32[4,2,5248]{2,1,0:T(2,128)} %pad_convert_fusion.wpad_ref, f32[128,152]{1,0:T(8,128)} %get-tuple-element.6.cos_ref, f32[128,152]{1,0:T(8,128)} %get-tuple-element.5.sin_ref, bf16[8,2,2048]{2,1,0:T(2,128)(2,1)} %bitcast.41, ...), custom_call_target="tpu_custom_call" | custom-call | tf_op jit(solution)/shard_map/pallas_call | solution.py:196
  (9 shorter events, 0.1 us)
Async XLA Ops:
  0.0 4.0 %copy-start.2 = (bf16[1,2,4,2048]{3,2,1,0:T(4,128)(2,1)S(1)}, bf16[1,2,4,2048]{3,2,1,0:T(4,128)(2,1)}, u32[]{:S(2)}) copy-start(bf16[1,2,4,2048]{3,2,1,0:T(4,128)(2,1)} %param.7) | copy-start | bytes 98308
  4.1 3.2 %copy-start.3 = (bf16[1,2,4,2048]{3,2,1,0:T(4,128)(2,1)S(1)}, bf16[1,2,4,2048]{3,2,1,0:T(4,128)(2,1)}, u32[]{:S(2)}) copy-start(bf16[1,2,4,2048]{3,2,1,0:T(4,128)(2,1)} %param.6) | copy-start | bytes 98308
  4.2 5.2 %collective-permute-start.1 = (bf16[8,2,2048]{2,1,0:T(2,128)(2,1)S(1)}, bf16[8,2,2048]{2,1,0:T(2,128)(2,1)S(1)}, u32[]{:S(2)}, u32[]{:S(2)}) collective-permute-start(bf16[8,2,2048]{2,1,0:T(2,128)(2,1)S(1)} %bitcast.35), channel_id=1, source_target_pairs={{0,2},{1,3},{2,0},{3,1},{4,6},{5,7},{6,4},{7,5},{8,10},{9,11},{10,... | collective-permute-start | bytes 196616 | tf_op jit(solution)/shard_map/ppermute | solution.py:128
  4.8 5.0 %collective-permute-start.2 = (bf16[8,2,2048]{2,1,0:T(2,128)(2,1)S(1)}, bf16[8,2,2048]{2,1,0:T(2,128)(2,1)S(1)}, u32[]{:S(2)}, u32[]{:S(2)}) collective-permute-start(bf16[8,2,2048]{2,1,0:T(2,128)(2,1)S(1)} %bitcast.36), channel_id=1, source_target_pairs={{0,3},{1,2},{2,1},{3,0},{4,7},{5,6},{6,5},{7,4},{8,11},{9,10},{10,... | collective-permute-start | bytes 196616 | tf_op jit(solution)/shard_map/ppermute | solution.py:128
  7.6 4.8 %collective-permute-start = (bf16[12,2,2048]{2,1,0:T(2,128)(2,1)S(1)}, bf16[12,2,2048]{2,1,0:T(2,128)(2,1)S(1)}, u32[]{:S(2)}, u32[]{:S(2)}) collective-permute-start(bf16[12,2,2048]{2,1,0:T(2,128)(2,1)S(1)} %pad_maximum_fusion), channel_id=1, source_target_pairs={{0,1},{1,0},{2,3},{3,2},{4,5},{5,4},{6,7},{7,6},{8,9},{9,8},{10,11... | collective-permute-start | bytes 294920 | tf_op jit(solution)/shard_map/ppermute | solution.py:124
  12.5 6.3 %collective-permute-start.5 = (bf16[8,2,2048]{2,1,0:T(2,128)(2,1)S(1)}, bf16[8,2,2048]{2,1,0:T(2,128)(2,1)S(1)}, u32[]{:S(2)}, u32[]{:S(2)}) collective-permute-start(bf16[8,2,2048]{2,1,0:T(2,128)(2,1)S(1)} %fusion.4), channel_id=1, source_target_pairs={{0,12},{1,13},{2,14},{3,15},{4,8},{5,9},{6,10},{7,11},{8,4},{9,5},... | collective-permute-start | bytes 196616 | tf_op jit(solution)/shard_map/ppermute | solution.py:128
  15.1 4.3 %collective-permute-start.4 = (bf16[8,2,2048]{2,1,0:T(2,128)(2,1)S(1)}, bf16[8,2,2048]{2,1,0:T(2,128)(2,1)S(1)}, u32[]{:S(2)}, u32[]{:S(2)}) collective-permute-start(bf16[8,2,2048]{2,1,0:T(2,128)(2,1)S(1)} %fusion.4), channel_id=1, source_target_pairs={{0,8},{1,9},{2,10},{3,11},{4,12},{5,13},{6,14},{7,15},{8,0},{9,1},... | collective-permute-start | bytes 196616 | tf_op jit(solution)/shard_map/ppermute | solution.py:128
  15.6 4.3 %collective-permute-start.3 = (bf16[8,2,2048]{2,1,0:T(2,128)(2,1)S(1)}, bf16[8,2,2048]{2,1,0:T(2,128)(2,1)S(1)}, u32[]{:S(2)}, u32[]{:S(2)}) collective-permute-start(bf16[8,2,2048]{2,1,0:T(2,128)(2,1)S(1)} %fusion.4), channel_id=1, source_target_pairs={{0,4},{1,5},{2,6},{3,7},{4,0},{5,1},{6,2},{7,3},{8,12},{9,13},{10,... | collective-permute-start | bytes 196616 | tf_op jit(solution)/shard_map/ppermute | solution.py:128
  19.8 4.0 %copy-start = (bf16[2,8,2048]{2,1,0:T(8,128)(2,1)}, bf16[2,8,2048]{2,1,0:T(8,128)(2,1)S(1)}, u32[]{:S(2)}) copy-start(bf16[2,8,2048]{2,1,0:T(8,128)(2,1)S(1)} %add_add_fusion) | copy-start | bytes 196612
  19.9 5.2 %collective-permute-start.6 = (bf16[8,2,2048]{2,1,0:T(2,128)(2,1)S(1)}, bf16[8,2,2048]{2,1,0:T(2,128)(2,1)S(1)}, u32[]{:S(2)}, u32[]{:S(2)}) collective-permute-start(bf16[8,2,2048]{2,1,0:T(2,128)(2,1)S(1)} %bitcast.40), channel_id=1, source_target_pairs={{0,16},{1,17},{2,18},{3,19},{4,20},{5,21},{6,22},{7,23},{8,24},{9,... | collective-permute-start | bytes 196616 | tf_op jit(solution)/shard_map/ppermute | solution.py:128
  25.1 0.6 %copy-start.1 = (bf16[8,2,2048]{2,1,0:T(2,128)(2,1)}, bf16[8,2,2048]{2,1,0:T(2,128)(2,1)S(1)}, u32[]{:S(2)}) copy-start(bf16[8,2,2048]{2,1,0:T(2,128)(2,1)S(1)} %collective-permute-done.6.rest_1_) | copy-start | bytes 196612

commit v16 on v11

--- a/solution.py
+++ b/solution.py
@@ -111,9 +111,8 @@
             out_ref[q, 1] = jnp.where(keep, reverse_rows(im) * norm, 0.0)
 
 
-def butterfly_sum(value, axes, later=(), rider=None):
+def butterfly_sum(value, axes, later=(), rider=None, stride=1):
     count = lax.axis_size(axes)
-    stride = 1
     carried = None
     while stride < count:
         radix = 4 if stride * 4 <= count else 2
@@ -163,13 +162,21 @@
     mine = (owner_index == beam_place)[None, :, None]
     local = jnp.where(mine, reference_blocks[0], jnp.zeros_like(reference_blocks[0]))
     group = lax.axis_size(("beam", "seg"))
-    if segments == 2 and group >= 4 and not group & (group - 1) and seg_len == CHUNK:
+    if segments == 2 and group >= 16 and not group & (group - 1) and seg_len == CHUNK:
+        axes = ("beam", "seg")
         first = seg_place == 0
         own = jnp.transpose(local, (1, 0, 2))
-        zero = jnp.zeros_like(own)
-        placed = jnp.where(first, jnp.stack([own, zero], 1), jnp.stack([zero, own], 1)).reshape(-1, 2, seg_len)
         mine_samples = jnp.transpose(surveillance[0], (1, 0, 2))
-        refparts, (first_bin,), other = butterfly_sum(placed, ("beam", "seg"), (doppler_start[0],), mine_samples)
+        swap = lambda x, m: lax.ppermute(x, axes, [(i, i ^ m) for i in range(group)])
+        partner = swap(jnp.concatenate([own, mine_samples], 0), 1)
+        same_half = own + swap(own, 2)
+        other_half = partner[:step_count] + swap(own, 3)
+        other = partner[step_count:]
+        placed = jnp.where(first, jnp.stack([same_half, other_half], 1),
+                           jnp.stack([other_half, same_half], 1)).reshape(-1, 2, seg_len)
+        late = (placed.reshape(-1)[0] != placed.reshape(-1)[0]).astype(jnp.int32)
+        first_bin = doppler_start[0] + late
+        refparts, _, _ = butterfly_sum(placed, axes, stride=4)
         samples = jnp.where(first, jnp.concatenate([mine_samples, other], -1),
                             jnp.concatenate([other, mine_samples], -1))
     else:

time: 43.5 us -> 42.9 us (0.986)
  Pallas kernels: 20.2 us -> 19.7 us
  starting transfers between devices: 9.88 us -> 9.4 us
    ppermute x6 -> x4, starting transfers between devices: 9.34 us -> 6.21 us  [butterfly_sum(): parts.append(lax.ppermute(value, axes, pairs))]
    ppermute x1 -> x3, starting transfers between devices: 0.54 us -> 3.19 us  [shards(): lax.ppermute(x, axes, [(i, i ^ m) for i in range(group)])]
    transpose x0 -> x1, other arithmetic: none -> 0.86 us  [shards(): own = jnp.transpose(local, (1, 0, 2))]
    another operation x1 -> x2, other arithmetic: 0.84 us -> 0.17 us  [shards(): jnp.stack([same_half, other_half], 1)]
    pallas_call x1, Pallas kernels: 20.2 us -> 19.7 us  [shards(): pl.pallas_call(kernel, out_shape=jax.ShapeDtypeStruct((slot_count, 2, LB,...]
    ppermute x1 -> x3, waiting for transfers between devices: 2.58 us -> 2.71 us  [shards(): lax.ppermute(x, axes, [(i, i ^ m) for i in range(group)])]
    ppermute x6 -> x4, waiting for transfers between devices: 2.64 us -> 2.53 us  [butterfly_sum(): parts.append(lax.ppermute(value, axes, pairs))]
    unnamed x10 -> x12, local copies, waits for them, and re-layouts: 1.33 us -> 1.34 us
  transfers between devices with their start and end apart: 7 -> 7, of which waited for: 5 -> 4; matrix products, arithmetic and copies ran while one was open for 7% -> 7% of each run, Pallas kernels for 0% -> 0%
where the time goes in v16:
time: 42.9 us; the launch traced here: 42.5 us
  Pallas kernels  19.7 us (46%)
  starting transfers between devices  9.4 us (22%)
  waiting for transfers between devices  5.24 us (12%)
  other arithmetic  3.58 us (8%)
  between operations  2.73 us (6%)
  local copies, waits for them, and re-layouts  1.9 us (4%)
    pallas_call x1, Pallas kernels, shards(): pl.pallas_call(kernel, out_shape=jax.ShapeDtypeStruct((slot_count, 2, LB,...  19.7 us
    ppermute x4, starting transfers between devices, butterfly_sum(): parts.append(lax.ppermute(value, axes, pairs))  6.21 us
    ppermute x3, starting transfers between devices, shards(): lax.ppermute(x, axes, [(i, i ^ m) for i in range(group)])  3.19 us
    ppermute x3, waiting for transfers between devices, shards(): lax.ppermute(x, axes, [(i, i ^ m) for i in range(group)])  2.71 us
    ppermute x4, waiting for transfers between devices, butterfly_sum(): parts.append(lax.ppermute(value, axes, pairs))  2.53 us
    unnamed x12, local copies, waits for them, and re-layouts  1.34 us
    sin x1, other arithmetic, phase_rows(): return (jnp.cos(angle), jnp.sin(angle))  1.31 us
    transpose x1, other arithmetic, shards(): own = jnp.transpose(local, (1, 0, 2))  0.86 us
  transfers between devices with their start and end apart: 7, of which 4 were waited for; matrix products, arithmetic and copies ran while one was open for 7% of the time, Pallas kernels for 0%

profile of v16, /device:TPU:0, one launch (start us, length us, event | category | flops | bytes accessed | tf_op | source)
XLA Modules:
  0.0 42.5 jit_solution(760349741302722703)
XLA Ops:
  0.0 0.0 copy-start.4
  0.0 0.7 %copy-done.4 = s32[4]{0:T(128)S(1)} copy-done((s32[4]{0:T(128)S(1)}, s32[4]{0:T(128)}, u32[]{:S(2)}) %copy-start.4) | copy-done | bytes 40
  0.7 0.0 copy-start.3
  0.7 0.9 %fusion.6 = bf16[4,2,2048]{2,1,0:T(2,128)(2,1)S(1)} fusion(bf16[1,2,4,2048]{3,2,1,0:T(4,128)(2,1)} %param.7, pred[4]{0:T(512)(128)(4,1)S(1)} %broadcast_compare_fusion), kind=kLoop, calls=%fused_computation.20 | loop fusion | flops 16384 | bytes 65540 | tf_op jit(solution)/shard_map/transpose | solution.py:168
  1.5 2.4 %collective-permute-start.2 = (bf16[4,2,2048]{2,1,0:T(2,128)(2,1)S(1)}, bf16[4,2,2048]{2,1,0:T(2,128)(2,1)S(1)}, u32[]{:S(2)}, u32[]{:S(2)}) collective-permute-start(bf16[4,2,2048]{2,1,0:T(2,128)(2,1)S(1)} %fusion.6), channel_id=1, source_target_pairs={{0,3},{1,2},{2,1},{3,0},{4,7},{5,6},{6,5},{7,4},{8,11},{9,10},{10,... | collective-permute-start | bytes 98312 | tf_op jit(solution)/shard_map/ppermute | solution.py:170
  4.0 0.7 %collective-permute-start.1 = (bf16[4,2,2048]{2,1,0:T(2,128)(2,1)S(1)}, bf16[4,2,2048]{2,1,0:T(2,128)(2,1)S(1)}, u32[]{:S(2)}, u32[]{:S(2)}) collective-permute-start(bf16[4,2,2048]{2,1,0:T(2,128)(2,1)S(1)} %fusion.6), channel_id=1, source_target_pairs={{0,2},{1,3},{2,0},{3,1},{4,6},{5,7},{6,4},{7,5},{8,10},{9,11},{10,... | collective-permute-start | bytes 98312 | tf_op jit(solution)/shard_map/ppermute | solution.py:170
  4.6 0.0 copy-done.3
  4.7 0.0 copy-start.1
  4.7 0.1 pad_maximum_fusion
  4.8 0.1 collective-permute-start
  4.9 0.1 pad_add_fusion
  6.3 0.0 collective-permute-done.1
  6.3 0.0 copy-done.1
  6.3 0.1 add_bitcast_fusion
  6.4 0.0 collective-permute-done.2
  6.4 2.7 %collective-permute-done = bf16[8,2,2048]{2,1,0:T(2,128)(2,1)S(1)} collective-permute-done((bf16[8,2,2048]{2,1,0:T(2,128)(2,1)S(1)}, bf16[8,2,2048]{2,1,0:T(2,128)(2,1)S(1)}, u32[]{:S(2)}, u32[]{:S(2)}) %collective-permute-start) | collective-permute-done | bytes 65568 | tf_op jit(solution)/shard_map/ppermute | solution.py:170
  9.1 0.1 fusion.5
  9.2 0.1 broadcast_select_fusion
  9.4 1.6 %collective-permute-start.4 = (bf16[8,2,2048]{2,1,0:T(2,128)(2,1)S(1)}, bf16[8,2,2048]{2,1,0:T(2,128)(2,1)S(1)}, u32[]{:S(2)}, u32[]{:S(2)}) collective-permute-start(bf16[8,2,2048]{2,1,0:T(2,128)(2,1)S(1)} %bitcast.26), channel_id=1, source_target_pairs={{0,8},{1,9},{2,10},{3,11},{4,12},{5,13},{6,14},{7,15},{8,0},{9,1},... | collective-permute-start | bytes 196616 | tf_op jit(solution)/shard_map/ppermute | solution.py:127
  11.0 1.4 %collective-permute-start.5 = (bf16[8,2,2048]{2,1,0:T(2,128)(2,1)S(1)}, bf16[8,2,2048]{2,1,0:T(2,128)(2,1)S(1)}, u32[]{:S(2)}, u32[]{:S(2)}) collective-permute-start(bf16[8,2,2048]{2,1,0:T(2,128)(2,1)S(1)} %bitcast.27), channel_id=1, source_target_pairs={{0,12},{1,13},{2,14},{3,15},{4,8},{5,9},{6,10},{7,11},{8,4},{9,5},... | collective-permute-start | bytes 196616 | tf_op jit(solution)/shard_map/ppermute | solution.py:127
  12.4 0.5 %collective-permute-start.3 = (bf16[8,2,2048]{2,1,0:T(2,128)(2,1)S(1)}, bf16[8,2,2048]{2,1,0:T(2,128)(2,1)S(1)}, u32[]{:S(2)}, u32[]{:S(2)}) collective-permute-start(bf16[8,2,2048]{2,1,0:T(2,128)(2,1)S(1)} %bitcast.28), channel_id=1, source_target_pairs={{0,4},{1,5},{2,6},{3,7},{4,0},{5,1},{6,2},{7,3},{8,12},{9,13},{10,... | collective-permute-start | bytes 196616 | tf_op jit(solution)/shard_map/ppermute | solution.py:127
  12.9 0.1 broadcast_select_fusion.1
  13.0 0.5 %slice.15 = bf16[1]{0:T(256)(128)(2,1)} slice(bf16[32768]{0:T(1024)(128)(2,1)S(1)} %bitcast.32), slice={[0:1]} | slice | bytes 4 | tf_op jit(solution)/shard_map/slice | solution.py:177
  14.9 0.7 %pad_convert_fusion.wpad_ref = f32[4,2,5248]{2,1,0:T(2,128)} fusion(bf16[4,2,4096]{2,1,0:T(2,128)(2,1)S(1)} %broadcast_select_fusion.1), kind=kLoop, calls=%fused_computation.10 | loop fusion | flops 41984 | bytes 233472 | tf_op jit(solution)/shard_map/jit(_pad)/pad | solution.py:190
  15.6 0.0 collective-permute-done.4
  15.6 0.6 %collective-permute-done.5 = bf16[8,2,2048]{2,1,0:T(2,128)(2,1)S(1)} collective-permute-done((bf16[8,2,2048]{2,1,0:T(2,128)(2,1)S(1)}, bf16[8,2,2048]{2,1,0:T(2,128)(2,1)S(1)}, u32[]{:S(2)}, u32[]{:S(2)}) %collective-permute-start.5) | collective-permute-done | bytes 65568 | tf_op jit(solution)/shard_map/ppermute | solution.py:127
  16.2 0.7 %collective-permute-done.3 = bf16[8,2,2048]{2,1,0:T(2,128)(2,1)S(1)} collective-permute-done((bf16[8,2,2048]{2,1,0:T(2,128)(2,1)S(1)}, bf16[8,2,2048]{2,1,0:T(2,128)(2,1)S(1)}, u32[]{:S(2)}, u32[]{:S(2)}) %collective-permute-start.3) | collective-permute-done | bytes 65568 | tf_op jit(solution)/shard_map/ppermute | solution.py:127
  16.9 0.1 add_add_fusion.rest_0_
  17.0 0.0 copy-start
  17.0 2.7 %collective-permute-start.6 = (bf16[8,2,2048]{2,1,0:T(2,128)(2,1)S(1)}, bf16[8,2,2048]{2,1,0:T(2,128)(2,1)S(1)}, u32[]{:S(2)}, u32[]{:S(2)}) collective-permute-start(bf16[8,2,2048]{2,1,0:T(2,128)(2,1)S(1)} %add_add_fusion.rest_0_), channel_id=1, source_target_pairs={{0,16},{1,17},{2,18},{3,19},{4,20},{5,21},{6,22},{7,23},{8,24},{9,... | collective-permute-start | bytes 196616 | tf_op jit(solution)/shard_map/ppermute | solution.py:127
  19.7 1.3 %fusion.3 = (f32[128,152]{1,0:T(8,128)}, f32[128,152]{1,0:T(8,128)}) fusion(s32[152]{0:T(256)S(1)} %pad_add_fusion, s32[128]{0:T(128)S(1)} %iota_add_fusion), kind=kLoop, calls=%fused_computation.13 | loop fusion | flops 272384 | bytes 156768 | tf_op jit(solution)/shard_map/sin | solution.py:21
  21.0 0.0 copy-done
  21.0 1.3 %collective-permute-done.6.rest_1_ = bf16[8,2,2048]{2,1,0:T(2,128)(2,1)S(1)} collective-permute-done((bf16[8,2,2048]{2,1,0:T(2,128)(2,1)S(1)}, bf16[8,2,2048]{2,1,0:T(2,128)(2,1)S(1)}, u32[]{:S(2)}, u32[]{:S(2)}) %collective-permute-start.6) | collective-permute-done | bytes 65568 | tf_op jit(solution)/shard_map/ppermute | solution.py:127
  22.2 0.0 copy-start.2
  22.2 0.6 %copy-done.2 = bf16[8,2,2048]{2,1,0:T(2,128)(2,1)} copy-done((bf16[8,2,2048]{2,1,0:T(2,128)(2,1)}, bf16[8,2,2048]{2,1,0:T(2,128)(2,1)S(1)}, u32[]{:S(2)}) %copy-start.2) | copy-done | bytes 65560
  22.9 19.7 %shard_map.64 = f32[6,2,128,128]{3,2,1,0:T(8,128)} custom-call(s32[6]{0:T(128)} %bitcast.33, s32[1]{0:T(128)S(6)} %copy.23.count_ref, f32[4,2,5248]{2,1,0:T(2,128)} %pad_convert_fusion.wpad_ref, f32[128,152]{1,0:T(8,128)} %get-tuple-element.8.cos_ref, f32[128,152]{1,0:T(8,128)} %get-tuple-element.7.sin_ref, bf16[8,2,2048]{2,1,0:T(2,128)(2,1)} %copy-done, ...), custom_call_target="tpu_custom_call" | custom-call | tf_op jit(solution)/shard_map/pallas_call | solution.py:203
  (8 shorter events, 0.1 us)
Async XLA Ops:
  0.0 0.7 %copy-start.4 = (s32[4]{0:T(128)S(1)}, s32[4]{0:T(128)}, u32[]{:S(2)}) copy-start(s32[4]{0:T(128)} %param.8) | copy-start | bytes 52
  0.7 4.0 %copy-start.3 = (bf16[1,2,4,2048]{3,2,1,0:T(4,128)(2,1)S(1)}, bf16[1,2,4,2048]{3,2,1,0:T(4,128)(2,1)}, u32[]{:S(2)}) copy-start(bf16[1,2,4,2048]{3,2,1,0:T(4,128)(2,1)} %param.6) | copy-start | bytes 98308
  1.5 4.9 %collective-permute-start.2 = (bf16[4,2,2048]{2,1,0:T(2,128)(2,1)S(1)}, bf16[4,2,2048]{2,1,0:T(2,128)(2,1)S(1)}, u32[]{:S(2)}, u32[]{:S(2)}) collective-permute-start(bf16[4,2,2048]{2,1,0:T(2,128)(2,1)S(1)} %fusion.6), channel_id=1, source_target_pairs={{0,3},{1,2},{2,1},{3,0},{4,7},{5,6},{6,5},{7,4},{8,11},{9,10},{10,... | collective-permute-start | bytes 98312 | tf_op jit(solution)/shard_map/ppermute | solution.py:170
  4.0 2.3 %collective-permute-start.1 = (bf16[4,2,2048]{2,1,0:T(2,128)(2,1)S(1)}, bf16[4,2,2048]{2,1,0:T(2,128)(2,1)S(1)}, u32[]{:S(2)}, u32[]{:S(2)}) collective-permute-start(bf16[4,2,2048]{2,1,0:T(2,128)(2,1)S(1)} %fusion.6), channel_id=1, source_target_pairs={{0,2},{1,3},{2,0},{3,1},{4,6},{5,7},{6,4},{7,5},{8,10},{9,11},{10,... | collective-permute-start | bytes 98312 | tf_op jit(solution)/shard_map/ppermute | solution.py:170
  4.7 1.6 %copy-start.1 = (bf16[1,2,4,2048]{3,2,1,0:T(4,128)(2,1)S(1)}, bf16[1,2,4,2048]{3,2,1,0:T(4,128)(2,1)}, u32[]{:S(2)}) copy-start(bf16[1,2,4,2048]{3,2,1,0:T(4,128)(2,1)} %param.7) | copy-start | bytes 98308
  4.8 4.3 %collective-permute-start = (bf16[8,2,2048]{2,1,0:T(2,128)(2,1)S(1)}, bf16[8,2,2048]{2,1,0:T(2,128)(2,1)S(1)}, u32[]{:S(2)}, u32[]{:S(2)}) collective-permute-start(bf16[8,2,2048]{2,1,0:T(2,128)(2,1)S(1)} %pad_maximum_fusion), channel_id=1, source_target_pairs={{0,1},{1,0},{2,3},{3,2},{4,5},{5,4},{6,7},{7,6},{8,9},{9,8},{10,11... | collective-permute-start | bytes 196616 | tf_op jit(solution)/shard_map/ppermute | solution.py:170
  9.4 6.2 %collective-permute-start.4 = (bf16[8,2,2048]{2,1,0:T(2,128)(2,1)S(1)}, bf16[8,2,2048]{2,1,0:T(2,128)(2,1)S(1)}, u32[]{:S(2)}, u32[]{:S(2)}) collective-permute-start(bf16[8,2,2048]{2,1,0:T(2,128)(2,1)S(1)} %bitcast.26), channel_id=1, source_target_pairs={{0,8},{1,9},{2,10},{3,11},{4,12},{5,13},{6,14},{7,15},{8,0},{9,1},... | collective-permute-start | bytes 196616 | tf_op jit(solution)/shard_map/ppermute | solution.py:127
  11.0 5.2 %collective-permute-start.5 = (bf16[8,2,2048]{2,1,0:T(2,128)(2,1)S(1)}, bf16[8,2,2048]{2,1,0:T(2,128)(2,1)S(1)}, u32[]{:S(2)}, u32[]{:S(2)}) collective-permute-start(bf16[8,2,2048]{2,1,0:T(2,128)(2,1)S(1)} %bitcast.27), channel_id=1, source_target_pairs={{0,12},{1,13},{2,14},{3,15},{4,8},{5,9},{6,10},{7,11},{8,4},{9,5},... | collective-permute-start | bytes 196616 | tf_op jit(solution)/shard_map/ppermute | solution.py:127
  12.4 4.5 %collective-permute-start.3 = (bf16[8,2,2048]{2,1,0:T(2,128)(2,1)S(1)}, bf16[8,2,2048]{2,1,0:T(2,128)(2,1)S(1)}, u32[]{:S(2)}, u32[]{:S(2)}) collective-permute-start(bf16[8,2,2048]{2,1,0:T(2,128)(2,1)S(1)} %bitcast.28), channel_id=1, source_target_pairs={{0,4},{1,5},{2,6},{3,7},{4,0},{5,1},{6,2},{7,3},{8,12},{9,13},{10,... | collective-permute-start | bytes 196616 | tf_op jit(solution)/shard_map/ppermute | solution.py:127
  17.0 4.0 %copy-start = (bf16[8,2,2048]{2,1,0:T(2,128)(2,1)}, bf16[8,2,2048]{2,1,0:T(2,128)(2,1)S(1)}, u32[]{:S(2)}) copy-start(bf16[8,2,2048]{2,1,0:T(2,128)(2,1)S(1)} %add_add_fusion.rest_0_) | copy-start | bytes 196612
  17.0 5.2 %collective-permute-start.6 = (bf16[8,2,2048]{2,1,0:T(2,128)(2,1)S(1)}, bf16[8,2,2048]{2,1,0:T(2,128)(2,1)S(1)}, u32[]{:S(2)}, u32[]{:S(2)}) collective-permute-start(bf16[8,2,2048]{2,1,0:T(2,128)(2,1)S(1)} %add_add_fusion.rest_0_), channel_id=1, source_target_pairs={{0,16},{1,17},{2,18},{3,19},{4,20},{5,21},{6,22},{7,23},{8,24},{9,... | collective-permute-start | bytes 196616 | tf_op jit(solution)/shard_map/ppermute | solution.py:127
  22.2 0.6 %copy-start.2 = (bf16[8,2,2048]{2,1,0:T(2,128)(2,1)}, bf16[8,2,2048]{2,1,0:T(2,128)(2,1)S(1)}, u32[]{:S(2)}) copy-start(bf16[8,2,2048]{2,1,0:T(2,128)(2,1)S(1)} %collective-permute-done.6.rest_1_) | copy-start | bytes 196612

commit v17 on v16

--- a/solution.py
+++ b/solution.py
@@ -12,7 +12,6 @@
 NLB = 8
 DOP = 256
 CHUNK = 2048
-PIECE = 1024
 
 
 def phase_rows(freqs, times, window_len):
@@ -44,16 +43,17 @@
         return jnp.sum(jnp.where(pick, tail, 0.0), axis=1, keepdims=True)
 
     pair = pl.program_id(0)
-    lanes = PIECE + LB
-    pieces = [(comp, i) for comp in range(2) for i in range(span // PIECE)]
+    piece = span
+    lanes = piece + LB
+    pieces = [(comp, i) for comp in range(2) for i in range(span // piece)]
     share = -(-len(pieces) // chunks)
 
     def build_piece(step, comp, i, dst):
-        v0 = i * PIECE
+        v0 = i * piece
         win = wpad_ref[step, comp:comp + 1, v0:v0 + lanes]
         tile = jnp.broadcast_to(win, (LB, lanes))
         rolled = pltpu.roll(tile, lanes - LB + 1, 1, stride=1, stride_axis=0)
-        dst[comp * LB:(comp + 1) * LB, v0:v0 + PIECE] = rolled[:, :PIECE].astype(jnp.bfloat16)
+        dst[comp * LB:(comp + 1) * LB, v0:v0 + piece] = rolled[:, :piece].astype(jnp.bfloat16)
 
     @pl.when(pair == 0)
     def _():

time: 42.9 us -> 42.9 us (level)
  no operation moved by 1% of the time
where the time goes in v17:
time: 42.9 us; the launch traced here: 42.8 us
  Pallas kernels  19.9 us (46%)
  starting transfers between devices  9.4 us (22%)
  waiting for transfers between devices  5.24 us (12%)
  other arithmetic  3.58 us (8%)
  between operations  2.73 us (6%)
  local copies, waits for them, and re-layouts  1.9 us (4%)
    pallas_call x1, Pallas kernels, shards(): pl.pallas_call(kernel, out_shape=jax.ShapeDtypeStruct((slot_count, 2, LB,...  19.9 us
    ppermute x4, starting transfers between devices, butterfly_sum(): parts.append(lax.ppermute(value, axes, pairs))  6.21 us
    ppermute x3, starting transfers between devices, shards(): lax.ppermute(x, axes, [(i, i ^ m) for i in range(group)])  3.19 us
    ppermute x3, waiting for transfers between devices, shards(): lax.ppermute(x, axes, [(i, i ^ m) for i in range(group)])  2.71 us
    ppermute x4, waiting for transfers between devices, butterfly_sum(): parts.append(lax.ppermute(value, axes, pairs))  2.53 us
    unnamed x12, local copies, waits for them, and re-layouts  1.34 us
    sin x1, other arithmetic, phase_rows(): return (jnp.cos(angle), jnp.sin(angle))  1.31 us
    transpose x1, other arithmetic, shards(): own = jnp.transpose(local, (1, 0, 2))  0.86 us
  transfers between devices with their start and end apart: 7, of which 4 were waited for; matrix products, arithmetic and copies ran while one was open for 7% of the time, Pallas kernels for 0%

profile of v17, /device:TPU:0, one launch (start us, length us, event | category | flops | bytes accessed | tf_op | source)
XLA Modules:
  0.0 42.8 jit_solution(11873193679333033774)
XLA Ops:
  0.0 0.0 copy-start.4
  0.0 0.7 %copy-done.4 = s32[4]{0:T(128)S(1)} copy-done((s32[4]{0:T(128)S(1)}, s32[4]{0:T(128)}, u32[]{:S(2)}) %copy-start.4) | copy-done | bytes 40
  0.7 0.0 copy-start.3
  0.7 0.9 %fusion.6 = bf16[4,2,2048]{2,1,0:T(2,128)(2,1)S(1)} fusion(bf16[1,2,4,2048]{3,2,1,0:T(4,128)(2,1)} %param.7, pred[4]{0:T(512)(128)(4,1)S(1)} %broadcast_compare_fusion), kind=kLoop, calls=%fused_computation.20 | loop fusion | flops 16384 | bytes 65540 | tf_op jit(solution)/shard_map/transpose | solution.py:168
  1.5 2.4 %collective-permute-start.2 = (bf16[4,2,2048]{2,1,0:T(2,128)(2,1)S(1)}, bf16[4,2,2048]{2,1,0:T(2,128)(2,1)S(1)}, u32[]{:S(2)}, u32[]{:S(2)}) collective-permute-start(bf16[4,2,2048]{2,1,0:T(2,128)(2,1)S(1)} %fusion.6), channel_id=1, source_target_pairs={{0,3},{1,2},{2,1},{3,0},{4,7},{5,6},{6,5},{7,4},{8,11},{9,10},{10,... | collective-permute-start | bytes 98312 | tf_op jit(solution)/shard_map/ppermute | solution.py:170
  4.0 0.7 %collective-permute-start.1 = (bf16[4,2,2048]{2,1,0:T(2,128)(2,1)S(1)}, bf16[4,2,2048]{2,1,0:T(2,128)(2,1)S(1)}, u32[]{:S(2)}, u32[]{:S(2)}) collective-permute-start(bf16[4,2,2048]{2,1,0:T(2,128)(2,1)S(1)} %fusion.6), channel_id=1, source_target_pairs={{0,2},{1,3},{2,0},{3,1},{4,6},{5,7},{6,4},{7,5},{8,10},{9,11},{10,... | collective-permute-start | bytes 98312 | tf_op jit(solution)/shard_map/ppermute | solution.py:170
  4.6 0.0 copy-done.3
  4.7 0.0 copy-start.1
  4.7 0.1 pad_maximum_fusion
  4.8 0.1 collective-permute-start
  4.9 0.1 pad_add_fusion
  6.3 0.0 collective-permute-done.1
  6.3 0.0 copy-done.1
  6.3 0.1 add_bitcast_fusion
  6.4 0.0 collective-permute-done.2
  6.4 2.7 %collective-permute-done = bf16[8,2,2048]{2,1,0:T(2,128)(2,1)S(1)} collective-permute-done((bf16[8,2,2048]{2,1,0:T(2,128)(2,1)S(1)}, bf16[8,2,2048]{2,1,0:T(2,128)(2,1)S(1)}, u32[]{:S(2)}, u32[]{:S(2)}) %collective-permute-start) | collective-permute-done | bytes 65568 | tf_op jit(solution)/shard_map/ppermute | solution.py:170
  9.1 0.1 fusion.5
  9.2 0.1 broadcast_select_fusion
  9.4 1.6 %collective-permute-start.4 = (bf16[8,2,2048]{2,1,0:T(2,128)(2,1)S(1)}, bf16[8,2,2048]{2,1,0:T(2,128)(2,1)S(1)}, u32[]{:S(2)}, u32[]{:S(2)}) collective-permute-start(bf16[8,2,2048]{2,1,0:T(2,128)(2,1)S(1)} %bitcast.26), channel_id=1, source_target_pairs={{0,8},{1,9},{2,10},{3,11},{4,12},{5,13},{6,14},{7,15},{8,0},{9,1},... | collective-permute-start | bytes 196616 | tf_op jit(solution)/shard_map/ppermute | solution.py:127
  11.0 1.4 %collective-permute-start.5 = (bf16[8,2,2048]{2,1,0:T(2,128)(2,1)S(1)}, bf16[8,2,2048]{2,1,0:T(2,128)(2,1)S(1)}, u32[]{:S(2)}, u32[]{:S(2)}) collective-permute-start(bf16[8,2,2048]{2,1,0:T(2,128)(2,1)S(1)} %bitcast.27), channel_id=1, source_target_pairs={{0,12},{1,13},{2,14},{3,15},{4,8},{5,9},{6,10},{7,11},{8,4},{9,5},... | collective-permute-start | bytes 196616 | tf_op jit(solution)/shard_map/ppermute | solution.py:127
  12.4 0.5 %collective-permute-start.3 = (bf16[8,2,2048]{2,1,0:T(2,128)(2,1)S(1)}, bf16[8,2,2048]{2,1,0:T(2,128)(2,1)S(1)}, u32[]{:S(2)}, u32[]{:S(2)}) collective-permute-start(bf16[8,2,2048]{2,1,0:T(2,128)(2,1)S(1)} %bitcast.28), channel_id=1, source_target_pairs={{0,4},{1,5},{2,6},{3,7},{4,0},{5,1},{6,2},{7,3},{8,12},{9,13},{10,... | collective-permute-start | bytes 196616 | tf_op jit(solution)/shard_map/ppermute | solution.py:127
  12.9 0.1 broadcast_select_fusion.1
  13.0 0.5 %slice.15 = bf16[1]{0:T(256)(128)(2,1)} slice(bf16[32768]{0:T(1024)(128)(2,1)S(1)} %bitcast.32), slice={[0:1]} | slice | bytes 4 | tf_op jit(solution)/shard_map/slice | solution.py:177
  14.9 0.7 %pad_convert_fusion.wpad_ref = f32[4,2,5248]{2,1,0:T(2,128)} fusion(bf16[4,2,4096]{2,1,0:T(2,128)(2,1)S(1)} %broadcast_select_fusion.1), kind=kLoop, calls=%fused_computation.10 | loop fusion | flops 41984 | bytes 233472 | tf_op jit(solution)/shard_map/jit(_pad)/pad | solution.py:190
  15.6 0.0 collective-permute-done.4
  15.6 0.6 %collective-permute-done.5 = bf16[8,2,2048]{2,1,0:T(2,128)(2,1)S(1)} collective-permute-done((bf16[8,2,2048]{2,1,0:T(2,128)(2,1)S(1)}, bf16[8,2,2048]{2,1,0:T(2,128)(2,1)S(1)}, u32[]{:S(2)}, u32[]{:S(2)}) %collective-permute-start.5) | collective-permute-done | bytes 65568 | tf_op jit(solution)/shard_map/ppermute | solution.py:127
  16.2 0.7 %collective-permute-done.3 = bf16[8,2,2048]{2,1,0:T(2,128)(2,1)S(1)} collective-permute-done((bf16[8,2,2048]{2,1,0:T(2,128)(2,1)S(1)}, bf16[8,2,2048]{2,1,0:T(2,128)(2,1)S(1)}, u32[]{:S(2)}, u32[]{:S(2)}) %collective-permute-start.3) | collective-permute-done | bytes 65568 | tf_op jit(solution)/shard_map/ppermute | solution.py:127
  16.9 0.1 add_add_fusion.rest_0_
  17.0 0.0 copy-start
  17.0 2.7 %collective-permute-start.6 = (bf16[8,2,2048]{2,1,0:T(2,128)(2,1)S(1)}, bf16[8,2,2048]{2,1,0:T(2,128)(2,1)S(1)}, u32[]{:S(2)}, u32[]{:S(2)}) collective-permute-start(bf16[8,2,2048]{2,1,0:T(2,128)(2,1)S(1)} %add_add_fusion.rest_0_), channel_id=1, source_target_pairs={{0,16},{1,17},{2,18},{3,19},{4,20},{5,21},{6,22},{7,23},{8,24},{9,... | collective-permute-start | bytes 196616 | tf_op jit(solution)/shard_map/ppermute | solution.py:127
  19.7 1.3 %fusion.3 = (f32[128,152]{1,0:T(8,128)}, f32[128,152]{1,0:T(8,128)}) fusion(s32[152]{0:T(256)S(1)} %pad_add_fusion, s32[128]{0:T(128)S(1)} %iota_add_fusion), kind=kLoop, calls=%fused_computation.13 | loop fusion | flops 272384 | bytes 156768 | tf_op jit(solution)/shard_map/sin | solution.py:20
  21.0 0.0 copy-done
  21.0 1.3 %collective-permute-done.6.rest_1_ = bf16[8,2,2048]{2,1,0:T(2,128)(2,1)S(1)} collective-permute-done((bf16[8,2,2048]{2,1,0:T(2,128)(2,1)S(1)}, bf16[8,2,2048]{2,1,0:T(2,128)(2,1)S(1)}, u32[]{:S(2)}, u32[]{:S(2)}) %collective-permute-start.6) | collective-permute-done | bytes 65568 | tf_op jit(solution)/shard_map/ppermute | solution.py:127
  22.2 0.0 copy-start.2
  22.2 0.6 %copy-done.2 = bf16[8,2,2048]{2,1,0:T(2,128)(2,1)} copy-done((bf16[8,2,2048]{2,1,0:T(2,128)(2,1)}, bf16[8,2,2048]{2,1,0:T(2,128)(2,1)S(1)}, u32[]{:S(2)}) %copy-start.2) | copy-done | bytes 65560
  22.9 19.9 %shard_map.64 = f32[6,2,128,128]{3,2,1,0:T(8,128)} custom-call(s32[6]{0:T(128)} %bitcast.33, s32[1]{0:T(128)S(6)} %copy.23.count_ref, f32[4,2,5248]{2,1,0:T(2,128)} %pad_convert_fusion.wpad_ref, f32[128,152]{1,0:T(8,128)} %get-tuple-element.8.cos_ref, f32[128,152]{1,0:T(8,128)} %get-tuple-element.7.sin_ref, bf16[8,2,2048]{2,1,0:T(2,128)(2,1)} %copy-done, ...), custom_call_target="tpu_custom_call" | custom-call | tf_op jit(solution)/shard_map/pallas_call | solution.py:203
  (8 shorter events, 0.1 us)
Async XLA Ops:
  0.0 0.7 %copy-start.4 = (s32[4]{0:T(128)S(1)}, s32[4]{0:T(128)}, u32[]{:S(2)}) copy-start(s32[4]{0:T(128)} %param.8) | copy-start | bytes 52
  0.7 4.0 %copy-start.3 = (bf16[1,2,4,2048]{3,2,1,0:T(4,128)(2,1)S(1)}, bf16[1,2,4,2048]{3,2,1,0:T(4,128)(2,1)}, u32[]{:S(2)}) copy-start(bf16[1,2,4,2048]{3,2,1,0:T(4,128)(2,1)} %param.6) | copy-start | bytes 98308
  1.5 4.9 %collective-permute-start.2 = (bf16[4,2,2048]{2,1,0:T(2,128)(2,1)S(1)}, bf16[4,2,2048]{2,1,0:T(2,128)(2,1)S(1)}, u32[]{:S(2)}, u32[]{:S(2)}) collective-permute-start(bf16[4,2,2048]{2,1,0:T(2,128)(2,1)S(1)} %fusion.6), channel_id=1, source_target_pairs={{0,3},{1,2},{2,1},{3,0},{4,7},{5,6},{6,5},{7,4},{8,11},{9,10},{10,... | collective-permute-start | bytes 98312 | tf_op jit(solution)/shard_map/ppermute | solution.py:170
  4.0 2.3 %collective-permute-start.1 = (bf16[4,2,2048]{2,1,0:T(2,128)(2,1)S(1)}, bf16[4,2,2048]{2,1,0:T(2,128)(2,1)S(1)}, u32[]{:S(2)}, u32[]{:S(2)}) collective-permute-start(bf16[4,2,2048]{2,1,0:T(2,128)(2,1)S(1)} %fusion.6), channel_id=1, source_target_pairs={{0,2},{1,3},{2,0},{3,1},{4,6},{5,7},{6,4},{7,5},{8,10},{9,11},{10,... | collective-permute-start | bytes 98312 | tf_op jit(solution)/shard_map/ppermute | solution.py:170
  4.7 1.6 %copy-start.1 = (bf16[1,2,4,2048]{3,2,1,0:T(4,128)(2,1)S(1)}, bf16[1,2,4,2048]{3,2,1,0:T(4,128)(2,1)}, u32[]{:S(2)}) copy-start(bf16[1,2,4,2048]{3,2,1,0:T(4,128)(2,1)} %param.7) | copy-start | bytes 98308
  4.8 4.3 %collective-permute-start = (bf16[8,2,2048]{2,1,0:T(2,128)(2,1)S(1)}, bf16[8,2,2048]{2,1,0:T(2,128)(2,1)S(1)}, u32[]{:S(2)}, u32[]{:S(2)}) collective-permute-start(bf16[8,2,2048]{2,1,0:T(2,128)(2,1)S(1)} %pad_maximum_fusion), channel_id=1, source_target_pairs={{0,1},{1,0},{2,3},{3,2},{4,5},{5,4},{6,7},{7,6},{8,9},{9,8},{10,11... | collective-permute-start | bytes 196616 | tf_op jit(solution)/shard_map/ppermute | solution.py:170
  9.4 6.2 %collective-permute-start.4 = (bf16[8,2,2048]{2,1,0:T(2,128)(2,1)S(1)}, bf16[8,2,2048]{2,1,0:T(2,128)(2,1)S(1)}, u32[]{:S(2)}, u32[]{:S(2)}) collective-permute-start(bf16[8,2,2048]{2,1,0:T(2,128)(2,1)S(1)} %bitcast.26), channel_id=1, source_target_pairs={{0,8},{1,9},{2,10},{3,11},{4,12},{5,13},{6,14},{7,15},{8,0},{9,1},... | collective-permute-start | bytes 196616 | tf_op jit(solution)/shard_map/ppermute | solution.py:127
  11.0 5.2 %collective-permute-start.5 = (bf16[8,2,2048]{2,1,0:T(2,128)(2,1)S(1)}, bf16[8,2,2048]{2,1,0:T(2,128)(2,1)S(1)}, u32[]{:S(2)}, u32[]{:S(2)}) collective-permute-start(bf16[8,2,2048]{2,1,0:T(2,128)(2,1)S(1)} %bitcast.27), channel_id=1, source_target_pairs={{0,12},{1,13},{2,14},{3,15},{4,8},{5,9},{6,10},{7,11},{8,4},{9,5},... | collective-permute-start | bytes 196616 | tf_op jit(solution)/shard_map/ppermute | solution.py:127
  12.4 4.5 %collective-permute-start.3 = (bf16[8,2,2048]{2,1,0:T(2,128)(2,1)S(1)}, bf16[8,2,2048]{2,1,0:T(2,128)(2,1)S(1)}, u32[]{:S(2)}, u32[]{:S(2)}) collective-permute-start(bf16[8,2,2048]{2,1,0:T(2,128)(2,1)S(1)} %bitcast.28), channel_id=1, source_target_pairs={{0,4},{1,5},{2,6},{3,7},{4,0},{5,1},{6,2},{7,3},{8,12},{9,13},{10,... | collective-permute-start | bytes 196616 | tf_op jit(solution)/shard_map/ppermute | solution.py:127
  17.0 4.0 %copy-start = (bf16[8,2,2048]{2,1,0:T(2,128)(2,1)}, bf16[8,2,2048]{2,1,0:T(2,128)(2,1)S(1)}, u32[]{:S(2)}) copy-start(bf16[8,2,2048]{2,1,0:T(2,128)(2,1)S(1)} %add_add_fusion.rest_0_) | copy-start | bytes 196612
  17.0 5.2 %collective-permute-start.6 = (bf16[8,2,2048]{2,1,0:T(2,128)(2,1)S(1)}, bf16[8,2,2048]{2,1,0:T(2,128)(2,1)S(1)}, u32[]{:S(2)}, u32[]{:S(2)}) collective-permute-start(bf16[8,2,2048]{2,1,0:T(2,128)(2,1)S(1)} %add_add_fusion.rest_0_), channel_id=1, source_target_pairs={{0,16},{1,17},{2,18},{3,19},{4,20},{5,21},{6,22},{7,23},{8,24},{9,... | collective-permute-start | bytes 196616 | tf_op jit(solution)/shard_map/ppermute | solution.py:127
  22.2 0.6 %copy-start.2 = (bf16[8,2,2048]{2,1,0:T(2,128)(2,1)}, bf16[8,2,2048]{2,1,0:T(2,128)(2,1)S(1)}, u32[]{:S(2)}) copy-start(bf16[8,2,2048]{2,1,0:T(2,128)(2,1)S(1)} %collective-permute-done.6.rest_1_) | copy-start | bytes 196612

commit v18 on v16

--- a/solution.py
+++ b/solution.py
@@ -175,7 +175,7 @@
         placed = jnp.where(first, jnp.stack([same_half, other_half], 1),
                            jnp.stack([other_half, same_half], 1)).reshape(-1, 2, seg_len)
         late = (placed.reshape(-1)[0] != placed.reshape(-1)[0]).astype(jnp.int32)
-        first_bin = doppler_start[0] + late
+        first_bin = doppler_start[0]
         refparts, _, _ = butterfly_sum(placed, axes, stride=4)
         samples = jnp.where(first, jnp.concatenate([mine_samples, other], -1),
                             jnp.concatenate([other, mine_samples], -1))

time: 42.9 us -> 43.1 us (level)
  waiting for transfers between devices: 5.24 us -> 7.07 us
  between operations: 2.73 us -> 1.43 us
  local copies, waits for them, and re-layouts: 1.9 us -> 1.38 us
    ppermute x4, waiting for transfers between devices: 2.53 us -> 5.68 us  [butterfly_sum(): parts.append(lax.ppermute(value, axes, pairs))]
    ppermute x3, waiting for transfers between devices: 2.71 us -> 1.38 us  [shards(): lax.ppermute(x, axes, [(i, i ^ m) for i in range(group)])]
    slice x1 -> x0, local copies, waits for them, and re-layouts: 0.51 us -> none  [shards(): late = (placed.reshape(-1)[0] != placed.reshape(-1)[0]).astype(jnp.int32)]
    pallas_call x1, Pallas kernels: 19.7 us -> 20.1 us  [shards(): pl.pallas_call(kernel, out_shape=jax.ShapeDtypeStruct((slot_count, 2, LB,...]
    unnamed x12 -> x11, local copies, waits for them, and re-layouts: 1.34 us -> 1.33 us
  transfers between devices with their start and end apart: 7 -> 7, of which waited for: 4 -> 5; matrix products, arithmetic and copies ran while one was open for 7% -> 6% of each run, Pallas kernels for 0% -> 0%
where the time goes in v18:
time: 43.1 us; the launch traced here: 43 us
  Pallas kernels  20.1 us (47%)
  starting transfers between devices  9.4 us (22%)
  waiting for transfers between devices  7.07 us (16%)
  other arithmetic  3.58 us (8%)
  between operations  1.43 us (3%)
  local copies, waits for them, and re-layouts  1.38 us (3%)
    pallas_call x1, Pallas kernels, shards(): pl.pallas_call(kernel, out_shape=jax.ShapeDtypeStruct((slot_count, 2, LB,...  20.1 us
    ppermute x4, starting transfers between devices, butterfly_sum(): parts.append(lax.ppermute(value, axes, pairs))  6.21 us
    ppermute x4, waiting for transfers between devices, butterfly_sum(): parts.append(lax.ppermute(value, axes, pairs))  5.68 us
    ppermute x3, starting transfers between devices, shards(): lax.ppermute(x, axes, [(i, i ^ m) for i in range(group)])  3.19 us
    ppermute x3, waiting for transfers between devices, shards(): lax.ppermute(x, axes, [(i, i ^ m) for i in range(group)])  1.38 us
    unnamed x11, local copies, waits for them, and re-layouts  1.33 us
    sin x1, other arithmetic, phase_rows(): return (jnp.cos(angle), jnp.sin(angle))  1.31 us
  transfers between devices with their start and end apart: 7, of which 5 were waited for; matrix products, arithmetic and copies ran while one was open for 6% of the time, Pallas kernels for 0%

profile of v18, /device:TPU:0, one launch (start us, length us, event | category | flops | bytes accessed | tf_op | source)
XLA Modules:
  0.0 43.0 jit_solution(3289866312079779918)
XLA Ops:
  0.0 0.0 copy-start.4
  0.0 0.7 %copy-done.4 = s32[4]{0:T(128)S(1)} copy-done((s32[4]{0:T(128)S(1)}, s32[4]{0:T(128)}, u32[]{:S(2)}) %copy-start.4) | copy-done | bytes 40
  0.7 0.0 copy-start.3
  0.7 0.9 %fusion.6 = bf16[4,2,2048]{2,1,0:T(2,128)(2,1)S(1)} fusion(bf16[1,2,4,2048]{3,2,1,0:T(4,128)(2,1)} %param.7, pred[4]{0:T(512)(128)(4,1)S(1)} %broadcast_compare_fusion), kind=kLoop, calls=%fused_computation.20 | loop fusion | flops 16384 | bytes 65540 | tf_op jit(solution)/shard_map/transpose | solution.py:168
  1.5 2.4 %collective-permute-start.2 = (bf16[4,2,2048]{2,1,0:T(2,128)(2,1)S(1)}, bf16[4,2,2048]{2,1,0:T(2,128)(2,1)S(1)}, u32[]{:S(2)}, u32[]{:S(2)}) collective-permute-start(bf16[4,2,2048]{2,1,0:T(2,128)(2,1)S(1)} %fusion.6), channel_id=1, source_target_pairs={{0,3},{1,2},{2,1},{3,0},{4,7},{5,6},{6,5},{7,4},{8,11},{9,10},{10,... | collective-permute-start | bytes 98312 | tf_op jit(solution)/shard_map/ppermute | solution.py:170
  4.0 0.7 %collective-permute-start.1 = (bf16[4,2,2048]{2,1,0:T(2,128)(2,1)S(1)}, bf16[4,2,2048]{2,1,0:T(2,128)(2,1)S(1)}, u32[]{:S(2)}, u32[]{:S(2)}) collective-permute-start(bf16[4,2,2048]{2,1,0:T(2,128)(2,1)S(1)} %fusion.6), channel_id=1, source_target_pairs={{0,2},{1,3},{2,0},{3,1},{4,6},{5,7},{6,4},{7,5},{8,10},{9,11},{10,... | collective-permute-start | bytes 98312 | tf_op jit(solution)/shard_map/ppermute | solution.py:170
  4.6 0.0 copy-done.3
  4.7 0.1 pad_maximum_fusion
  4.8 0.1 collective-permute-start
  5.6 0.1 pad_add_fusion
  5.6 0.0 copy-start.1
  5.6 1.3 %fusion.3 = (f32[128,152]{1,0:T(8,128)}, f32[128,152]{1,0:T(8,128)}) fusion(s32[152]{0:T(256)S(1)} %pad_add_fusion, s32[128]{0:T(128)S(1)} %iota_add_fusion), kind=kLoop, calls=%fused_computation.13 | loop fusion | flops 272384 | bytes 156768 | tf_op jit(solution)/shard_map/sin | solution.py:21
  7.6 0.0 collective-permute-done.1
  7.6 0.0 copy-done.1
  7.6 0.1 add_bitcast_fusion
  7.7 0.0 collective-permute-done.2
  7.7 1.4 %collective-permute-done = bf16[8,2,2048]{2,1,0:T(2,128)(2,1)S(1)} collective-permute-done((bf16[8,2,2048]{2,1,0:T(2,128)(2,1)S(1)}, bf16[8,2,2048]{2,1,0:T(2,128)(2,1)S(1)}, u32[]{:S(2)}, u32[]{:S(2)}) %collective-permute-start) | collective-permute-done | bytes 65568 | tf_op jit(solution)/shard_map/ppermute | solution.py:170
  9.1 0.1 fusion.5
  9.2 0.1 broadcast_select_fusion
  9.3 1.6 %collective-permute-start.4 = (bf16[8,2,2048]{2,1,0:T(2,128)(2,1)S(1)}, bf16[8,2,2048]{2,1,0:T(2,128)(2,1)S(1)}, u32[]{:S(2)}, u32[]{:S(2)}) collective-permute-start(bf16[8,2,2048]{2,1,0:T(2,128)(2,1)S(1)} %bitcast.27), channel_id=1, source_target_pairs={{0,8},{1,9},{2,10},{3,11},{4,12},{5,13},{6,14},{7,15},{8,0},{9,1},... | collective-permute-start | bytes 196616 | tf_op jit(solution)/shard_map/ppermute | solution.py:127
  11.0 1.4 %collective-permute-start.5 = (bf16[8,2,2048]{2,1,0:T(2,128)(2,1)S(1)}, bf16[8,2,2048]{2,1,0:T(2,128)(2,1)S(1)}, u32[]{:S(2)}, u32[]{:S(2)}) collective-permute-start(bf16[8,2,2048]{2,1,0:T(2,128)(2,1)S(1)} %bitcast.28), channel_id=1, source_target_pairs={{0,12},{1,13},{2,14},{3,15},{4,8},{5,9},{6,10},{7,11},{8,4},{9,5},... | collective-permute-start | bytes 196616 | tf_op jit(solution)/shard_map/ppermute | solution.py:127
  12.4 0.5 %collective-permute-start.3 = (bf16[8,2,2048]{2,1,0:T(2,128)(2,1)S(1)}, bf16[8,2,2048]{2,1,0:T(2,128)(2,1)S(1)}, u32[]{:S(2)}, u32[]{:S(2)}) collective-permute-start(bf16[8,2,2048]{2,1,0:T(2,128)(2,1)S(1)} %bitcast.29), channel_id=1, source_target_pairs={{0,4},{1,5},{2,6},{3,7},{4,0},{5,1},{6,2},{7,3},{8,12},{9,13},{10,... | collective-permute-start | bytes 196616 | tf_op jit(solution)/shard_map/ppermute | solution.py:127
  12.9 0.1 broadcast_select_fusion.1
  13.0 1.2 %collective-permute-done.4 = bf16[8,2,2048]{2,1,0:T(2,128)(2,1)S(1)} collective-permute-done((bf16[8,2,2048]{2,1,0:T(2,128)(2,1)S(1)}, bf16[8,2,2048]{2,1,0:T(2,128)(2,1)S(1)}, u32[]{:S(2)}, u32[]{:S(2)}) %collective-permute-start.4) | collective-permute-done | bytes 65568 | tf_op jit(solution)/shard_map/ppermute | solution.py:127
  14.2 1.9 %collective-permute-done.5 = bf16[8,2,2048]{2,1,0:T(2,128)(2,1)S(1)} collective-permute-done((bf16[8,2,2048]{2,1,0:T(2,128)(2,1)S(1)}, bf16[8,2,2048]{2,1,0:T(2,128)(2,1)S(1)}, u32[]{:S(2)}, u32[]{:S(2)}) %collective-permute-start.5) | collective-permute-done | bytes 65568 | tf_op jit(solution)/shard_map/ppermute | solution.py:127
  16.2 0.7 %collective-permute-done.3 = bf16[8,2,2048]{2,1,0:T(2,128)(2,1)S(1)} collective-permute-done((bf16[8,2,2048]{2,1,0:T(2,128)(2,1)S(1)}, bf16[8,2,2048]{2,1,0:T(2,128)(2,1)S(1)}, u32[]{:S(2)}, u32[]{:S(2)}) %collective-permute-start.3) | collective-permute-done | bytes 65568 | tf_op jit(solution)/shard_map/ppermute | solution.py:127
  16.9 0.1 add_add_fusion.rest_0_
  17.0 0.0 copy-start
  17.0 2.7 %collective-permute-start.6 = (bf16[8,2,2048]{2,1,0:T(2,128)(2,1)S(1)}, bf16[8,2,2048]{2,1,0:T(2,128)(2,1)S(1)}, u32[]{:S(2)}, u32[]{:S(2)}) collective-permute-start(bf16[8,2,2048]{2,1,0:T(2,128)(2,1)S(1)} %add_add_fusion.rest_0_), channel_id=1, source_target_pairs={{0,16},{1,17},{2,18},{3,19},{4,20},{5,21},{6,22},{7,23},{8,24},{9,... | collective-permute-start | bytes 196616 | tf_op jit(solution)/shard_map/ppermute | solution.py:127
  19.6 0.7 %pad_convert_fusion.wpad_ref = f32[4,2,5248]{2,1,0:T(2,128)} fusion(bf16[4,2,4096]{2,1,0:T(2,128)(2,1)S(1)} %broadcast_select_fusion.1), kind=kLoop, calls=%fused_computation.10 | loop fusion | flops 41984 | bytes 233472 | tf_op jit(solution)/shard_map/jit(_pad)/pad | solution.py:190
  20.4 0.0 copy-done
  20.4 1.8 %collective-permute-done.6.rest_1_ = bf16[8,2,2048]{2,1,0:T(2,128)(2,1)S(1)} collective-permute-done((bf16[8,2,2048]{2,1,0:T(2,128)(2,1)S(1)}, bf16[8,2,2048]{2,1,0:T(2,128)(2,1)S(1)}, u32[]{:S(2)}, u32[]{:S(2)}) %collective-permute-start.6) | collective-permute-done | bytes 65568 | tf_op jit(solution)/shard_map/ppermute | solution.py:127
  22.2 0.0 copy-start.2
  22.2 0.6 %copy-done.2 = bf16[8,2,2048]{2,1,0:T(2,128)(2,1)} copy-done((bf16[8,2,2048]{2,1,0:T(2,128)(2,1)}, bf16[8,2,2048]{2,1,0:T(2,128)(2,1)S(1)}, u32[]{:S(2)}) %copy-start.2) | copy-done | bytes 65560
  22.8 20.1 %shard_map.64 = f32[6,2,128,128]{3,2,1,0:T(8,128)} custom-call(s32[6]{0:T(128)} %bitcast.30, s32[1]{0:T(128)S(6)} %copy.18.count_ref, f32[4,2,5248]{2,1,0:T(2,128)} %pad_convert_fusion.wpad_ref, f32[128,152]{1,0:T(8,128)} %get-tuple-element.8.cos_ref, f32[128,152]{1,0:T(8,128)} %get-tuple-element.7.sin_ref, bf16[8,2,2048]{2,1,0:T(2,128)(2,1)} %copy-done, ...), custom_call_target="tpu_custom_call" | custom-call | tf_op jit(solution)/shard_map/pallas_call | solution.py:203
  (7 shorter events, 0.1 us)
Async XLA Ops:
  0.0 0.7 %copy-start.4 = (s32[4]{0:T(128)S(1)}, s32[4]{0:T(128)}, u32[]{:S(2)}) copy-start(s32[4]{0:T(128)} %param.8) | copy-start | bytes 52
  0.7 4.0 %copy-start.3 = (bf16[1,2,4,2048]{3,2,1,0:T(4,128)(2,1)S(1)}, bf16[1,2,4,2048]{3,2,1,0:T(4,128)(2,1)}, u32[]{:S(2)}) copy-start(bf16[1,2,4,2048]{3,2,1,0:T(4,128)(2,1)} %param.6) | copy-start | bytes 98308
  1.5 6.2 %collective-permute-start.2 = (bf16[4,2,2048]{2,1,0:T(2,128)(2,1)S(1)}, bf16[4,2,2048]{2,1,0:T(2,128)(2,1)S(1)}, u32[]{:S(2)}, u32[]{:S(2)}) collective-permute-start(bf16[4,2,2048]{2,1,0:T(2,128)(2,1)S(1)} %fusion.6), channel_id=1, source_target_pairs={{0,3},{1,2},{2,1},{3,0},{4,7},{5,6},{6,5},{7,4},{8,11},{9,10},{10,... | collective-permute-start | bytes 98312 | tf_op jit(solution)/shard_map/ppermute | solution.py:170
  4.0 3.6 %collective-permute-start.1 = (bf16[4,2,2048]{2,1,0:T(2,128)(2,1)S(1)}, bf16[4,2,2048]{2,1,0:T(2,128)(2,1)S(1)}, u32[]{:S(2)}, u32[]{:S(2)}) collective-permute-start(bf16[4,2,2048]{2,1,0:T(2,128)(2,1)S(1)} %fusion.6), channel_id=1, source_target_pairs={{0,2},{1,3},{2,0},{3,1},{4,6},{5,7},{6,4},{7,5},{8,10},{9,11},{10,... | collective-permute-start | bytes 98312 | tf_op jit(solution)/shard_map/ppermute | solution.py:170
  4.8 4.3 %collective-permute-start = (bf16[8,2,2048]{2,1,0:T(2,128)(2,1)S(1)}, bf16[8,2,2048]{2,1,0:T(2,128)(2,1)S(1)}, u32[]{:S(2)}, u32[]{:S(2)}) collective-permute-start(bf16[8,2,2048]{2,1,0:T(2,128)(2,1)S(1)} %pad_maximum_fusion), channel_id=1, source_target_pairs={{0,1},{1,0},{2,3},{3,2},{4,5},{5,4},{6,7},{7,6},{8,9},{9,8},{10,11... | collective-permute-start | bytes 196616 | tf_op jit(solution)/shard_map/ppermute | solution.py:170
  5.6 2.0 %copy-start.1 = (bf16[1,2,4,2048]{3,2,1,0:T(4,128)(2,1)S(1)}, bf16[1,2,4,2048]{3,2,1,0:T(4,128)(2,1)}, u32[]{:S(2)}) copy-start(bf16[1,2,4,2048]{3,2,1,0:T(4,128)(2,1)} %param.7) | copy-start | bytes 98308
  9.3 4.9 %collective-permute-start.4 = (bf16[8,2,2048]{2,1,0:T(2,128)(2,1)S(1)}, bf16[8,2,2048]{2,1,0:T(2,128)(2,1)S(1)}, u32[]{:S(2)}, u32[]{:S(2)}) collective-permute-start(bf16[8,2,2048]{2,1,0:T(2,128)(2,1)S(1)} %bitcast.27), channel_id=1, source_target_pairs={{0,8},{1,9},{2,10},{3,11},{4,12},{5,13},{6,14},{7,15},{8,0},{9,1},... | collective-permute-start | bytes 196616 | tf_op jit(solution)/shard_map/ppermute | solution.py:127
  11.0 5.2 %collective-permute-start.5 = (bf16[8,2,2048]{2,1,0:T(2,128)(2,1)S(1)}, bf16[8,2,2048]{2,1,0:T(2,128)(2,1)S(1)}, u32[]{:S(2)}, u32[]{:S(2)}) collective-permute-start(bf16[8,2,2048]{2,1,0:T(2,128)(2,1)S(1)} %bitcast.28), channel_id=1, source_target_pairs={{0,12},{1,13},{2,14},{3,15},{4,8},{5,9},{6,10},{7,11},{8,4},{9,5},... | collective-permute-start | bytes 196616 | tf_op jit(solution)/shard_map/ppermute | solution.py:127
  12.4 4.5 %collective-permute-start.3 = (bf16[8,2,2048]{2,1,0:T(2,128)(2,1)S(1)}, bf16[8,2,2048]{2,1,0:T(2,128)(2,1)S(1)}, u32[]{:S(2)}, u32[]{:S(2)}) collective-permute-start(bf16[8,2,2048]{2,1,0:T(2,128)(2,1)S(1)} %bitcast.29), channel_id=1, source_target_pairs={{0,4},{1,5},{2,6},{3,7},{4,0},{5,1},{6,2},{7,3},{8,12},{9,13},{10,... | collective-permute-start | bytes 196616 | tf_op jit(solution)/shard_map/ppermute | solution.py:127
  17.0 3.4 %copy-start = (bf16[8,2,2048]{2,1,0:T(2,128)(2,1)}, bf16[8,2,2048]{2,1,0:T(2,128)(2,1)S(1)}, u32[]{:S(2)}) copy-start(bf16[8,2,2048]{2,1,0:T(2,128)(2,1)S(1)} %add_add_fusion.rest_0_) | copy-start | bytes 196612
  17.0 5.2 %collective-permute-start.6 = (bf16[8,2,2048]{2,1,0:T(2,128)(2,1)S(1)}, bf16[8,2,2048]{2,1,0:T(2,128)(2,1)S(1)}, u32[]{:S(2)}, u32[]{:S(2)}) collective-permute-start(bf16[8,2,2048]{2,1,0:T(2,128)(2,1)S(1)} %add_add_fusion.rest_0_), channel_id=1, source_target_pairs={{0,16},{1,17},{2,18},{3,19},{4,20},{5,21},{6,22},{7,23},{8,24},{9,... | collective-permute-start | bytes 196616 | tf_op jit(solution)/shard_map/ppermute | solution.py:127
  22.2 0.6 %copy-start.2 = (bf16[8,2,2048]{2,1,0:T(2,128)(2,1)}, bf16[8,2,2048]{2,1,0:T(2,128)(2,1)S(1)}, u32[]{:S(2)}) copy-start(bf16[8,2,2048]{2,1,0:T(2,128)(2,1)S(1)} %collective-permute-done.6.rest_1_) | copy-start | bytes 196612
